TPU v7x, 256 devices: a whole 4x4x8 slice. The times are simulated.
256 devices in a mesh: section: 16 (over y, x_hi, core), expert: 16 (over x_lo, z).
Axes of the slice: x: 4 (x_hi: 2, x_lo: 2; x = x_hi * 2 + x_lo), y: 4, z: 8, core: 2. Of those that a mesh axis runs over, the one named last changes fastest.
Arguments:
- tokens: bfloat16 [16, 2048, 7168], P('section', 'expert'), may hold values from -6 to 6
- cotangent: bfloat16 [16, 2048, 7168], P('section', 'expert'), may hold values from -6 to 6
- expert_ids: int32 [16, 2048, 8], P('section', 'expert'), may hold values from 0 to 31, as said below
- slot_index: int32 [16, 2048, 8], P('section', 'expert'), may hold values from 0 to 31, as said below
- gate_scale: float32 [16, 2048, 8], P('section', 'expert'), may hold values from 0.2 to 1.2
- gate_weight: bfloat16 [16, 7168, 2048], P('section', None, 'expert'), may hold values from -0.0625 to 0.0625
- up_weight: bfloat16 [16, 7168, 2048], P('section', None, 'expert'), may hold values from -0.0625 to 0.0625
- down_weight: bfloat16 [16, 2048, 7168], P('section', 'expert'), may hold values from -0.125 to 0.125
Outputs:
- next_input: bfloat16 [16, 2048, 7168], P('section', 'expert')
- prior_grad: bfloat16 [16, 2048, 7168], P('section', 'expert')
Inputs may be any that keep to these rules, and one draw needn't show every extreme that they name: `expert_ids`: each token names 8 different experts; among the 128 tokens of one device every expert is named exactly 32 times. `slot_index`: among the routes of one device's tokens to one expert, the slots are 0 to 31, each once.
All inputs are finite; a program needn't handle non-finite values.
Results may differ from a plain program's by a relative error of at most 0.011.
Values may be sent and summed in bfloat16 or wider, within the bound.
No kernel may reach another device: no remote copies, remote signals or barrier semaphores. Data moves between devices by JAX's collectives and lax.ppermute only.
A program may use at most 128 MiB of HBM per device.

v0:
```python
import jax
import jax.numpy as jnp
from jax import lax
from jax.sharding import PartitionSpec as P

CAP = 32


def from_behind(x, axis, by):
    length = lax.axis_size(axis)
    pairs = [(i, i + by) for i in range(length) if 0 <= i + by < length]
    return lax.ppermute(x, axis, pairs)


def silu_parts(gate):
    sig = jax.nn.sigmoid(gate)
    return (gate * sig, sig * (1.0 + gate * (1.0 - sig)))


def body(
    tokens, cotangent, expert_ids, slot_index, gate_scale, gate_weight, up_weight, down_weight
):
    section = lax.axis_index("section")
    local = tokens[0]
    grad_out = cotangent[0]
    named = expert_ids[0]
    gate_mat = gate_weight[0]
    up_mat = up_weight[0]
    down_mat = down_weight[0]
    width_local = gate_mat.shape[1]
    hit = named == section
    chosen = jnp.any(hit, axis=1)
    slot = jnp.sum(jnp.where(hit, slot_index[0], 0), axis=1)
    weight = jnp.sum(jnp.where(hit, gate_scale[0], jnp.float32(0.0)), axis=1)
    places = jnp.arange(CAP, dtype=jnp.int32)
    table = ((places[:, None] == slot[None, :]) & chosen[None, :]).astype(jnp.bfloat16)
    sent = jnp.dot(table, local, preferred_element_type=jnp.float32).astype(jnp.bfloat16)
    carried = (weight[:, None] * grad_out.astype(jnp.float32)).astype(jnp.bfloat16)
    back = jnp.dot(table, carried, preferred_element_type=jnp.float32).astype(jnp.bfloat16)
    piece = lax.all_gather(sent, "expert", axis=0, tiled=True)
    gate_up = jnp.concatenate(
        [
            jnp.dot(piece, gate_mat, preferred_element_type=jnp.float32),
            jnp.dot(piece, up_mat, preferred_element_type=jnp.float32),
        ],
        axis=1,
    )
    gate = gate_up[:, :width_local]
    up = gate_up[:, width_local:]
    act, slope = silu_parts(gate)
    hidden = (act * up).astype(jnp.bfloat16)
    combined = lax.psum_scatter(
        jnp.dot(hidden, down_mat, preferred_element_type=jnp.float32).astype(jnp.bfloat16),
        "expert",
        scatter_dimension=0,
        tiled=True,
    ).astype(jnp.float32)
    grad_hidden = jnp.dot(
        lax.all_gather(back, "expert", axis=0, tiled=True),
        down_mat.T,
        preferred_element_type=jnp.float32,
    )
    grad_up = (grad_hidden * act).astype(jnp.bfloat16)
    grad_gate = (grad_hidden * up * slope).astype(jnp.bfloat16)
    behind = jnp.dot(grad_gate, gate_mat.T, preferred_element_type=jnp.float32)
    inward = lax.psum_scatter(
        (behind + jnp.dot(grad_up, up_mat.T, preferred_element_type=jnp.float32)).astype(
            jnp.bfloat16
        ),
        "expert",
        scatter_dimension=0,
        tiled=True,
    ).astype(jnp.float32)
    output = local.astype(jnp.float32) + weight[:, None] * jnp.take(combined, slot, axis=0)
    grad_in = grad_out.astype(jnp.float32) + jnp.where(
        chosen[:, None], jnp.take(inward, slot, axis=0), jnp.float32(0.0)
    )
    next_input = from_behind(output.astype(jnp.bfloat16)[None], "section", 1)
    prior_grad = from_behind(grad_in.astype(jnp.bfloat16)[None], "section", -1)
    return (next_input, prior_grad)


def solution(mesh):
    in_specs = (
        P("section", "expert", None),
        P("section", "expert", None),
        P("section", "expert", None),
        P("section", "expert", None),
        P("section", "expert", None),
        P("section", None, "expert"),
        P("section", None, "expert"),
        P("section", "expert", None),
    )
    out_specs = (P("section", "expert", None), P("section", "expert", None))
    return jax.shard_map(body, mesh=mesh, in_specs=in_specs, out_specs=out_specs, check_vma=False)
```

profile of v0, /device:TPU:5, one launch (start us, length us, event | category | flops | bytes accessed | tf_op | source)
XLA Modules:
  0.0 466.3 jit_solution(15120559337887811934)
XLA Ops:
  7.2 0.0 copy-start
  7.2 0.0 all-gather.3.cloned.1.call-start
  7.2 0.8 select_reduce_fusion.1
  8.1 0.7 select_reduce_fusion
  8.8 2.6 convolution_convert_fusion.2
  11.4 0.0 all-gather.3.cloned.1.call-update
  11.5 0.0 all-gather.5.cloned.1.call-start
  11.5 2.8 convolution_convert_fusion.1
  14.3 0.0 all-gather.5.cloned.1.call-update
  14.3 0.0 reduce-scatter.5.cloned.1.call-start
  14.4 90.1 %all-gather.3.cloned.1.call-done = bf16[512,7168]{1,0:T(8,128)(2,1)} async-done(((bf16[32,7168]{1,0:T(8,128)(2,1)}), bf16[512,7168]{1,0:T(8,128)(2,1)}) %all-gather.3.cloned.1.call-update) | async-done | bytes 7340048 | tf_op jit(solution)/shard_map/all_gather | solution.py:40
  104.5 0.0 copy-done
  104.5 0.0 copy-start.2
  104.5 0.0 copy-start.5
  104.5 5.3 %fusion.16 = f32[512,128]{1,0:T(8,128)S(1)} fusion(bf16[512,7168]{1,0:T(8,128)(2,1)} %all-gather.3.cloned.1.call-done, bf16[1,7168,128]{2,1,0:T(8,128)(2,1)S(1)} %copy-done), kind=kOutput, calls=%fused_computation.25 | convolution fusion | flops 939524096 | bytes 9437184 | tf_op jit(solution)/shard_map/dot_general | solution.py:43
  109.8 0.0 copy-done.2
  109.8 0.4 copy-done.5
  110.2 2.1 fusion.12
  112.3 82.7 %all-gather.5.cloned.1.call-done = bf16[512,7168]{1,0:T(8,128)(2,1)} async-done(((bf16[32,7168]{1,0:T(8,128)(2,1)}), bf16[512,7168]{1,0:T(8,128)(2,1)}) %all-gather.5.cloned.1.call-update) | async-done | bytes 7340048 | tf_op jit(solution)/shard_map/all_gather | solution.py:59
  195.0 5.6 %fusion.8 = f32[512,128]{1,0:T(8,128)S(1)} fusion(bf16[512,7168]{1,0:T(8,128)(2,1)} %all-gather.5.cloned.1.call-done, bf16[1,128,7168]{2,1,0:T(8,128)(2,1)} %param.17), kind=kOutput, calls=%fused_computation.17 | convolution fusion | flops 939524096 | bytes 9437184 | tf_op jit(solution)/shard_map/dot_general | solution.py:58
  200.6 0.0 copy-start.3
  200.6 7.3 %fusion.14 = f32[512,7168]{1,0:T(8,128)} fusion(bf16[1,7168,128]{2,1,0:T(8,128)(2,1)S(1)} %copy-done, f32[512,128]{1,0:T(8,128)S(1)} %fusion.16, f32[512,128]{1,0:T(8,128)S(1)} %fusion.8, f32[512,128]{1,0:T(8,128)S(1)} %fusion.12), kind=kOutput, calls=%fused_computation.23 | convolution fusion | flops 940179456 | bytes 17301504 | tf_op jit(solution)/shard_map/dot_general | solution.py:65
  207.9 0.0 copy-done.3
  207.9 10.2 %add_convert_fusion = bf16[512,7168]{1,0:T(8,128)(2,1)} fusion(f32[512,7168]{1,0:T(8,128)} %fusion.14, bf16[1,7168,128]{2,1,0:T(8,128)(2,1)S(1)} %copy-done.3, f32[512,128]{1,0:T(8,128)S(1)} %fusion.8, f32[512,128]{1,0:T(8,128)S(1)} %fusion.16), kind=kOutput, calls=%fused_computation.2 | convolution fusion | flops 947257344 | bytes 24379392 | tf_op jit(solution)/shard_map/dot_general | solution.py:67
  218.1 0.0 copy-start.4
  218.1 0.0 reduce-scatter.5.cloned.1.call-update
  218.1 0.2 reduce-scatter.3.cloned.1.call-start
  218.4 1.2 copy-done.4
  219.6 5.0 %convolution_convert_fusion = bf16[512,7168]{1,0:T(8,128)(2,1)} fusion(bf16[1,128,7168]{2,1,0:T(8,128)(2,1)S(1)} %copy-done.4, f32[512,128]{1,0:T(8,128)S(1)} %fusion.12, f32[512,128]{1,0:T(8,128)S(1)} %fusion.16), kind=kOutput, calls=%fused_computation.3 | convolution fusion | flops 943587328 | bytes 9699328 | tf_op jit(solution)/shard_map/dot_general | solution.py:53
  224.6 0.0 reduce-scatter.3.cloned.1.call-update
  224.7 79.9 %reduce-scatter.5.cloned.1.call-done = bf16[32,7168]{1,0:T(8,128)(2,1)} async-done(((bf16[512,7168]{1,0:T(8,128)(2,1)}), bf16[32,7168]{1,0:T(8,128)(2,1)}) %reduce-scatter.5.cloned.1.call-update) | async-done | bytes 458768 | tf_op jit(solution)/shard_map/reduce_scatter | solution.py:66
  304.6 1.1 convert_element_type.60
  305.7 3.6 gather_fusion.1
  309.3 87.7 %reduce-scatter.3.cloned.1.call-done = bf16[32,7168]{1,0:T(8,128)(2,1)} async-done(((bf16[512,7168]{1,0:T(8,128)(2,1)}), bf16[32,7168]{1,0:T(8,128)(2,1)}) %reduce-scatter.3.cloned.1.call-update) | async-done | bytes 458768 | tf_op jit(solution)/shard_map/reduce_scatter | solution.py:52
  397.0 1.1 convert_element_type.51
  398.1 3.4 gather_fusion
  401.5 5.7 %fusion.5 = (bf16[1,128,7168]{2,1,0:T(8,128)(2,1)S(1)}, bf16[1,128,7168]{2,1,0:T(8,128)(2,1)S(1)}) fusion(f32[128,7168]{1,0:T(8,128)} %gather_fusion.1, bf16[1,128,7168]{2,1,0:T(8,128)(2,1)} %param.11, pred[128]{0:T(512)(128)(4,1)S(1)} %compare_and_fusion, pred[128]{0:T(512)(128)(4,1)S(1)} %reduce_or.9, f32[128,7168]{1,0:T(8,128)} %gather_fusion, ...), kind=kLoop, calls=%fused_computation.15 | loop fusion | flops 9175040 | bytes 14680832 | tf_op jit(solution)/shard_map/broadcast_in_dim | solution.py:79
  407.2 7.2 %collective-permute-start = (bf16[1,128,7168]{2,1,0:T(8,128)(2,1)S(1)}, bf16[1,128,7168]{2,1,0:T(8,128)(2,1)S(1)}, u32[]{:S(2)}, u32[]{:S(2)}) collective-permute-start(bf16[1,128,7168]{2,1,0:T(8,128)(2,1)S(1)} %get-tuple-element.6), channel_id=1, source_target_pairs={{0,16},{16,32},{32,48},{48,64},{64,80},{80,96},{96,112},{112,128},... | collective-permute-start | bytes 5505032 | tf_op jit(solution)/shard_map/ppermute | solution.py:12
  414.4 0.0 copy-start.1
  414.4 2.1 collective-permute-start.1
  416.5 33.6 %collective-permute-done = bf16[1,128,7168]{2,1,0:T(8,128)(2,1)S(1)} collective-permute-done((bf16[1,128,7168]{2,1,0:T(8,128)(2,1)S(1)}, bf16[1,128,7168]{2,1,0:T(8,128)(2,1)S(1)}, u32[]{:S(2)}, u32[]{:S(2)}) %collective-permute-start) | collective-permute-done | bytes 1835040 | tf_op jit(solution)/shard_map/ppermute | solution.py:12
  450.1 7.2 %collective-permute-done.1 = bf16[1,128,7168]{2,1,0:T(8,128)(2,1)S(1)} collective-permute-done((bf16[1,128,7168]{2,1,0:T(8,128)(2,1)S(1)}, bf16[1,128,7168]{2,1,0:T(8,128)(2,1)S(1)}, u32[]{:S(2)}, u32[]{:S(2)}) %collective-permute-start.1) | collective-permute-done | bytes 1835040 | tf_op jit(solution)/shard_map/ppermute | solution.py:12
  457.3 1.2 copy.12
  458.5 1.2 copy.13
  459.8 0.0 copy-done.1
  (4 shorter events, 0.0 us)
Async XLA Ops:
  7.2 97.3 %copy-start = (bf16[1,7168,128]{2,1,0:T(8,128)(2,1)S(1)}, bf16[1,7168,128]{2,1,0:T(8,128)(2,1)}, u32[]{:S(2)}) copy-start(bf16[1,7168,128]{2,1,0:T(8,128)(2,1)} %param.15) | copy-start | bytes 5505028
  7.2 97.3 %all-gather.3.cloned.1.call-start = ((), (), s32[]{:S(2)}) async-start(), calls=%async_computation.2 | async-start | bytes 7798784 | tf_op jit(solution)/shard_map/all_gather | solution.py:40
  11.5 183.5 %all-gather.5.cloned.1.call-start = ((), (), s32[]{:S(2)}) async-start(), calls=%async_computation.4 | async-start | bytes 7798784 | tf_op jit(solution)/shard_map/all_gather | solution.py:59
  14.3 290.3 %reduce-scatter.5.cloned.1.call-start = ((), (), s32[]{:S(2)}) async-start(), calls=%async_computation.5 | async-start | bytes 7798784 | tf_op jit(solution)/shard_map/reduce_scatter | solution.py:66
  104.5 5.3 %copy-start.2 = (bf16[1,7168,128]{2,1,0:T(8,128)(2,1)S(1)}, bf16[1,7168,128]{2,1,0:T(8,128)(2,1)}, u32[]{:S(2)}) copy-start(bf16[1,7168,128]{2,1,0:T(8,128)(2,1)} %param.16) | copy-start | bytes 5505028
  104.5 5.7 %copy-start.5 = (bf16[512,7168]{1,0:T(8,128)(2,1)S(1)}, bf16[512,7168]{1,0:T(8,128)(2,1)}, u32[]{:S(2)}) copy-start(bf16[512,7168]{1,0:T(8,128)(2,1)} %all-gather.3.cloned.1.call-done) | copy-start | bytes 22020100
  200.6 7.3 %copy-start.3 = (bf16[1,7168,128]{2,1,0:T(8,128)(2,1)S(1)}, bf16[1,7168,128]{2,1,0:T(8,128)(2,1)}, u32[]{:S(2)}) copy-start(bf16[1,7168,128]{2,1,0:T(8,128)(2,1)} %param.16) | copy-start | bytes 5505028
  218.1 1.5 copy-start.4
  218.1 178.9 %reduce-scatter.3.cloned.1.call-start = ((), (), s32[]{:S(2)}) async-start(), calls=%async_computation.3 | async-start | bytes 7798784 | tf_op jit(solution)/shard_map/reduce_scatter | solution.py:52
  407.2 42.8 %collective-permute-start = (bf16[1,128,7168]{2,1,0:T(8,128)(2,1)S(1)}, bf16[1,128,7168]{2,1,0:T(8,128)(2,1)S(1)}, u32[]{:S(2)}, u32[]{:S(2)}) collective-permute-start(bf16[1,128,7168]{2,1,0:T(8,128)(2,1)S(1)} %get-tuple-element.6), channel_id=1, source_target_pairs={{0,16},{16,32},{32,48},{48,64},{64,80},{80,96},{96,112},{112,128},... | collective-permute-start | bytes 5505032 | tf_op jit(solution)/shard_map/ppermute | solution.py:12
  414.4 45.3 %copy-start.1 = (bf16[1,7168,128]{2,1,0:T(8,128)(2,1)S(1)}, bf16[1,7168,128]{2,1,0:T(8,128)(2,1)}, u32[]{:S(2)}) copy-start(bf16[1,7168,128]{2,1,0:T(8,128)(2,1)} %param.15) | copy-start | bytes 5505028
  414.4 42.9 %collective-permute-start.1 = (bf16[1,128,7168]{2,1,0:T(8,128)(2,1)S(1)}, bf16[1,128,7168]{2,1,0:T(8,128)(2,1)S(1)}, u32[]{:S(2)}, u32[]{:S(2)}) collective-permute-start(bf16[1,128,7168]{2,1,0:T(8,128)(2,1)S(1)} %get-tuple-element.5), channel_id=1, source_target_pairs={{16,0},{32,16},{48,32},{64,48},{80,64},{96,80},{112,96},{128,112},... | collective-permute-start | bytes 5505032 | tf_op jit(solution)/shard_map/ppermute | solution.py:12
Sparse Core Ops, SparseCore 0:
  11.6 92.8 all-gather.2
  106.8 88.0 all-gather.4
  218.2 86.3 reduce-scatter.4
  307.1 89.9 reduce-scatter.2
where the time goes:
time: 468 us; the launch traced here: 466 us
  waiting for transfers between devices  381 us (81%)
  matrix products  40.9 us (9%)
  between operations  13.9 us (3%)
  local copies, waits for them, and re-layouts  11.2 us (2%)
  starting transfers between devices  9.6 us (2%)
  other arithmetic  9.46 us (2%)
    all_gather x1, waiting for transfers between devices, body(): piece = lax.all_gather(sent, 'expert', axis=0, tiled=True)  90.1 us
    reduce_scatter x1, waiting for transfers between devices, body(): lax.psum_scatter(jnp.dot(hidden, down_mat, preferred_element_type=jnp.flo...  87.7 us
    all_gather x1, waiting for transfers between devices, body(): lax.all_gather(back, 'expert', axis=0, tiled=True)  82.7 us
    reduce_scatter x1, waiting for transfers between devices, body(): lax.psum_scatter((behind + jnp.dot(grad_up, up_mat.T, preferred_element_t...  79.9 us
    ppermute x2, waiting for transfers between devices, from_behind(): return lax.ppermute(x, axis, pairs)  40.8 us
    dot_general x1, matrix products, body(): jnp.dot(grad_up, up_mat.T, preferred_element_type=jnp.float32)  10.2 us
  transfers between devices with their start and end apart: 6, of which 6 were waited for; matrix products, arithmetic and copies ran while one was open for 4% of the time, Pallas kernels for 0%

commit v1 on v0

--- a/solution.py
+++ b/solution.py
@@ -17,6 +17,11 @@
     return (gate * sig, sig * (1.0 + gate * (1.0 - sig)))
 
 
+def pick_rows(route, rows, bulk):
+    taken = jnp.take(rows, jnp.maximum(route - 1, 0), axis=0)
+    return jnp.where((route > 0)[:, None], taken, bulk)
+
+
 def body(
     tokens, cotangent, expert_ids, slot_index, gate_scale, gate_weight, up_weight, down_weight
 ):
@@ -32,11 +37,20 @@
     chosen = jnp.any(hit, axis=1)
     slot = jnp.sum(jnp.where(hit, slot_index[0], 0), axis=1)
     weight = jnp.sum(jnp.where(hit, gate_scale[0], jnp.float32(0.0)), axis=1)
+    route = jnp.where(chosen, slot + 1, 0).astype(jnp.int32)
+
+    tok_prev = from_behind(local, "section", 1)
+    cot_next = from_behind(grad_out, "section", -1)
+    route_prev = from_behind(route, "section", 1)
+    route_next = from_behind(route, "section", -1)
+
     places = jnp.arange(CAP, dtype=jnp.int32)
-    table = ((places[:, None] == slot[None, :]) & chosen[None, :]).astype(jnp.bfloat16)
+    mask = (places[:, None] == slot[None, :]) & chosen[None, :]
+    table = mask.astype(jnp.bfloat16)
     sent = jnp.dot(table, local, preferred_element_type=jnp.float32).astype(jnp.bfloat16)
-    carried = (weight[:, None] * grad_out.astype(jnp.float32)).astype(jnp.bfloat16)
-    back = jnp.dot(table, carried, preferred_element_type=jnp.float32).astype(jnp.bfloat16)
+    cot_sent = jnp.dot(table, grad_out, preferred_element_type=jnp.float32).astype(jnp.bfloat16)
+    wslot = jnp.sum(jnp.where(mask, weight[None, :], jnp.float32(0.0)), axis=1)
+    back = (wslot[:, None] * cot_sent.astype(jnp.float32)).astype(jnp.bfloat16)
     piece = lax.all_gather(sent, "expert", axis=0, tiled=True)
     gate_up = jnp.concatenate(
         [
@@ -71,13 +85,13 @@
         scatter_dimension=0,
         tiled=True,
     ).astype(jnp.float32)
-    output = local.astype(jnp.float32) + weight[:, None] * jnp.take(combined, slot, axis=0)
-    grad_in = grad_out.astype(jnp.float32) + jnp.where(
-        chosen[:, None], jnp.take(inward, slot, axis=0), jnp.float32(0.0)
-    )
-    next_input = from_behind(output.astype(jnp.bfloat16)[None], "section", 1)
-    prior_grad = from_behind(grad_in.astype(jnp.bfloat16)[None], "section", -1)
-    return (next_input, prior_grad)
+    out_rows = (sent.astype(jnp.float32) + wslot[:, None] * combined).astype(jnp.bfloat16)
+    grad_rows = (cot_sent.astype(jnp.float32) + inward).astype(jnp.bfloat16)
+    out_prev = from_behind(out_rows, "section", 1)
+    grad_next = from_behind(grad_rows, "section", -1)
+    next_input = pick_rows(route_prev, out_prev, tok_prev)
+    prior_grad = pick_rows(route_next, grad_next, cot_next)
+    return (next_input[None], prior_grad[None])
 
 
 def solution(mesh):

time: 468 us -> 487 us (1.041)
  waiting for transfers between devices: 381 us -> 394 us
  starting transfers between devices: 9.6 us -> 20.3 us
    ppermute x2 -> x6, waiting for transfers between devices: 40.8 us -> 124 us  [from_behind(): return lax.ppermute(x, axis, pairs)]
    reduce_scatter x1, waiting for transfers between devices: 79.9 us -> 0.01 us  [body(): lax.psum_scatter((behind + jnp.dot(grad_up, up_mat.T, preferred_element_t...]
    ppermute x2 -> x6, starting transfers between devices: 9.25 us -> 20.1 us  [from_behind(): return lax.ppermute(x, axis, pairs)]
    all_gather x1, waiting for transfers between devices: 82.7 us -> 91 us  [body(): lax.all_gather(back, 'expert', axis=0, tiled=True)]
  transfers between devices with their start and end apart: 6 -> 10, of which waited for: 6 -> 5; matrix products, arithmetic and copies ran while one was open for 4% -> 2% of each run, Pallas kernels for 0% -> 0%
where the time goes in v1:
time: 487 us; the launch traced here: 486 us
  waiting for transfers between devices  394 us (81%)
  matrix products  41.2 us (8%)
  starting transfers between devices  20.3 us (4%)
  between operations  14 us (3%)
  other arithmetic  9.68 us (2%)
  local copies, waits for them, and re-layouts  7.05 us (1%)
    ppermute x6, waiting for transfers between devices, from_behind(): return lax.ppermute(x, axis, pairs)  124 us
    all_gather x1, waiting for transfers between devices, body(): piece = lax.all_gather(sent, 'expert', axis=0, tiled=True)  93 us
    all_gather x1, waiting for transfers between devices, body(): lax.all_gather(back, 'expert', axis=0, tiled=True)  91 us
    reduce_scatter x1, waiting for transfers between devices, body(): lax.psum_scatter(jnp.dot(hidden, down_mat, preferred_element_type=jnp.flo...  86.8 us
    ppermute x6, starting transfers between devices, from_behind(): return lax.ppermute(x, axis, pairs)  20.1 us
    dot_general x1, matrix products, body(): jnp.dot(grad_up, up_mat.T, preferred_element_type=jnp.float32)  10.2 us
  transfers between devices with their start and end apart: 10, of which 5 were waited for; matrix products, arithmetic and copies ran while one was open for 2% of the time, Pallas kernels for 0%

profile of v1, /device:TPU:5, one launch (start us, length us, event | category | flops | bytes accessed | tf_op | source)
XLA Modules:
  0.0 486.4 jit_solution(13773406212519820138)
XLA Ops:
  7.2 0.0 copy-start
  7.2 0.0 all-gather.3.cloned.1.call-start
  7.2 0.8 select_reduce_fusion.1
  8.1 0.7 select_reduce_fusion.2
  8.8 2.6 convolution_convert_fusion.2
  11.4 0.0 all-gather.3.cloned.1.call-update
  11.5 0.0 reduce-scatter.3.cloned.1.call-start
  11.5 93.0 %all-gather.3.cloned.1.call-done = bf16[512,7168]{1,0:T(8,128)(2,1)} async-done(((bf16[32,7168]{1,0:T(8,128)(2,1)}), bf16[512,7168]{1,0:T(8,128)(2,1)}) %all-gather.3.cloned.1.call-update) | async-done | bytes 7340048 | tf_op jit(solution)/shard_map/all_gather | solution.py:54
  104.5 5.8 %fusion.9 = f32[512,128]{1,0:T(8,128)S(1)} fusion(bf16[512,7168]{1,0:T(8,128)(2,1)} %all-gather.3.cloned.1.call-done, bf16[1,7168,128]{2,1,0:T(8,128)(2,1)} %param.15), kind=kOutput, calls=%fused_computation.15 | convolution fusion | flops 939524096 | bytes 9437184 | tf_op jit(solution)/shard_map/dot_general | solution.py:57
  110.3 0.0 copy-done.5
  110.3 0.5 copy-done.10
  110.7 2.1 fusion.5
  112.8 0.0 copy-start.7
  112.8 0.7 copy-done.7
  113.5 0.0 copy-done
  113.5 5.0 %convolution_convert_fusion = bf16[512,7168]{1,0:T(8,128)(2,1)} fusion(bf16[1,128,7168]{2,1,0:T(8,128)(2,1)S(1)} %copy-done, f32[512,128]{1,0:T(8,128)S(1)} %fusion.5, f32[512,128]{1,0:T(8,128)S(1)} %fusion.9), kind=kOutput, calls=%fused_computation.3 | convolution fusion | flops 943587328 | bytes 9699328 | tf_op jit(solution)/shard_map/dot_general | solution.py:67
  118.5 0.0 reduce-scatter.3.cloned.1.call-update
  118.5 0.0 all-gather.5.cloned.1.call-start
  118.6 0.1 select_reduce_fusion
  118.7 86.8 %reduce-scatter.3.cloned.1.call-done = bf16[32,7168]{1,0:T(8,128)(2,1)} async-done(((bf16[512,7168]{1,0:T(8,128)(2,1)}), bf16[32,7168]{1,0:T(8,128)(2,1)}) %reduce-scatter.3.cloned.1.call-update) | async-done | bytes 458768 | tf_op jit(solution)/shard_map/reduce_scatter | solution.py:66
  205.5 2.9 multiply_convert_fusion
  208.4 0.0 all-gather.5.cloned.1.call-update
  208.5 0.0 reduce-scatter.5.cloned.1.call-start
  208.5 91.0 %all-gather.5.cloned.1.call-done = bf16[512,7168]{1,0:T(8,128)(2,1)} async-done(((bf16[32,7168]{1,0:T(8,128)(2,1)}), bf16[512,7168]{1,0:T(8,128)(2,1)}) %all-gather.5.cloned.1.call-update) | async-done | bytes 7340048 | tf_op jit(solution)/shard_map/all_gather | solution.py:73
  299.5 5.3 %fusion.1 = f32[512,128]{1,0:T(8,128)S(1)} fusion(bf16[512,7168]{1,0:T(8,128)(2,1)} %all-gather.5.cloned.1.call-done, bf16[1,128,7168]{2,1,0:T(8,128)(2,1)S(1)} %copy-done), kind=kOutput, calls=%fused_computation.7 | convolution fusion | flops 939524096 | bytes 9437184 | tf_op jit(solution)/shard_map/dot_general | solution.py:72
  304.8 0.0 copy-start.6
  304.8 7.3 %fusion.7 = f32[512,7168]{1,0:T(8,128)} fusion(bf16[1,7168,128]{2,1,0:T(8,128)(2,1)S(1)} %copy-done.4, f32[512,128]{1,0:T(8,128)S(1)} %fusion.9, f32[512,128]{1,0:T(8,128)S(1)} %fusion.1, f32[512,128]{1,0:T(8,128)S(1)} %copy-done.8), kind=kOutput, calls=%fused_computation.13 | convolution fusion | flops 940179456 | bytes 17301504 | tf_op jit(solution)/shard_map/dot_general | solution.py:79
  312.1 0.0 copy-done.6
  312.1 10.2 %add_convert_fusion = bf16[512,7168]{1,0:T(8,128)(2,1)} fusion(f32[512,7168]{1,0:T(8,128)} %fusion.7, bf16[1,7168,128]{2,1,0:T(8,128)(2,1)S(1)} %copy-done.6, f32[512,128]{1,0:T(8,128)S(1)} %fusion.1, f32[512,128]{1,0:T(8,128)S(1)} %fusion.9), kind=kOutput, calls=%fused_computation.2 | convolution fusion | flops 947257344 | bytes 24379392 | tf_op jit(solution)/shard_map/dot_general | solution.py:81
  322.3 0.0 reduce-scatter.5.cloned.1.call-update
  322.3 2.9 collective-permute-start.3
  325.2 5.2 %collective-permute-start = (s32[128]{0:T(128)S(1)}, s32[128]{0:T(128)S(1)}, u32[]{:S(2)}, u32[]{:S(2)}) collective-permute-start(s32[128]{0:T(128)S(1)} %add_select_fusion), channel_id=1, source_target_pairs={{0,16},{16,32},{32,48},{48,64},{64,80},{80,96},{96,112},{112,128},... | collective-permute-start | bytes 1544 | tf_op jit(solution)/shard_map/ppermute | solution.py:12
  330.4 2.1 collective-permute-start.5
  332.5 6.0 %collective-permute-start.2 = (bf16[128,7168]{1,0:T(8,128)(2,1)}, bf16[128,7168]{1,0:T(8,128)(2,1)}, u32[]{:S(2)}, u32[]{:S(2)}) collective-permute-start(bf16[128,7168]{1,0:T(8,128)(2,1)} %bitcast), channel_id=1, source_target_pairs={{0,16},{16,32},{32,48},{48,64},{64,80},{80,96},{96,112},{112,128},... | collective-permute-start | bytes 5505032 | tf_op jit(solution)/shard_map/ppermute | solution.py:12
  338.6 0.0 collective-permute-done.3
  338.6 0.0 collective-permute-done
  338.6 1.9 collective-permute-start.1
  340.6 115.5 %collective-permute-done.1 = bf16[32,7168]{1,0:T(8,128)(2,1)S(1)} collective-permute-done((bf16[32,7168]{1,0:T(8,128)(2,1)S(1)}, bf16[32,7168]{1,0:T(8,128)(2,1)S(1)}, u32[]{:S(2)}, u32[]{:S(2)}) %collective-permute-start.1) | collective-permute-done | bytes 458784 | tf_op jit(solution)/shard_map/ppermute | solution.py:12
  456.2 2.9 gather_fusion
  459.1 1.2 add_convert_fusion.1
  460.3 1.9 collective-permute-start.4
  462.3 0.0 collective-permute-done.2
  462.3 3.0 fusion.12
  465.3 8.0 %collective-permute-done.4 = bf16[32,7168]{1,0:T(8,128)(2,1)S(1)} collective-permute-done((bf16[32,7168]{1,0:T(8,128)(2,1)S(1)}, bf16[32,7168]{1,0:T(8,128)(2,1)S(1)}, u32[]{:S(2)}, u32[]{:S(2)}) %collective-permute-start.4) | collective-permute-done | bytes 458784 | tf_op jit(solution)/shard_map/ppermute | solution.py:12
  473.3 2.9 gather_fusion.1
  476.2 0.0 collective-permute-done.5
  476.2 3.7 fusion.11
  479.9 0.0 copy-done.1
  (22 shorter events, 0.1 us)
Async XLA Ops:
  7.2 106.3 %copy-start = (bf16[1,128,7168]{2,1,0:T(8,128)(2,1)S(1)}, bf16[1,128,7168]{2,1,0:T(8,128)(2,1)}, u32[]{:S(2)}) copy-start(bf16[1,128,7168]{2,1,0:T(8,128)(2,1)} %param.17) | copy-start | bytes 5505028
  7.2 97.3 %all-gather.3.cloned.1.call-start = ((), (), s32[]{:S(2)}) async-start(), calls=%async_computation.2 | async-start | bytes 7798784 | tf_op jit(solution)/shard_map/all_gather | solution.py:54
  11.5 194.0 %reduce-scatter.3.cloned.1.call-start = ((), (), s32[]{:S(2)}) async-start(), calls=%async_computation.3 | async-start | bytes 7798784 | tf_op jit(solution)/shard_map/reduce_scatter | solution.py:66
  104.5 5.8 %copy-start.5 = (bf16[1,7168,128]{2,1,0:T(8,128)(2,1)S(1)}, bf16[1,7168,128]{2,1,0:T(8,128)(2,1)}, u32[]{:S(2)}) copy-start(bf16[1,7168,128]{2,1,0:T(8,128)(2,1)} %param.16) | copy-start | bytes 5505028
  104.5 6.3 %copy-start.10 = (bf16[512,7168]{1,0:T(8,128)(2,1)S(1)}, bf16[512,7168]{1,0:T(8,128)(2,1)}, u32[]{:S(2)}) copy-start(bf16[512,7168]{1,0:T(8,128)(2,1)} %all-gather.3.cloned.1.call-done) | copy-start | bytes 22020100
  112.8 0.7 copy-start.7
  118.5 87.0 %copy-start.3 = (bf16[32,7168]{1,0:T(8,128)(2,1)S(1)}, bf16[32,7168]{1,0:T(8,128)(2,1)}, u32[]{:S(2)}) copy-start(bf16[32,7168]{1,0:T(8,128)(2,1)} %convolution_convert_fusion.2) | copy-start | bytes 1376260
  118.5 180.9 %all-gather.5.cloned.1.call-start = ((), (), s32[]{:S(2)}) async-start(), calls=%async_computation.4 | async-start | bytes 7798784 | tf_op jit(solution)/shard_map/all_gather | solution.py:73
  208.5 96.3 %copy-start.8 = (f32[512,128]{1,0:T(8,128)S(1)}, f32[512,128]{1,0:T(8,128)}, u32[]{:S(2)}) copy-start(f32[512,128]{1,0:T(8,128)} %copy-done.7) | copy-start | bytes 786436
  208.5 250.6 %reduce-scatter.5.cloned.1.call-start = ((), (), s32[]{:S(2)}) async-start(), calls=%async_computation.5 | async-start | bytes 7798784 | tf_op jit(solution)/shard_map/reduce_scatter | solution.py:80
  299.5 5.3 %copy-start.4 = (bf16[1,7168,128]{2,1,0:T(8,128)(2,1)S(1)}, bf16[1,7168,128]{2,1,0:T(8,128)(2,1)}, u32[]{:S(2)}) copy-start(bf16[1,7168,128]{2,1,0:T(8,128)(2,1)} %param.15) | copy-start | bytes 5505028
  304.8 7.3 %copy-start.6 = (bf16[1,7168,128]{2,1,0:T(8,128)(2,1)S(1)}, bf16[1,7168,128]{2,1,0:T(8,128)(2,1)}, u32[]{:S(2)}) copy-start(bf16[1,7168,128]{2,1,0:T(8,128)(2,1)} %param.16) | copy-start | bytes 5505028
  322.3 16.4 %copy-start.9 = (bf16[32,7168]{1,0:T(8,128)(2,1)S(1)}, bf16[32,7168]{1,0:T(8,128)(2,1)}, u32[]{:S(2)}) copy-start(bf16[32,7168]{1,0:T(8,128)(2,1)} %get-tuple-element.8) | copy-start | bytes 1376260
  322.3 16.3 %collective-permute-start.3 = (s32[128]{0:T(128)S(1)}, s32[128]{0:T(128)S(1)}, u32[]{:S(2)}, u32[]{:S(2)}) collective-permute-start(s32[128]{0:T(128)S(1)} %add_select_fusion), channel_id=1, source_target_pairs={{16,0},{32,16},{48,32},{64,48},{80,64},{96,80},{112,96},{128,112},... | collective-permute-start | bytes 1544 | tf_op jit(solution)/shard_map/ppermute | solution.py:12
  325.2 13.4 %collective-permute-start = (s32[128]{0:T(128)S(1)}, s32[128]{0:T(128)S(1)}, u32[]{:S(2)}, u32[]{:S(2)}) collective-permute-start(s32[128]{0:T(128)S(1)} %add_select_fusion), channel_id=1, source_target_pairs={{0,16},{16,32},{32,48},{48,64},{64,80},{80,96},{96,112},{112,128},... | collective-permute-start | bytes 1544 | tf_op jit(solution)/shard_map/ppermute | solution.py:12
  330.4 145.8 %collective-permute-start.5 = (bf16[128,7168]{1,0:T(8,128)(2,1)}, bf16[128,7168]{1,0:T(8,128)(2,1)}, u32[]{:S(2)}, u32[]{:S(2)}) collective-permute-start(bf16[128,7168]{1,0:T(8,128)(2,1)} %bitcast.5), channel_id=1, source_target_pairs={{16,0},{32,16},{48,32},{64,48},{80,64},{96,80},{112,96},{128,112},... | collective-permute-start | bytes 5505032 | tf_op jit(solution)/shard_map/ppermute | solution.py:12
  332.5 129.7 %collective-permute-start.2 = (bf16[128,7168]{1,0:T(8,128)(2,1)}, bf16[128,7168]{1,0:T(8,128)(2,1)}, u32[]{:S(2)}, u32[]{:S(2)}) collective-permute-start(bf16[128,7168]{1,0:T(8,128)(2,1)} %bitcast), channel_id=1, source_target_pairs={{0,16},{16,32},{32,48},{48,64},{64,80},{80,96},{96,112},{112,128},... | collective-permute-start | bytes 5505032 | tf_op jit(solution)/shard_map/ppermute | solution.py:12
  338.6 117.5 %collective-permute-start.1 = (bf16[32,7168]{1,0:T(8,128)(2,1)S(1)}, bf16[32,7168]{1,0:T(8,128)(2,1)S(1)}, u32[]{:S(2)}, u32[]{:S(2)}) collective-permute-start(bf16[32,7168]{1,0:T(8,128)(2,1)S(1)} %copy-done.9), channel_id=1, source_target_pairs={{0,16},{16,32},{32,48},{48,64},{64,80},{80,96},{96,112},{112,128},... | collective-permute-start | bytes 1376264 | tf_op jit(solution)/shard_map/ppermute | solution.py:12
  459.1 3.2 copy-start.2
  460.3 12.9 %collective-permute-start.4 = (bf16[32,7168]{1,0:T(8,128)(2,1)S(1)}, bf16[32,7168]{1,0:T(8,128)(2,1)S(1)}, u32[]{:S(2)}, u32[]{:S(2)}) collective-permute-start(bf16[32,7168]{1,0:T(8,128)(2,1)S(1)} %add_convert_fusion.1), channel_id=1, source_target_pairs={{16,0},{32,16},{48,32},{64,48},{80,64},{96,80},{112,96},{128,112},... | collective-permute-start | bytes 1376264 | tf_op jit(solution)/shard_map/ppermute | solution.py:12
  476.2 3.7 copy-start.1
Sparse Core Ops, SparseCore 0:
  11.6 92.8 all-gather.2
  118.7 86.7 reduce-scatter.2
  208.6 90.8 all-gather.4
  322.4 86.1 reduce-scatter.4

commit v2 on v1

v2 whole, which is shorter than its diff:
```python
import jax
import jax.numpy as jnp
from jax import lax
from jax.sharding import Mesh
from jax.sharding import PartitionSpec as P


CAP = 32
SWAP = [(0, 1), (1, 0)]


def from_behind(x, axis, by):
    length = lax.axis_size(axis)
    pairs = [(i, i + by) for i in range(length) if 0 <= i + by < length]
    return lax.ppermute(x, axis, pairs)


def silu_parts(gate):
    sig = jax.nn.sigmoid(gate)
    return (gate * sig, sig * (1.0 + gate * (1.0 - sig)))


def pick_rows(route, rows, bulk):
    taken = jnp.take(rows, jnp.maximum(route - 1, 0), axis=0)
    return jnp.where((route > 0)[:, None], taken, bulk)


def in_order(first, mine, other, axis):
    return jnp.where(first, jnp.stack([mine, other], axis), jnp.stack([other, mine], axis))


def gather_wide(x, first):
    own = lax.all_gather(x, "z", axis=0, tiled=True)
    other = lax.ppermute(own, "xlo", SWAP)
    zs = own.shape[0] // x.shape[0]
    rows = x.shape[0]
    both = in_order(first, own.reshape(zs, rows, -1), other.reshape(zs, rows, -1), 1)
    return both.reshape(zs * 2 * rows, -1)


def gather_narrow(x, first):
    other = lax.ppermute(x, "xlo", SWAP)
    pair = in_order(first, x, other, 0).reshape(2 * x.shape[0], -1)
    return lax.all_gather(pair, "z", axis=0, tiled=True)


def scatter_wide(q, first, rows):
    zs = q.shape[0] // (2 * rows)
    q = q.reshape(zs, 2, rows, -1)
    keep = jnp.where(first, q[:, 0], q[:, 1])
    give = jnp.where(first, q[:, 1], q[:, 0])
    got = lax.ppermute(give, "xlo", SWAP)
    total = (keep.astype(jnp.float32) + got.astype(jnp.float32)).astype(jnp.bfloat16)
    part = lax.psum_scatter(total.reshape(zs * rows, -1), "z", scatter_dimension=0, tiled=True)
    return part.astype(jnp.float32)


def scatter_narrow(q, first, rows):
    t = lax.psum_scatter(q, "z", scatter_dimension=0, tiled=True)
    t = t.reshape(2, rows, -1)
    keep = jnp.where(first, t[0], t[1])
    give = jnp.where(first, t[1], t[0])
    got = lax.ppermute(give, "xlo", SWAP)
    return keep.astype(jnp.float32) + got.astype(jnp.float32)


def body(
    tokens, cotangent, expert_ids, slot_index, gate_scale, gate_weight, up_weight, down_weight
):
    section = lax.axis_index("section")
    first = lax.axis_index("xlo") == 0
    local = tokens[0]
    grad_out = cotangent[0]
    named = expert_ids[0]
    gate_mat = gate_weight[0]
    up_mat = up_weight[0]
    down_mat = down_weight[0]
    width = local.shape[1]
    wide = (width // 7 * 4) // 128 * 128
    hit = named == section
    chosen = jnp.any(hit, axis=1)
    slot = jnp.sum(jnp.where(hit, slot_index[0], 0), axis=1)
    weight = jnp.sum(jnp.where(hit, gate_scale[0], jnp.float32(0.0)), axis=1)
    route = jnp.where(chosen, slot + 1, 0).astype(jnp.int32)

    tok_prev = from_behind(local, "section", 1)
    cot_next = from_behind(grad_out, "section", -1)
    route_prev = from_behind(route, "section", 1)
    route_next = from_behind(route, "section", -1)

    places = jnp.arange(CAP, dtype=jnp.int32)
    mask = (places[:, None] == slot[None, :]) & chosen[None, :]
    table = mask.astype(jnp.bfloat16)
    sent = jnp.dot(table, local, preferred_element_type=jnp.float32).astype(jnp.bfloat16)
    cot_sent = jnp.dot(table, grad_out, preferred_element_type=jnp.float32).astype(jnp.bfloat16)
    wslot = jnp.sum(jnp.where(mask, weight[None, :], jnp.float32(0.0)), axis=1)
    carried = (weight[:, None] * grad_out.astype(jnp.float32)).astype(jnp.bfloat16)
    back = jnp.dot(table, carried, preferred_element_type=jnp.float32).astype(jnp.bfloat16)

    sent_a = gather_wide(sent[:, :wide], first)
    back_a = gather_wide(back[:, :wide], first)
    sent_b = gather_narrow(sent[:, wide:], first)
    back_b = gather_narrow(back[:, wide:], first)

    f32 = jnp.float32
    gate = jnp.dot(sent_a, gate_mat[:wide], preferred_element_type=f32) + jnp.dot(
        sent_b, gate_mat[wide:], preferred_element_type=f32
    )
    up = jnp.dot(sent_a, up_mat[:wide], preferred_element_type=f32) + jnp.dot(
        sent_b, up_mat[wide:], preferred_element_type=f32
    )
    act, slope = silu_parts(gate)
    hidden = (act * up).astype(jnp.bfloat16)
    ahead_a = jnp.dot(hidden, down_mat[:, :wide], preferred_element_type=f32).astype(jnp.bfloat16)
    ahead_b = jnp.dot(hidden, down_mat[:, wide:], preferred_element_type=f32).astype(jnp.bfloat16)
    comb_b = scatter_narrow(ahead_b, first, CAP)
    grad_hidden = jnp.dot(back_a, down_mat[:, :wide].T, preferred_element_type=f32) + jnp.dot(
        back_b, down_mat[:, wide:].T, preferred_element_type=f32
    )
    grad_up = (grad_hidden * act).astype(jnp.bfloat16)
    grad_gate = (grad_hidden * up * slope).astype(jnp.bfloat16)
    behind_b = (
        jnp.dot(grad_gate, gate_mat[wide:].T, preferred_element_type=f32)
        + jnp.dot(grad_up, up_mat[wide:].T, preferred_element_type=f32)
    ).astype(jnp.bfloat16)
    behind_a = (
        jnp.dot(grad_gate, gate_mat[:wide].T, preferred_element_type=f32)
        + jnp.dot(grad_up, up_mat[:wide].T, preferred_element_type=f32)
    ).astype(jnp.bfloat16)
    comb_a = scatter_wide(ahead_a, first, CAP)
    inw_b = scatter_narrow(behind_b, first, CAP)
    inw_a = scatter_wide(behind_a, first, CAP)
    combined = jnp.concatenate([comb_a, comb_b], axis=1)
    inward = jnp.concatenate([inw_a, inw_b], axis=1)

    out_rows = (sent.astype(f32) + wslot[:, None] * combined).astype(jnp.bfloat16)
    grad_rows = (cot_sent.astype(f32) + inward).astype(jnp.bfloat16)
    out_prev = from_behind(out_rows, "section", 1)
    grad_next = from_behind(grad_rows, "section", -1)
    next_input = pick_rows(route_prev, out_prev, tok_prev)
    prior_grad = pick_rows(route_next, grad_next, cot_next)
    return (next_input[None], prior_grad[None])


def solution(mesh):
    sections, experts = mesh.devices.shape
    grid = Mesh(mesh.devices.reshape(sections, 2, experts // 2), ("section", "xlo", "z"))
    ex = ("xlo", "z")
    in_specs = (
        P("section", ex, None),
        P("section", ex, None),
        P("section", ex, None),
        P("section", ex, None),
        P("section", ex, None),
        P("section", None, ex),
        P("section", None, ex),
        P("section", ex, None),
    )
    out_specs = (P("section", ex, None), P("section", ex, None))

    return jax.shard_map(body, mesh=grid, in_specs=in_specs, out_specs=out_specs, check_vma=False)
```

time: 487 us -> 423 us (0.87)
  waiting for transfers between devices: 394 us -> 310 us
  other arithmetic: 9.68 us -> 23.6 us
  starting transfers between devices: 20.3 us -> 33.8 us
  matrix products: 41.2 us -> 29.4 us
    ppermute x6, waiting for transfers between devices: 124 us -> 4.07 us  [from_behind(): return lax.ppermute(x, axis, pairs)]
    ppermute x0 -> x8, waiting for transfers between devices: none -> 98.2 us  [the longest x2 89.3 us: scatter_wide(): got = lax.ppermute(give, 'xlo', SWAP)]
    reduce_scatter x2 -> x4, waiting for transfers between devices: 86.8 us -> 53.7 us  [the longest x2 53.7 us: scatter_wide(): lax.psum_scatter(total.reshape(zs * rows, -1), 'z', scatter_dimension=0,...]
    all_gather x2 -> x4, waiting for transfers between devices: 184 us -> 154 us  [the longest x2 89.2 us: gather_narrow(): return lax.all_gather(pair, 'z', axis=0, tiled=True)]
    dot_general x6 -> x13, matrix products: 35.6 us -> 25.7 us  [the longest x1 3.21 us: body(): jnp.dot(back_b, down_mat[:, wide:].T, preferred_element_type=f32)]
    select_n x0 -> x7, other arithmetic: none -> 8.04 us  [the longest x3 5.45 us: in_order(): jnp.where(first, jnp.stack([mine, other], axis), jnp.stack([other, mine],...]
    ppermute x0 -> x8, starting transfers between devices: none -> 7.62 us  [the longest x2 2 us: gather_narrow(): other = lax.ppermute(x, 'xlo', SWAP)]
    convert_element_type x1 -> x5, other arithmetic: 1.23 us -> 7.19 us  [the longest x2 5.04 us: scatter_wide(): (keep.astype(jnp.float32) + got.astype(jnp.float32)).astype(jnp.bfloat16)]
  transfers between devices with their start and end apart: 10 -> 22, of which waited for: 5 -> 12; matrix products, arithmetic and copies ran while one was open for 2% -> 10% of each run, Pallas kernels for 0% -> 0%
where the time goes in v2:
time: 423 us; the launch traced here: 418 us
  waiting for transfers between devices  310 us (73%)
  starting transfers between devices  33.8 us (8%)
  matrix products  29.4 us (7%)
  other arithmetic  23.6 us (6%)
  between operations  14.6 us (3%)
  local copies, waits for them, and re-layouts  6.81 us (2%)
    ppermute x2, waiting for transfers between devices, scatter_wide(): got = lax.ppermute(give, 'xlo', SWAP)  89.3 us
    all_gather x2, waiting for transfers between devices, gather_narrow(): return lax.all_gather(pair, 'z', axis=0, tiled=True)  89.2 us
    all_gather x2, waiting for transfers between devices, gather_wide(): own = lax.all_gather(x, 'z', axis=0, tiled=True)  64.7 us
    reduce_scatter x2, waiting for transfers between devices, scatter_wide(): lax.psum_scatter(total.reshape(zs * rows, -1), 'z', scatter_dimension=0,...  53.7 us
    ppermute x6, starting transfers between devices, from_behind(): return lax.ppermute(x, axis, pairs)  25.7 us
    ppermute x2, waiting for transfers between devices, gather_narrow(): other = lax.ppermute(x, 'xlo', SWAP)  8.89 us
  transfers between devices with their start and end apart: 22, of which 12 were waited for; matrix products, arithmetic and copies ran while one was open for 10% of the time, Pallas kernels for 0%

profile of v2, /device:TPU:5, one launch (start us, length us, event | category | flops | bytes accessed | tf_op | source)
XLA Modules:
  0.0 418.1 jit_solution(16050137974475848301)
XLA Ops:
  8.7 2.0 convolution_convert_fusion
  11.5 1.9 convolution_convert_fusion.2
  14.2 1.0 collective-permute-start.2
  15.2 4.9 %collective-permute-done.2 = bf16[32,3072]{1,0:T(8,128)(2,1)S(1)} collective-permute-done((bf16[32,3072]{1,0:T(8,128)(2,1)S(1)}, bf16[32,3072]{1,0:T(8,128)(2,1)S(1)}, u32[]{:S(2)}, u32[]{:S(2)}) %collective-permute-start.2) | collective-permute-done | bytes 196640 | tf_op jit(solution)/shard_map/ppermute | solution.py:42
  21.0 1.0 collective-permute-start.9
  22.0 4.0 collective-permute-done.9
  26.9 24.3 %all-gather.9.cloned.1.call-done = bf16[256,4096]{1,0:T(8,128)(2,1)} async-done(((bf16[32,4096]{1,0:T(8,128)(2,1)}), bf16[256,4096]{1,0:T(8,128)(2,1)}) %all-gather.9.cloned.1.call-update) | async-done | bytes 2097168 | tf_op jit(solution)/shard_map/all_gather | solution.py:33
  52.1 40.3 %all-gather.5.cloned.1.call-done = bf16[256,4096]{1,0:T(8,128)(2,1)} async-done(((bf16[32,4096]{1,0:T(8,128)(2,1)}), bf16[256,4096]{1,0:T(8,128)(2,1)}) %all-gather.5.cloned.1.call-update) | async-done | bytes 2097168 | tf_op jit(solution)/shard_map/all_gather | solution.py:33
  93.3 48.7 %all-gather.7.cloned.1.call-done = bf16[512,3072]{1,0:T(8,128)(2,1)} async-done(((bf16[64,3072]{1,0:T(8,128)(2,1)}), bf16[512,3072]{1,0:T(8,128)(2,1)}) %all-gather.7.cloned.1.call-update) | async-done | bytes 3145744 | tf_op jit(solution)/shard_map/all_gather | solution.py:44
  142.0 3.2 fusion.21
  145.2 2.1 fusion.25
  147.3 40.5 %all-gather.11.cloned.1.call-done = bf16[512,3072]{1,0:T(8,128)(2,1)} async-done(((bf16[64,3072]{1,0:T(8,128)(2,1)}), bf16[512,3072]{1,0:T(8,128)(2,1)}) %all-gather.11.cloned.1.call-update) | async-done | bytes 3145744 | tf_op jit(solution)/shard_map/all_gather | solution.py:44
  187.9 3.2 fusion.27
  191.3 3.9 maximum_select_fusion
  195.2 1.3 convolution_add_fusion.1
  196.6 1.3 convolution_add_fusion.2
  198.1 1.3 multiply_convert_fusion.2
  199.4 1.0 fusion.23
  200.4 2.6 add_convert_fusion.1
  203.3 2.6 convolution_convert_fusion.4
  206.0 2.6 fusion.8
  208.6 1.3 add_convert_fusion
  210.1 1.0 collective-permute-start.10
  211.1 45.1 %collective-permute-done.10 = bf16[8,32,4096]{2,1,0:T(8,128)(2,1)S(1)} collective-permute-done((bf16[8,32,4096]{2,1,0:T(8,128)(2,1)S(1)}, bf16[8,32,4096]{2,1,0:T(8,128)(2,1)S(1)}, u32[]{:S(2)}, u32[]{:S(2)}) %collective-permute-start.10) | collective-permute-done | bytes 2097184 | tf_op jit(solution)/shard_map/ppermute | solution.py:52
  256.2 2.4 fusion.1
  258.7 1.2 convolution_convert_fusion.3
  260.1 1.0 collective-permute-start.3
  261.1 44.2 %collective-permute-done.3 = bf16[8,32,4096]{2,1,0:T(8,128)(2,1)S(1)} collective-permute-done((bf16[8,32,4096]{2,1,0:T(8,128)(2,1)S(1)}, bf16[8,32,4096]{2,1,0:T(8,128)(2,1)S(1)}, u32[]{:S(2)}, u32[]{:S(2)}) %collective-permute-start.3) | collective-permute-done | bytes 2097184 | tf_op jit(solution)/shard_map/ppermute | solution.py:52
  305.3 2.6 fusion.2
  308.0 4.9 %collective-permute-start.7 = (s32[128]{0:T(128)S(1)}, s32[128]{0:T(128)S(1)}, u32[]{:S(2)}, u32[]{:S(2)}) collective-permute-start(s32[128]{0:T(128)S(1)} %add_select_fusion), channel_id=1, source_target_pairs={{16,0},{32,16},{48,32},{64,48},{80,64},{96,80},{112,96},{128,112},... | collective-permute-start | bytes 1544 | tf_op jit(solution)/shard_map/ppermute | solution.py:15
  312.8 3.1 collective-permute-start
  316.0 1.9 collective-permute-start.13
  317.9 6.0 %collective-permute-start.6 = (bf16[128,7168]{1,0:T(8,128)(2,1)}, bf16[128,7168]{1,0:T(8,128)(2,1)}, u32[]{:S(2)}, u32[]{:S(2)}) collective-permute-start(bf16[128,7168]{1,0:T(8,128)(2,1)} %bitcast), channel_id=1, source_target_pairs={{0,16},{16,32},{32,48},{48,64},{64,80},{80,96},{96,112},{112,128},... | collective-permute-start | bytes 5505032 | tf_op jit(solution)/shard_map/ppermute | solution.py:15
  324.1 1.1 broadcast_select_fusion
  325.2 1.8 collective-permute-start.11
  327.0 1.1 broadcast_select_fusion.1
  328.2 10.1 %reduce-scatter.9.cloned.1.call-done = bf16[32,4096]{1,0:T(8,128)(2,1)} async-done(((bf16[256,4096]{1,0:T(8,128)(2,1)}), bf16[32,4096]{1,0:T(8,128)(2,1)}) %reduce-scatter.9.cloned.1.call-update) | async-done | bytes 262160 | tf_op jit(solution)/shard_map/reduce_scatter | solution.py:54
  338.3 1.0 convert_element_type.116
  339.3 43.6 %reduce-scatter.5.cloned.1.call-done = bf16[32,4096]{1,0:T(8,128)(2,1)} async-done(((bf16[256,4096]{1,0:T(8,128)(2,1)}), bf16[32,4096]{1,0:T(8,128)(2,1)}) %reduce-scatter.5.cloned.1.call-update) | async-done | bytes 262160 | tf_op jit(solution)/shard_map/reduce_scatter | solution.py:54
  382.9 1.0 convert_element_type.99
  384.0 1.9 fusion.19
  385.9 6.6 %collective-permute-start.12 = (bf16[32,7168]{1,0:T(8,128)(2,1)S(1)}, bf16[32,7168]{1,0:T(8,128)(2,1)S(1)}, u32[]{:S(2)}, u32[]{:S(2)}) collective-permute-start(bf16[32,7168]{1,0:T(8,128)(2,1)S(1)} %fusion.19), channel_id=1, source_target_pairs={{16,0},{32,16},{48,32},{64,48},{80,64},{96,80},{112,96},{128,112},... | collective-permute-start | bytes 1376264 | tf_op jit(solution)/shard_map/ppermute | solution.py:15
  392.7 3.2 collective-permute-start.5
  396.0 3.9 collective-permute-done.12
  399.9 2.9 gather_fusion.1
  403.0 1.7 gather_fusion
  404.7 3.6 fusion.3
  408.3 3.0 fusion.4
  (70 shorter events, 8.9 us)
Async XLA Ops:
  7.2 44.0 %all-gather.9.cloned.1.call-start = ((), (), s32[]{:S(2)}) async-start(), calls=%async_computation.8 | async-start | bytes 2359296 | tf_op jit(solution)/shard_map/all_gather | solution.py:33
  11.4 81.0 %all-gather.5.cloned.1.call-start = ((), (), s32[]{:S(2)}) async-start(), calls=%async_computation.4 | async-start | bytes 2359296 | tf_op jit(solution)/shard_map/all_gather | solution.py:33
  14.1 127.9 %all-gather.7.cloned.1.call-start = ((), (), s32[]{:S(2)}) async-start(), calls=%async_computation.5 | async-start | bytes 3538944 | tf_op jit(solution)/shard_map/all_gather | solution.py:44
  14.2 5.9 %collective-permute-start.2 = (bf16[32,3072]{1,0:T(8,128)(2,1)S(1)}, bf16[32,3072]{1,0:T(8,128)(2,1)S(1)}, u32[]{:S(2)}, u32[]{:S(2)}) collective-permute-start(bf16[32,3072]{1,0:T(8,128)(2,1)S(1)} %get-tuple-element.11), channel_id=1, source_target_pairs={{0,8},{8,0},{1,9},{9,1},{2,10},{10,2},{3,11},{11,3},{4,12},{12,4},... | collective-permute-start | bytes 589832 | tf_op jit(solution)/shard_map/ppermute | solution.py:42
  20.9 167.0 %all-gather.11.cloned.1.call-start = ((), (), s32[]{:S(2)}) async-start(), calls=%async_computation.9 | async-start | bytes 3538944 | tf_op jit(solution)/shard_map/all_gather | solution.py:44
  21.0 5.0 %collective-permute-start.9 = (bf16[32,3072]{1,0:T(8,128)(2,1)S(1)}, bf16[32,3072]{1,0:T(8,128)(2,1)S(1)}, u32[]{:S(2)}, u32[]{:S(2)}) collective-permute-start(bf16[32,3072]{1,0:T(8,128)(2,1)S(1)} %get-tuple-element.9), channel_id=1, source_target_pairs={{0,8},{8,0},{1,9},{9,1},{2,10},{10,2},{3,11},{11,3},{4,12},{12,4},... | collective-permute-start | bytes 589832 | tf_op jit(solution)/shard_map/ppermute | solution.py:42
  26.8 297.3 %reduce-scatter.11.cloned.1.call-start = ((), (), s32[]{:S(2)}) async-start(), calls=%async_computation.11 | async-start | bytes 3538944 | tf_op jit(solution)/shard_map/reduce_scatter | solution.py:59
  51.2 139.9 %collective-permute-start.8 = (bf16[256,4096]{1,0:T(8,128)(2,1)}, bf16[256,4096]{1,0:T(8,128)(2,1)S(1)}, u32[]{:S(2)}, u32[]{:S(2)}) collective-permute-start(bf16[256,4096]{1,0:T(8,128)(2,1)} %all-gather.9.cloned.1.call-done), channel_id=1, source_target_pairs={{0,8},{8,0},{1,9},{9,1},{2,10},{10,2},{3,11},{11,3},{4,12},{12,4},... | collective-permute-start | bytes 6291464 | tf_op jit(solution)/shard_map/ppermute | solution.py:34
  92.4 98.7 %collective-permute-start.1 = (bf16[256,4096]{1,0:T(8,128)(2,1)}, bf16[256,4096]{1,0:T(8,128)(2,1)}, u32[]{:S(2)}, u32[]{:S(2)}) collective-permute-start(bf16[256,4096]{1,0:T(8,128)(2,1)} %all-gather.5.cloned.1.call-done), channel_id=1, source_target_pairs={{0,8},{8,0},{1,9},{9,1},{2,10},{10,2},{3,11},{11,3},{4,12},{12,4},... | collective-permute-start | bytes 6291464 | tf_op jit(solution)/shard_map/ppermute | solution.py:34
  142.0 3.2 copy-start.8
  187.9 3.2 copy-start
  187.9 3.4 copy-start.1
  191.3 3.9 copy-start.4
  195.1 1.5 copy-start.3
  196.6 1.5 copy-start.2
  203.0 124.0 %reduce-scatter.7.cloned.1.call-start = ((), (), s32[]{:S(2)}) async-start(), calls=%async_computation.7 | async-start | bytes 3538944 | tf_op jit(solution)/shard_map/reduce_scatter | solution.py:59
  205.9 132.4 %reduce-scatter.9.cloned.1.call-start = ((), (), s32[]{:S(2)}) async-start(), calls=%async_computation.10 | async-start | bytes 2359296 | tf_op jit(solution)/shard_map/reduce_scatter | solution.py:54
  206.0 2.6 copy-start.5
  210.1 46.0 %collective-permute-start.10 = (bf16[8,32,4096]{2,1,0:T(8,128)(2,1)S(1)}, bf16[8,32,4096]{2,1,0:T(8,128)(2,1)S(1)}, u32[]{:S(2)}, u32[]{:S(2)}) collective-permute-start(bf16[8,32,4096]{2,1,0:T(8,128)(2,1)S(1)} %select_bitcast_fusion), channel_id=1, source_target_pairs={{0,8},{8,0},{1,9},{9,1},{2,10},{10,2},{3,11},{11,3},{4,12},{12,4},... | collective-permute-start | bytes 6291464 | tf_op jit(solution)/shard_map/ppermute | solution.py:52
  258.6 124.3 %reduce-scatter.5.cloned.1.call-start = ((), (), s32[]{:S(2)}) async-start(), calls=%async_computation.6 | async-start | bytes 2359296 | tf_op jit(solution)/shard_map/reduce_scatter | solution.py:54
  260.1 45.2 %collective-permute-start.3 = (bf16[8,32,4096]{2,1,0:T(8,128)(2,1)S(1)}, bf16[8,32,4096]{2,1,0:T(8,128)(2,1)S(1)}, u32[]{:S(2)}, u32[]{:S(2)}) collective-permute-start(bf16[8,32,4096]{2,1,0:T(8,128)(2,1)S(1)} %select_bitcast_fusion.1), channel_id=1, source_target_pairs={{0,8},{8,0},{1,9},{9,1},{2,10},{10,2},{3,11},{11,3},{4,12},{12,4},... | collective-permute-start | bytes 6291464 | tf_op jit(solution)/shard_map/ppermute | solution.py:52
  308.0 16.1 %collective-permute-start.7 = (s32[128]{0:T(128)S(1)}, s32[128]{0:T(128)S(1)}, u32[]{:S(2)}, u32[]{:S(2)}) collective-permute-start(s32[128]{0:T(128)S(1)} %add_select_fusion), channel_id=1, source_target_pairs={{16,0},{32,16},{48,32},{64,48},{80,64},{96,80},{112,96},{128,112},... | collective-permute-start | bytes 1544 | tf_op jit(solution)/shard_map/ppermute | solution.py:15
  312.8 83.1 %collective-permute-start = (s32[128]{0:T(128)S(1)}, s32[128]{0:T(128)S(1)}, u32[]{:S(2)}, u32[]{:S(2)}) collective-permute-start(s32[128]{0:T(128)S(1)} %add_select_fusion), channel_id=1, source_target_pairs={{0,16},{16,32},{32,48},{48,64},{64,80},{80,96},{96,112},{112,128},... | collective-permute-start | bytes 1544 | tf_op jit(solution)/shard_map/ppermute | solution.py:15
  316.0 88.7 %collective-permute-start.13 = (bf16[128,7168]{1,0:T(8,128)(2,1)}, bf16[128,7168]{1,0:T(8,128)(2,1)}, u32[]{:S(2)}, u32[]{:S(2)}) collective-permute-start(bf16[128,7168]{1,0:T(8,128)(2,1)} %bitcast.21), channel_id=1, source_target_pairs={{16,0},{32,16},{48,32},{64,48},{80,64},{96,80},{112,96},{128,112},... | collective-permute-start | bytes 5505032 | tf_op jit(solution)/shard_map/ppermute | solution.py:15
  317.9 90.4 %collective-permute-start.6 = (bf16[128,7168]{1,0:T(8,128)(2,1)}, bf16[128,7168]{1,0:T(8,128)(2,1)}, u32[]{:S(2)}, u32[]{:S(2)}) collective-permute-start(bf16[128,7168]{1,0:T(8,128)(2,1)} %bitcast), channel_id=1, source_target_pairs={{0,16},{16,32},{32,48},{48,64},{64,80},{80,96},{96,112},{112,128},... | collective-permute-start | bytes 5505032 | tf_op jit(solution)/shard_map/ppermute | solution.py:15
  324.1 59.7 %copy-start.7 = (bf16[64,3072]{1,0:T(8,128)(2,1)S(1)}, bf16[64,3072]{1,0:T(8,128)(2,1)}, u32[]{:S(2)}) copy-start(bf16[64,3072]{1,0:T(8,128)(2,1)} %reduce-scatter.11.cloned.1.call-done) | copy-start | bytes 1179652
  325.2 58.6 %collective-permute-start.11 = (bf16[32,3072]{1,0:T(8,128)(2,1)S(1)}, bf16[32,3072]{1,0:T(8,128)(2,1)S(1)}, u32[]{:S(2)}, u32[]{:S(2)}) collective-permute-start(bf16[32,3072]{1,0:T(8,128)(2,1)S(1)} %broadcast_select_fusion), channel_id=1, source_target_pairs={{0,8},{8,0},{1,9},{9,1},{2,10},{10,2},{3,11},{11,3},{4,12},{12,4},... | collective-permute-start | bytes 589832 | tf_op jit(solution)/shard_map/ppermute | solution.py:63
  328.0 64.4 %collective-permute-start.4 = (bf16[32,3072]{1,0:T(8,128)(2,1)S(1)}, bf16[32,3072]{1,0:T(8,128)(2,1)S(1)}, u32[]{:S(2)}, u32[]{:S(2)}) collective-permute-start(bf16[32,3072]{1,0:T(8,128)(2,1)S(1)} %broadcast_select_fusion.1), channel_id=1, source_target_pairs={{0,8},{8,0},{1,9},{9,1},{2,10},{10,2},{3,11},{11,3},{4,12},{12,4},... | collective-permute-start | bytes 589832 | tf_op jit(solution)/shard_map/ppermute | solution.py:63
  383.8 8.6 %copy-start.6 = (bf16[64,3072]{1,0:T(8,128)(2,1)S(1)}, bf16[64,3072]{1,0:T(8,128)(2,1)}, u32[]{:S(2)}) copy-start(bf16[64,3072]{1,0:T(8,128)(2,1)} %reduce-scatter.7.cloned.1.call-done) | copy-start | bytes 1179652
  385.9 14.0 %collective-permute-start.12 = (bf16[32,7168]{1,0:T(8,128)(2,1)S(1)}, bf16[32,7168]{1,0:T(8,128)(2,1)S(1)}, u32[]{:S(2)}, u32[]{:S(2)}) collective-permute-start(bf16[32,7168]{1,0:T(8,128)(2,1)S(1)} %fusion.19), channel_id=1, source_target_pairs={{16,0},{32,16},{48,32},{64,48},{80,64},{96,80},{112,96},{128,112},... | collective-permute-start | bytes 1376264 | tf_op jit(solution)/shard_map/ppermute | solution.py:15
  392.7 10.2 %collective-permute-start.5 = (bf16[32,7168]{1,0:T(8,128)(2,1)S(1)}, bf16[32,7168]{1,0:T(8,128)(2,1)S(1)}, u32[]{:S(2)}, u32[]{:S(2)}) collective-permute-start(bf16[32,7168]{1,0:T(8,128)(2,1)S(1)} %fusion.18), channel_id=1, source_target_pairs={{0,16},{16,32},{32,48},{48,64},{64,80},{80,96},{96,112},{112,128},... | collective-permute-start | bytes 1376264 | tf_op jit(solution)/shard_map/ppermute | solution.py:15
Sparse Core Ops, SparseCore 0:
  11.6 39.5 all-gather.8
  53.0 39.4 all-gather.4
  94.8 47.1 all-gather.6
  144.2 43.5 all-gather.10
  203.2 42.9 reduce-scatter.10
  248.6 46.5 reduce-scatter.6
  297.7 40.5 reduce-scatter.8
  340.8 41.9 reduce-scatter.4

commit v3 on v1

--- a/solution.py
+++ b/solution.py
@@ -2,6 +2,7 @@
 import jax.numpy as jnp
 from jax import lax
 from jax.sharding import PartitionSpec as P
+
 
 CAP = 32
 
@@ -50,8 +51,12 @@
     sent = jnp.dot(table, local, preferred_element_type=jnp.float32).astype(jnp.bfloat16)
     cot_sent = jnp.dot(table, grad_out, preferred_element_type=jnp.float32).astype(jnp.bfloat16)
     wslot = jnp.sum(jnp.where(mask, weight[None, :], jnp.float32(0.0)), axis=1)
-    back = (wslot[:, None] * cot_sent.astype(jnp.float32)).astype(jnp.bfloat16)
-    piece = lax.all_gather(sent, "expert", axis=0, tiled=True)
+    carried = (weight[:, None] * grad_out.astype(jnp.float32)).astype(jnp.bfloat16)
+    back = jnp.dot(table, carried, preferred_element_type=jnp.float32).astype(jnp.bfloat16)
+    both = lax.all_gather(jnp.concatenate([sent, back], axis=1), "expert", axis=0, tiled=True)
+    width = local.shape[1]
+    piece = both[:, :width]
+    piece_back = both[:, width:]
     gate_up = jnp.concatenate(
         [
             jnp.dot(piece, gate_mat, preferred_element_type=jnp.float32),
@@ -63,28 +68,19 @@
     up = gate_up[:, width_local:]
     act, slope = silu_parts(gate)
     hidden = (act * up).astype(jnp.bfloat16)
-    combined = lax.psum_scatter(
-        jnp.dot(hidden, down_mat, preferred_element_type=jnp.float32).astype(jnp.bfloat16),
-        "expert",
-        scatter_dimension=0,
-        tiled=True,
-    ).astype(jnp.float32)
-    grad_hidden = jnp.dot(
-        lax.all_gather(back, "expert", axis=0, tiled=True),
-        down_mat.T,
-        preferred_element_type=jnp.float32,
-    )
+    ahead = jnp.dot(hidden, down_mat, preferred_element_type=jnp.float32).astype(jnp.bfloat16)
+    grad_hidden = jnp.dot(piece_back, down_mat.T, preferred_element_type=jnp.float32)
     grad_up = (grad_hidden * act).astype(jnp.bfloat16)
     grad_gate = (grad_hidden * up * slope).astype(jnp.bfloat16)
     behind = jnp.dot(grad_gate, gate_mat.T, preferred_element_type=jnp.float32)
-    inward = lax.psum_scatter(
-        (behind + jnp.dot(grad_up, up_mat.T, preferred_element_type=jnp.float32)).astype(
-            jnp.bfloat16
-        ),
-        "expert",
-        scatter_dimension=0,
-        tiled=True,
-    ).astype(jnp.float32)
+    behind = (behind + jnp.dot(grad_up, up_mat.T, preferred_element_type=jnp.float32)).astype(
+        jnp.bfloat16
+    )
+    sums = lax.psum_scatter(
+        jnp.concatenate([ahead, behind], axis=1), "expert", scatter_dimension=0, tiled=True
+    )
+    combined = sums[:, :width].astype(jnp.float32)
+    inward = sums[:, width:].astype(jnp.float32)
     out_rows = (sent.astype(jnp.float32) + wslot[:, None] * combined).astype(jnp.bfloat16)
     grad_rows = (cot_sent.astype(jnp.float32) + inward).astype(jnp.bfloat16)
     out_prev = from_behind(out_rows, "section", 1)
@@ -106,4 +102,5 @@
         P("section", "expert", None),
     )
     out_specs = (P("section", "expert", None), P("section", "expert", None))
+
     return jax.shard_map(body, mesh=mesh, in_specs=in_specs, out_specs=out_specs, check_vma=False)

time: 487 us -> 457 us (0.938)
  waiting for transfers between devices: 394 us -> 351 us
  other arithmetic: 9.68 us -> 21.7 us
    ppermute x6, waiting for transfers between devices: 124 us -> 37.7 us  [from_behind(): return lax.ppermute(x, axis, pairs)]
    reduce_scatter x2 -> x1, waiting for transfers between devices: 86.8 us -> 146 us  [body(): lax.psum_scatter(jnp.concatenate([ahead, behind], axis=1), 'expert', scat...]
    all_gather x2 -> x1, waiting for transfers between devices: 184 us -> 167 us  [body(): lax.all_gather(jnp.concatenate([sent, back], axis=1), 'expert', axis=0, t...]
    concatenate x0 -> x2, other arithmetic: none -> 12.9 us  [the longest x1 11.9 us: body(): jnp.concatenate([ahead, behind], axis=1)]
  transfers between devices with their start and end apart: 10 -> 8, of which waited for: 5 -> 3; matrix products, arithmetic and copies ran while one was open for 2% -> 3% of each run, Pallas kernels for 0% -> 0%
where the time goes in v3:
time: 457 us; the launch traced here: 455 us
  waiting for transfers between devices  351 us (77%)
  matrix products  38.6 us (8%)
  starting transfers between devices  24.2 us (5%)
  other arithmetic  21.7 us (5%)
  between operations  14.3 us (3%)
  local copies, waits for them, and re-layouts  5.91 us (1%)
    all_gather x1, waiting for transfers between devices, body(): lax.all_gather(jnp.concatenate([sent, back], axis=1), 'expert', axis=0, t...  167 us
    reduce_scatter x1, waiting for transfers between devices, body(): lax.psum_scatter(jnp.concatenate([ahead, behind], axis=1), 'expert', scat...  146 us
    ppermute x6, waiting for transfers between devices, from_behind(): return lax.ppermute(x, axis, pairs)  37.7 us
    ppermute x6, starting transfers between devices, from_behind(): return lax.ppermute(x, axis, pairs)  24.1 us
    concatenate x1, other arithmetic, body(): jnp.concatenate([ahead, behind], axis=1)  11.9 us
    dot_general x1, matrix products, body(): jnp.dot(grad_up, up_mat.T, preferred_element_type=jnp.float32)  10.2 us
  transfers between devices with their start and end apart: 8, of which 3 were waited for; matrix products, arithmetic and copies ran while one was open for 3% of the time, Pallas kernels for 0%

profile of v3, /device:TPU:5, one launch (start us, length us, event | category | flops | bytes accessed | tf_op | source)
XLA Modules:
  0.0 455.4 jit_solution(11774441405681659346)
XLA Ops:
  7.2 0.0 copy-start
  7.2 0.0 all-gather.2.cloned.1.call-start
  7.2 0.8 select_reduce_fusion.1
  8.1 0.7 select_reduce_fusion.2
  8.8 1.9 convolution_convert_fusion.3
  10.7 2.0 convolution_convert_fusion.2
  12.7 1.0 pad_maximum_fusion.1
  13.7 0.0 all-gather.2.cloned.1.call-update
  13.7 0.0 reduce-scatter.2.cloned.1.call-start
  13.7 166.7 %all-gather.2.cloned.1.call-done = bf16[512,14336]{1,0:T(8,128)(2,1)} async-done(((bf16[32,14336]{1,0:T(8,128)(2,1)}), bf16[512,14336]{1,0:T(8,128)(2,1)}) %all-gather.2.cloned.1.call-update) | async-done | bytes 14680080 | tf_op jit(solution)/shard_map/all_gather | solution.py:56
  180.4 5.8 %fusion.7 = f32[512,128]{1,0:T(8,128)S(1)} fusion(bf16[512,14336]{1,0:T(8,128)(2,1)} %all-gather.2.cloned.1.call-done, bf16[1,7168,128]{2,1,0:T(8,128)(2,1)} %param.15), kind=kOutput, calls=%fused_computation.15 | convolution fusion | flops 939524096 | bytes 9437184 | tf_op jit(solution)/shard_map/dot_general | solution.py:62
  186.2 0.0 copy-done.4
  186.2 0.0 slice-start.2
  186.3 5.3 %fusion.5 = f32[512,128]{1,0:T(8,128)S(1)} fusion(bf16[512,14336]{1,0:T(8,128)(2,1)} %all-gather.2.cloned.1.call-done, bf16[1,7168,128]{2,1,0:T(8,128)(2,1)S(1)} %copy-done.4), kind=kOutput, calls=%fused_computation.13 | convolution fusion | flops 939524096 | bytes 9437184 | tf_op jit(solution)/shard_map/dot_general | solution.py:63
  191.5 0.0 copy-done
  191.6 0.0 slice-start.3
  191.6 2.1 convolution_convert_fusion
  193.7 0.0 slice-done
  193.7 0.0 slice-done.1
  193.7 0.0 slice-done.2
  193.7 0.0 slice-done.3
  193.7 0.0 copy-start.3
  193.7 2.1 fusion.3
  195.8 0.0 copy-done.3
  195.8 7.3 %fusion.13 = f32[512,7168]{1,0:T(8,128)} fusion(bf16[1,7168,128]{2,1,0:T(8,128)(2,1)S(1)} %copy-done.3, f32[512,128]{1,0:T(8,128)S(1)} %fusion.7, f32[512,128]{1,0:T(8,128)S(1)} %fusion.3, f32[512,128]{1,0:T(8,128)S(1)} %fusion.5), kind=kOutput, calls=%fused_computation.22 | convolution fusion | flops 940179456 | bytes 17301504 | tf_op jit(solution)/shard_map/dot_general | solution.py:75
  203.1 10.2 %add_convert_fusion = bf16[512,7168]{1,0:T(8,128)(2,1)} fusion(f32[512,7168]{1,0:T(8,128)} %fusion.13, bf16[1,7168,128]{2,1,0:T(8,128)(2,1)S(1)} %copy-done.4, f32[512,128]{1,0:T(8,128)S(1)} %fusion.3, f32[512,128]{1,0:T(8,128)S(1)} %fusion.7), kind=kOutput, calls=%fused_computation.3 | convolution fusion | flops 947257344 | bytes 24379392 | tf_op jit(solution)/shard_map/dot_general | solution.py:76
  213.3 11.9 %pad_maximum_fusion = bf16[512,14336]{1,0:T(8,128)(2,1)} fusion(bf16[512,7168]{1,0:T(8,128)(2,1)} %add_convert_fusion, bf16[512,7168]{1,0:T(8,128)(2,1)S(1)} %convolution_convert_fusion), kind=kLoop, calls=%fused_computation.2 | loop fusion | flops 29360128 | bytes 29360128 | tf_op jit(solution)/shard_map/concatenate | solution.py:80
  225.2 0.0 reduce-scatter.2.cloned.1.call-update
  225.3 2.7 collective-permute-start.3
  228.0 5.2 %collective-permute-start = (s32[128]{0:T(128)S(1)}, s32[128]{0:T(128)S(1)}, u32[]{:S(2)}, u32[]{:S(2)}) collective-permute-start(s32[128]{0:T(128)S(1)} %add_select_fusion), channel_id=1, source_target_pairs={{0,16},{16,32},{32,48},{48,64},{64,80},{80,96},{96,112},{112,128},... | collective-permute-start | bytes 1544 | tf_op jit(solution)/shard_map/ppermute | solution.py:13
  233.2 1.9 collective-permute-start.5
  235.2 6.2 %collective-permute-start.2 = (bf16[128,7168]{1,0:T(8,128)(2,1)}, bf16[128,7168]{1,0:T(8,128)(2,1)}, u32[]{:S(2)}, u32[]{:S(2)}) collective-permute-start(bf16[128,7168]{1,0:T(8,128)(2,1)} %bitcast), channel_id=1, source_target_pairs={{0,16},{16,32},{32,48},{48,64},{64,80},{80,96},{96,112},{112,128},... | collective-permute-start | bytes 5505032 | tf_op jit(solution)/shard_map/ppermute | solution.py:13
  241.4 0.1 select_reduce_fusion
  241.5 0.0 collective-permute-done.3
  241.6 146.3 %reduce-scatter.2.cloned.1.call-done = bf16[32,14336]{1,0:T(8,128)(2,1)} async-done(((bf16[512,14336]{1,0:T(8,128)(2,1)}), bf16[32,14336]{1,0:T(8,128)(2,1)}) %reduce-scatter.2.cloned.1.call-update) | async-done | bytes 917520 | tf_op jit(solution)/shard_map/reduce_scatter | solution.py:79
  387.8 2.0 fusion.2
  389.8 2.7 collective-permute-start.4
  392.6 0.2 add_convert_fusion.1
  392.8 5.2 %collective-permute-start.1 = (bf16[32,7168]{1,0:T(8,128)(2,1)S(1)}, bf16[32,7168]{1,0:T(8,128)(2,1)S(1)}, u32[]{:S(2)}, u32[]{:S(2)}) collective-permute-start(bf16[32,7168]{1,0:T(8,128)(2,1)S(1)} %add_convert_fusion.1), channel_id=1, source_target_pairs={{0,16},{16,32},{32,48},{48,64},{64,80},{80,96},{96,112},{112,128},... | collective-permute-start | bytes 1376264 | tf_op jit(solution)/shard_map/ppermute | solution.py:13
  398.0 0.0 collective-permute-done
  398.1 37.7 %collective-permute-done.4 = bf16[32,7168]{1,0:T(8,128)(2,1)S(1)} collective-permute-done((bf16[32,7168]{1,0:T(8,128)(2,1)S(1)}, bf16[32,7168]{1,0:T(8,128)(2,1)S(1)}, u32[]{:S(2)}, u32[]{:S(2)}) %collective-permute-start.4) | collective-permute-done | bytes 458784 | tf_op jit(solution)/shard_map/ppermute | solution.py:13
  435.8 2.9 gather_fusion.1
  438.7 0.0 collective-permute-done.1
  438.7 2.9 gather_fusion
  441.7 0.0 collective-permute-done.5
  441.7 3.7 fusion.16
  445.4 0.0 collective-permute-done.2
  445.4 3.2 fusion.17
  (18 shorter events, 0.1 us)
Async XLA Ops:
  7.2 184.4 %copy-start = (bf16[1,128,7168]{2,1,0:T(8,128)(2,1)S(1)}, bf16[1,128,7168]{2,1,0:T(8,128)(2,1)}, u32[]{:S(2)}) copy-start(bf16[1,128,7168]{2,1,0:T(8,128)(2,1)} %param.17) | copy-start | bytes 5505028
  7.2 173.3 %all-gather.2.cloned.1.call-start = ((), (), s32[]{:S(2)}) async-start(), calls=%async_computation.1 | async-start | bytes 15597568 | tf_op jit(solution)/shard_map/all_gather | solution.py:56
  13.7 374.1 %reduce-scatter.2.cloned.1.call-start = ((), (), s32[]{:S(2)}) async-start(), calls=%async_computation.2 | async-start | bytes 15597568 | tf_op jit(solution)/shard_map/reduce_scatter | solution.py:79
  180.4 5.8 %copy-start.4 = (bf16[1,7168,128]{2,1,0:T(8,128)(2,1)S(1)}, bf16[1,7168,128]{2,1,0:T(8,128)(2,1)}, u32[]{:S(2)}) copy-start(bf16[1,7168,128]{2,1,0:T(8,128)(2,1)} %param.16) | copy-start | bytes 5505028
  180.4 13.2 %slice-start = ((s8[14680064]{0:T(1024)(128)(4,1)}), s8[4194304]{0:T(1024)(128)(4,1)S(1)}, s32[]{:S(2)}) async-start(s8[14680064]{0:T(1024)(128)(4,1)} %bitcast.29), calls=%async_computation.3 | async-start | bytes 8388608
  180.4 13.2 %slice-start.1 = ((s8[14680064]{0:T(1024)(128)(4,1)}), s8[4194304]{0:T(1024)(128)(4,1)S(1)}, s32[]{:S(2)}) async-start(s8[14680064]{0:T(1024)(128)(4,1)} %bitcast.29), calls=%async_computation.4 | async-start | bytes 8388608
  186.2 7.4 %slice-start.2 = ((s8[14680064]{0:T(1024)(128)(4,1)}), s8[4194304]{0:T(1024)(128)(4,1)S(1)}, s32[]{:S(2)}) async-start(s8[14680064]{0:T(1024)(128)(4,1)} %bitcast.29), calls=%async_computation.5 | async-start | bytes 8388608
  191.6 2.1 slice-start.3
  193.7 2.1 copy-start.3
  225.3 16.3 %collective-permute-start.3 = (s32[128]{0:T(128)S(1)}, s32[128]{0:T(128)S(1)}, u32[]{:S(2)}, u32[]{:S(2)}) collective-permute-start(s32[128]{0:T(128)S(1)} %add_select_fusion), channel_id=1, source_target_pairs={{16,0},{32,16},{48,32},{64,48},{80,64},{96,80},{112,96},{128,112},... | collective-permute-start | bytes 1544 | tf_op jit(solution)/shard_map/ppermute | solution.py:13
  228.0 170.0 %collective-permute-start = (s32[128]{0:T(128)S(1)}, s32[128]{0:T(128)S(1)}, u32[]{:S(2)}, u32[]{:S(2)}) collective-permute-start(s32[128]{0:T(128)S(1)} %add_select_fusion), channel_id=1, source_target_pairs={{0,16},{16,32},{32,48},{48,64},{64,80},{80,96},{96,112},{112,128},... | collective-permute-start | bytes 1544 | tf_op jit(solution)/shard_map/ppermute | solution.py:13
  233.2 208.4 %collective-permute-start.5 = (bf16[128,7168]{1,0:T(8,128)(2,1)}, bf16[128,7168]{1,0:T(8,128)(2,1)}, u32[]{:S(2)}, u32[]{:S(2)}) collective-permute-start(bf16[128,7168]{1,0:T(8,128)(2,1)} %bitcast.1), channel_id=1, source_target_pairs={{16,0},{32,16},{48,32},{64,48},{80,64},{96,80},{112,96},{128,112},... | collective-permute-start | bytes 5505032 | tf_op jit(solution)/shard_map/ppermute | solution.py:13
  235.2 210.2 %collective-permute-start.2 = (bf16[128,7168]{1,0:T(8,128)(2,1)}, bf16[128,7168]{1,0:T(8,128)(2,1)}, u32[]{:S(2)}, u32[]{:S(2)}) collective-permute-start(bf16[128,7168]{1,0:T(8,128)(2,1)} %bitcast), channel_id=1, source_target_pairs={{0,16},{16,32},{32,48},{48,64},{64,80},{80,96},{96,112},{112,128},... | collective-permute-start | bytes 5505032 | tf_op jit(solution)/shard_map/ppermute | solution.py:13
  387.8 4.8 %copy-start.5 = (bf16[32,14336]{1,0:T(8,128)(2,1)S(1)}, bf16[32,14336]{1,0:T(8,128)(2,1)}, u32[]{:S(2)}) copy-start(bf16[32,14336]{1,0:T(8,128)(2,1)} %reduce-scatter.2.cloned.1.call-done) | copy-start | bytes 2752516
  389.8 46.0 %collective-permute-start.4 = (bf16[32,7168]{1,0:T(8,128)(2,1)S(1)}, bf16[32,7168]{1,0:T(8,128)(2,1)S(1)}, u32[]{:S(2)}, u32[]{:S(2)}) collective-permute-start(bf16[32,7168]{1,0:T(8,128)(2,1)S(1)} %fusion.2), channel_id=1, source_target_pairs={{16,0},{32,16},{48,32},{64,48},{80,64},{96,80},{112,96},{128,112},... | collective-permute-start | bytes 1376264 | tf_op jit(solution)/shard_map/ppermute | solution.py:13
  392.8 46.0 %collective-permute-start.1 = (bf16[32,7168]{1,0:T(8,128)(2,1)S(1)}, bf16[32,7168]{1,0:T(8,128)(2,1)S(1)}, u32[]{:S(2)}, u32[]{:S(2)}) collective-permute-start(bf16[32,7168]{1,0:T(8,128)(2,1)S(1)} %add_convert_fusion.1), channel_id=1, source_target_pairs={{0,16},{16,32},{32,48},{48,64},{64,80},{80,96},{96,112},{112,128},... | collective-permute-start | bytes 1376264 | tf_op jit(solution)/shard_map/ppermute | solution.py:13
  441.7 3.7 copy-start.2
  445.4 3.2 copy-start.1
Sparse Core Ops, SparseCore 0:
  13.8 166.5 all-gather.1
  225.4 162.4 reduce-scatter.1

commit v4 on v3

--- a/solution.py
+++ b/solution.py
@@ -19,7 +19,9 @@
 
 
 def pick_rows(route, rows, bulk):
-    taken = jnp.take(rows, jnp.maximum(route - 1, 0), axis=0)
+    places = jnp.arange(1, rows.shape[0] + 1, dtype=jnp.int32)
+    table = (route[:, None] == places[None, :]).astype(rows.dtype)
+    taken = jnp.dot(table, rows, preferred_element_type=jnp.float32).astype(rows.dtype)
     return jnp.where((route > 0)[:, None], taken, bulk)
 
 
@@ -53,10 +55,8 @@
     wslot = jnp.sum(jnp.where(mask, weight[None, :], jnp.float32(0.0)), axis=1)
     carried = (weight[:, None] * grad_out.astype(jnp.float32)).astype(jnp.bfloat16)
     back = jnp.dot(table, carried, preferred_element_type=jnp.float32).astype(jnp.bfloat16)
-    both = lax.all_gather(jnp.concatenate([sent, back], axis=1), "expert", axis=0, tiled=True)
-    width = local.shape[1]
-    piece = both[:, :width]
-    piece_back = both[:, width:]
+    piece = lax.all_gather(sent, "expert", axis=0, tiled=True)
+    piece_back = lax.all_gather(back, "expert", axis=0, tiled=True)
     gate_up = jnp.concatenate(
         [
             jnp.dot(piece, gate_mat, preferred_element_type=jnp.float32),
@@ -69,6 +69,8 @@
     act, slope = silu_parts(gate)
     hidden = (act * up).astype(jnp.bfloat16)
     ahead = jnp.dot(hidden, down_mat, preferred_element_type=jnp.float32).astype(jnp.bfloat16)
+    combined = lax.psum_scatter(ahead, "expert", scatter_dimension=0, tiled=True)
+    combined = combined.astype(jnp.float32)
     grad_hidden = jnp.dot(piece_back, down_mat.T, preferred_element_type=jnp.float32)
     grad_up = (grad_hidden * act).astype(jnp.bfloat16)
     grad_gate = (grad_hidden * up * slope).astype(jnp.bfloat16)
@@ -76,11 +78,8 @@
     behind = (behind + jnp.dot(grad_up, up_mat.T, preferred_element_type=jnp.float32)).astype(
         jnp.bfloat16
     )
-    sums = lax.psum_scatter(
-        jnp.concatenate([ahead, behind], axis=1), "expert", scatter_dimension=0, tiled=True
-    )
-    combined = sums[:, :width].astype(jnp.float32)
-    inward = sums[:, width:].astype(jnp.float32)
+    inward = lax.psum_scatter(behind, "expert", scatter_dimension=0, tiled=True)
+    inward = inward.astype(jnp.float32)
     out_rows = (sent.astype(jnp.float32) + wslot[:, None] * combined).astype(jnp.bfloat16)
     grad_rows = (cot_sent.astype(jnp.float32) + inward).astype(jnp.bfloat16)
     out_prev = from_behind(out_rows, "section", 1)

time: 457 us -> 445 us (0.974)
  other arithmetic: 21.7 us -> 2.92 us
  matrix products: 38.6 us -> 51.2 us
  waiting for transfers between devices: 351 us -> 341 us
  starting transfers between devices: 24.2 us -> 32.2 us
  local copies, waits for them, and re-layouts: 5.91 us -> 0.46 us
    ppermute x6, waiting for transfers between devices: 37.7 us -> 22.4 us  [from_behind(): return lax.ppermute(x, axis, pairs)]
    concatenate x2 -> x0, other arithmetic: 12.9 us -> none  [the longest x1 11.9 us: body(): jnp.concatenate([ahead, behind], axis=1)]
    ppermute x6, starting transfers between devices: 24.1 us -> 32.1 us  [from_behind(): return lax.ppermute(x, axis, pairs)]
    broadcast_in_dim x2 -> x0, other arithmetic: 6.86 us -> none  [body(): return (next_input[None], prior_grad[None])]
    dot_general x0 -> x2, matrix products: none -> 6.83 us  [pick_rows(): jnp.dot(table, rows, preferred_element_type=jnp.float32).astype(rows.dtype)]
    all_gather x1 -> x2, waiting for transfers between devices: 167 us -> 173 us  [the longest x1 90.1 us: body(): piece = lax.all_gather(sent, 'expert', axis=0, tiled=True)]
    gather x2 -> x0, local copies, waits for them, and re-layouts: 5.86 us -> none  [pick_rows(): taken = jnp.take(rows, jnp.maximum(route - 1, 0), axis=0)]
    reduce_scatter x1 -> x2, waiting for transfers between devices: 146 us -> 146 us  [the longest x1 82.8 us: body(): lax.psum_scatter(ahead, 'expert', scatter_dimension=0, tiled=True)]
  transfers between devices with their start and end apart: 8 -> 10, of which waited for: 3 -> 6; matrix products, arithmetic and copies ran while one was open for 3% -> 5% of each run, Pallas kernels for 0% -> 0%
where the time goes in v4:
time: 445 us; the launch traced here: 442 us
  waiting for transfers between devices  341 us (77%)
  matrix products  51.2 us (12%)
  starting transfers between devices  32.2 us (7%)
  between operations  13.9 us (3%)
    all_gather x1, waiting for transfers between devices, body(): piece = lax.all_gather(sent, 'expert', axis=0, tiled=True)  90.1 us
    reduce_scatter x1, waiting for transfers between devices, body(): lax.psum_scatter(ahead, 'expert', scatter_dimension=0, tiled=True)  82.8 us
    all_gather x1, waiting for transfers between devices, body(): piece_back = lax.all_gather(back, 'expert', axis=0, tiled=True)  82.7 us
    reduce_scatter x1, waiting for transfers between devices, body(): inward = lax.psum_scatter(behind, 'expert', scatter_dimension=0, tiled=True)  63.3 us
    ppermute x6, starting transfers between devices, from_behind(): return lax.ppermute(x, axis, pairs)  32.1 us
    ppermute x6, waiting for transfers between devices, from_behind(): return lax.ppermute(x, axis, pairs)  22.4 us
    dot_general x1, matrix products, body(): jnp.dot(grad_up, up_mat.T, preferred_element_type=jnp.float32)  10.2 us
  transfers between devices with their start and end apart: 10, of which 6 were waited for; matrix products, arithmetic and copies ran while one was open for 5% of the time, Pallas kernels for 0%

profile of v4, /device:TPU:5, one launch (start us, length us, event | category | flops | bytes accessed | tf_op | source)
XLA Modules:
  0.0 442.1 jit_solution(2259747368383165389)
XLA Ops:
  7.2 0.0 copy-start
  7.2 0.0 all-gather.3.cloned.1.call-start
  7.2 0.8 select_reduce_fusion.1
  8.1 0.7 select_reduce_fusion.2
  8.8 2.6 convolution_convert_fusion.5
  11.4 0.0 all-gather.3.cloned.1.call-update
  11.5 0.0 all-gather.5.cloned.1.call-start
  11.5 2.8 convolution_convert_fusion.3
  14.3 0.0 all-gather.5.cloned.1.call-update
  14.3 0.0 reduce-scatter.5.cloned.1.call-start
  14.4 90.1 %all-gather.3.cloned.1.call-done = bf16[512,7168]{1,0:T(8,128)(2,1)} async-done(((bf16[32,7168]{1,0:T(8,128)(2,1)}), bf16[512,7168]{1,0:T(8,128)(2,1)}) %all-gather.3.cloned.1.call-update) | async-done | bytes 7340048 | tf_op jit(solution)/shard_map/all_gather | solution.py:58
  104.5 0.0 copy-done
  104.5 0.0 copy-start.2
  104.5 5.3 %fusion.11 = f32[512,128]{1,0:T(8,128)S(1)} fusion(bf16[512,7168]{1,0:T(8,128)(2,1)} %all-gather.3.cloned.1.call-done, bf16[1,7168,128]{2,1,0:T(8,128)(2,1)S(1)} %copy-done), kind=kOutput, calls=%fused_computation.19 | convolution fusion | flops 939524096 | bytes 9437184 | tf_op jit(solution)/shard_map/dot_general | solution.py:62
  109.8 0.0 copy-done.2
  109.8 0.4 copy-done.4
  110.2 2.1 fusion.7
  112.3 82.7 %all-gather.5.cloned.1.call-done = bf16[512,7168]{1,0:T(8,128)(2,1)} async-done(((bf16[32,7168]{1,0:T(8,128)(2,1)}), bf16[512,7168]{1,0:T(8,128)(2,1)}) %all-gather.5.cloned.1.call-update) | async-done | bytes 7340048 | tf_op jit(solution)/shard_map/all_gather | solution.py:59
  195.0 5.6 %fusion.3 = f32[512,128]{1,0:T(8,128)S(1)} fusion(bf16[512,7168]{1,0:T(8,128)(2,1)} %all-gather.5.cloned.1.call-done, bf16[1,128,7168]{2,1,0:T(8,128)(2,1)} %param.15), kind=kOutput, calls=%fused_computation.11 | convolution fusion | flops 939524096 | bytes 9437184 | tf_op jit(solution)/shard_map/dot_general | solution.py:74
  200.6 0.0 copy-start.3
  200.6 7.3 %fusion.9 = f32[512,7168]{1,0:T(8,128)} fusion(bf16[1,7168,128]{2,1,0:T(8,128)(2,1)S(1)} %copy-done, f32[512,128]{1,0:T(8,128)S(1)} %fusion.11, f32[512,128]{1,0:T(8,128)S(1)} %fusion.3, f32[512,128]{1,0:T(8,128)S(1)} %fusion.7), kind=kOutput, calls=%fused_computation.17 | convolution fusion | flops 940179456 | bytes 17301504 | tf_op jit(solution)/shard_map/dot_general | solution.py:77
  207.9 0.0 copy-done.3
  207.9 10.2 %add_convert_fusion = bf16[512,7168]{1,0:T(8,128)(2,1)} fusion(f32[512,7168]{1,0:T(8,128)} %fusion.9, bf16[1,7168,128]{2,1,0:T(8,128)(2,1)S(1)} %copy-done.3, f32[512,128]{1,0:T(8,128)S(1)} %fusion.3, f32[512,128]{1,0:T(8,128)S(1)} %fusion.11), kind=kOutput, calls=%fused_computation | convolution fusion | flops 947257344 | bytes 24379392 | tf_op jit(solution)/shard_map/dot_general | solution.py:78
  218.1 0.0 reduce-scatter.5.cloned.1.call-update
  218.1 0.0 reduce-scatter.3.cloned.1.call-start
  218.2 6.5 %convolution_convert_fusion = bf16[512,7168]{1,0:T(8,128)(2,1)} fusion(bf16[1,128,7168]{2,1,0:T(8,128)(2,1)} %param.15, f32[512,128]{1,0:T(8,128)S(1)} %fusion.7, f32[512,128]{1,0:T(8,128)S(1)} %fusion.11), kind=kOutput, calls=%fused_computation.1 | convolution fusion | flops 943587328 | bytes 9699328 | tf_op jit(solution)/shard_map/dot_general | solution.py:71
  224.7 0.0 reduce-scatter.3.cloned.1.call-update
  224.7 0.0 copy-start.1
  224.8 2.9 collective-permute-start.3
  227.7 5.2 %collective-permute-start = (s32[128]{0:T(128)S(1)}, s32[128]{0:T(128)S(1)}, u32[]{:S(2)}, u32[]{:S(2)}) collective-permute-start(s32[128]{0:T(128)S(1)} %add_select_fusion), channel_id=1, source_target_pairs={{0,16},{16,32},{32,48},{48,64},{64,80},{80,96},{96,112},{112,128},... | collective-permute-start | bytes 1544 | tf_op jit(solution)/shard_map/ppermute | solution.py:13
  232.9 1.9 collective-permute-start.5
  234.8 6.0 %collective-permute-start.2 = (bf16[128,7168]{1,0:T(8,128)(2,1)}, bf16[128,7168]{1,0:T(8,128)(2,1)}, u32[]{:S(2)}, u32[]{:S(2)}) collective-permute-start(bf16[128,7168]{1,0:T(8,128)(2,1)} %bitcast.35), channel_id=1, source_target_pairs={{0,16},{16,32},{32,48},{48,64},{64,80},{80,96},{96,112},{112,128},... | collective-permute-start | bytes 5505032 | tf_op jit(solution)/shard_map/ppermute | solution.py:13
  240.9 0.1 select_reduce_fusion
  241.0 0.0 collective-permute-done.3
  241.0 63.3 %reduce-scatter.5.cloned.1.call-done = bf16[32,7168]{1,0:T(8,128)(2,1)} async-done(((bf16[512,7168]{1,0:T(8,128)(2,1)}), bf16[32,7168]{1,0:T(8,128)(2,1)}) %reduce-scatter.5.cloned.1.call-update) | async-done | bytes 458768 | tf_op jit(solution)/shard_map/reduce_scatter | solution.py:81
  304.3 1.9 fusion.2
  306.3 7.2 %collective-permute-start.4 = (bf16[32,7168]{1,0:T(8,128)(2,1)S(1)}, bf16[32,7168]{1,0:T(8,128)(2,1)S(1)}, u32[]{:S(2)}, u32[]{:S(2)}) collective-permute-start(bf16[32,7168]{1,0:T(8,128)(2,1)S(1)} %fusion.2), channel_id=1, source_target_pairs={{16,0},{32,16},{48,32},{64,48},{80,64},{96,80},{112,96},{128,112},... | collective-permute-start | bytes 1376264 | tf_op jit(solution)/shard_map/ppermute | solution.py:13
  313.5 82.8 %reduce-scatter.3.cloned.1.call-done = bf16[32,7168]{1,0:T(8,128)(2,1)} async-done(((bf16[512,7168]{1,0:T(8,128)(2,1)}), bf16[32,7168]{1,0:T(8,128)(2,1)}) %reduce-scatter.3.cloned.1.call-update) | async-done | bytes 458768 | tf_op jit(solution)/shard_map/reduce_scatter | solution.py:72
  396.2 0.0 copy-done.1
  396.2 1.2 add_convert_fusion.1
  397.5 8.8 %collective-permute-start.1 = (bf16[32,7168]{1,0:T(8,128)(2,1)S(1)}, bf16[32,7168]{1,0:T(8,128)(2,1)S(1)}, u32[]{:S(2)}, u32[]{:S(2)}) collective-permute-start(bf16[32,7168]{1,0:T(8,128)(2,1)S(1)} %add_convert_fusion.1), channel_id=1, source_target_pairs={{0,16},{16,32},{32,48},{48,64},{64,80},{80,96},{96,112},{112,128},... | collective-permute-start | bytes 1376264 | tf_op jit(solution)/shard_map/ppermute | solution.py:13
  406.3 0.0 collective-permute-done
  406.3 12.7 %collective-permute-done.5 = bf16[128,7168]{1,0:T(8,128)(2,1)} collective-permute-done((bf16[128,7168]{1,0:T(8,128)(2,1)}, bf16[128,7168]{1,0:T(8,128)(2,1)}, u32[]{:S(2)}, u32[]{:S(2)}) %collective-permute-start.5) | collective-permute-done | bytes 1835040 | tf_op jit(solution)/shard_map/ppermute | solution.py:13
  419.0 9.7 %collective-permute-done.4 = bf16[32,7168]{1,0:T(8,128)(2,1)S(1)} collective-permute-done((bf16[32,7168]{1,0:T(8,128)(2,1)S(1)}, bf16[32,7168]{1,0:T(8,128)(2,1)S(1)}, u32[]{:S(2)}, u32[]{:S(2)}) %collective-permute-start.4) | collective-permute-done | bytes 458784 | tf_op jit(solution)/shard_map/ppermute | solution.py:13
  428.7 3.4 select_bitcast_fusion
  432.1 0.0 collective-permute-done.2
  432.1 0.0 collective-permute-done.1
  432.1 3.4 select_bitcast_fusion.1
  (6 shorter events, 0.0 us)
Async XLA Ops:
  7.2 97.3 %copy-start = (bf16[1,7168,128]{2,1,0:T(8,128)(2,1)S(1)}, bf16[1,7168,128]{2,1,0:T(8,128)(2,1)}, u32[]{:S(2)}) copy-start(bf16[1,7168,128]{2,1,0:T(8,128)(2,1)} %param.13) | copy-start | bytes 5505028
  7.2 97.3 %all-gather.3.cloned.1.call-start = ((), (), s32[]{:S(2)}) async-start(), calls=%async_computation.2 | async-start | bytes 7798784 | tf_op jit(solution)/shard_map/all_gather | solution.py:58
  11.5 183.5 %all-gather.5.cloned.1.call-start = ((), (), s32[]{:S(2)}) async-start(), calls=%async_computation.4 | async-start | bytes 7798784 | tf_op jit(solution)/shard_map/all_gather | solution.py:59
  14.3 290.0 %reduce-scatter.5.cloned.1.call-start = ((), (), s32[]{:S(2)}) async-start(), calls=%async_computation.5 | async-start | bytes 7798784 | tf_op jit(solution)/shard_map/reduce_scatter | solution.py:81
  104.5 5.3 %copy-start.2 = (bf16[1,7168,128]{2,1,0:T(8,128)(2,1)S(1)}, bf16[1,7168,128]{2,1,0:T(8,128)(2,1)}, u32[]{:S(2)}) copy-start(bf16[1,7168,128]{2,1,0:T(8,128)(2,1)} %param.14) | copy-start | bytes 5505028
  104.5 5.7 %copy-start.4 = (bf16[512,7168]{1,0:T(8,128)(2,1)S(1)}, bf16[512,7168]{1,0:T(8,128)(2,1)}, u32[]{:S(2)}) copy-start(bf16[512,7168]{1,0:T(8,128)(2,1)} %all-gather.3.cloned.1.call-done) | copy-start | bytes 22020100
  200.6 7.3 %copy-start.3 = (bf16[1,7168,128]{2,1,0:T(8,128)(2,1)S(1)}, bf16[1,7168,128]{2,1,0:T(8,128)(2,1)}, u32[]{:S(2)}) copy-start(bf16[1,7168,128]{2,1,0:T(8,128)(2,1)} %param.14) | copy-start | bytes 5505028
  218.1 178.1 %reduce-scatter.3.cloned.1.call-start = ((), (), s32[]{:S(2)}) async-start(), calls=%async_computation.3 | async-start | bytes 7798784 | tf_op jit(solution)/shard_map/reduce_scatter | solution.py:72
  224.7 171.5 %copy-start.1 = (bf16[32,7168]{1,0:T(8,128)(2,1)S(1)}, bf16[32,7168]{1,0:T(8,128)(2,1)}, u32[]{:S(2)}) copy-start(bf16[32,7168]{1,0:T(8,128)(2,1)} %convolution_convert_fusion.5) | copy-start | bytes 1376260
  224.8 16.2 %collective-permute-start.3 = (s32[128]{0:T(128)S(1)}, s32[128]{0:T(128)S(1)}, u32[]{:S(2)}, u32[]{:S(2)}) collective-permute-start(s32[128]{0:T(128)S(1)} %add_select_fusion), channel_id=1, source_target_pairs={{16,0},{32,16},{48,32},{64,48},{80,64},{96,80},{112,96},{128,112},... | collective-permute-start | bytes 1544 | tf_op jit(solution)/shard_map/ppermute | solution.py:13
  227.7 178.6 %collective-permute-start = (s32[128]{0:T(128)S(1)}, s32[128]{0:T(128)S(1)}, u32[]{:S(2)}, u32[]{:S(2)}) collective-permute-start(s32[128]{0:T(128)S(1)} %add_select_fusion), channel_id=1, source_target_pairs={{0,16},{16,32},{32,48},{48,64},{64,80},{80,96},{96,112},{112,128},... | collective-permute-start | bytes 1544 | tf_op jit(solution)/shard_map/ppermute | solution.py:13
  232.9 186.1 %collective-permute-start.5 = (bf16[128,7168]{1,0:T(8,128)(2,1)}, bf16[128,7168]{1,0:T(8,128)(2,1)}, u32[]{:S(2)}, u32[]{:S(2)}) collective-permute-start(bf16[128,7168]{1,0:T(8,128)(2,1)} %bitcast.34), channel_id=1, source_target_pairs={{16,0},{32,16},{48,32},{64,48},{80,64},{96,80},{112,96},{128,112},... | collective-permute-start | bytes 5505032 | tf_op jit(solution)/shard_map/ppermute | solution.py:13
  234.8 197.3 %collective-permute-start.2 = (bf16[128,7168]{1,0:T(8,128)(2,1)}, bf16[128,7168]{1,0:T(8,128)(2,1)}, u32[]{:S(2)}, u32[]{:S(2)}) collective-permute-start(bf16[128,7168]{1,0:T(8,128)(2,1)} %bitcast.35), channel_id=1, source_target_pairs={{0,16},{16,32},{32,48},{48,64},{64,80},{80,96},{96,112},{112,128},... | collective-permute-start | bytes 5505032 | tf_op jit(solution)/shard_map/ppermute | solution.py:13
  306.3 122.5 %collective-permute-start.4 = (bf16[32,7168]{1,0:T(8,128)(2,1)S(1)}, bf16[32,7168]{1,0:T(8,128)(2,1)S(1)}, u32[]{:S(2)}, u32[]{:S(2)}) collective-permute-start(bf16[32,7168]{1,0:T(8,128)(2,1)S(1)} %fusion.2), channel_id=1, source_target_pairs={{16,0},{32,16},{48,32},{64,48},{80,64},{96,80},{112,96},{128,112},... | collective-permute-start | bytes 1376264 | tf_op jit(solution)/shard_map/ppermute | solution.py:13
  397.5 34.7 %collective-permute-start.1 = (bf16[32,7168]{1,0:T(8,128)(2,1)S(1)}, bf16[32,7168]{1,0:T(8,128)(2,1)S(1)}, u32[]{:S(2)}, u32[]{:S(2)}) collective-permute-start(bf16[32,7168]{1,0:T(8,128)(2,1)S(1)} %add_convert_fusion.1), channel_id=1, source_target_pairs={{0,16},{16,32},{32,48},{48,64},{64,80},{80,96},{96,112},{112,128},... | collective-permute-start | bytes 1376264 | tf_op jit(solution)/shard_map/ppermute | solution.py:13
Sparse Core Ops, SparseCore 0:
  11.6 92.8 all-gather.2
  106.8 88.0 all-gather.4
  218.2 86.0 reduce-scatter.4
  306.7 89.4 reduce-scatter.2

commit v5 on v2

--- a/solution.py
+++ b/solution.py
@@ -21,7 +21,9 @@
 
 
 def pick_rows(route, rows, bulk):
-    taken = jnp.take(rows, jnp.maximum(route - 1, 0), axis=0)
+    places = jnp.arange(1, rows.shape[0] + 1, dtype=jnp.int32)
+    table = (route[:, None] == places[None, :]).astype(rows.dtype)
+    taken = jnp.dot(table, rows, preferred_element_type=jnp.float32).astype(rows.dtype)
     return jnp.where((route > 0)[:, None], taken, bulk)
 
 
@@ -97,10 +99,11 @@
     carried = (weight[:, None] * grad_out.astype(jnp.float32)).astype(jnp.bfloat16)
     back = jnp.dot(table, carried, preferred_element_type=jnp.float32).astype(jnp.bfloat16)
 
-    sent_a = gather_wide(sent[:, :wide], first)
-    back_a = gather_wide(back[:, :wide], first)
-    sent_b = gather_narrow(sent[:, wide:], first)
-    back_b = gather_narrow(back[:, wide:], first)
+    narrow = width - wide
+    both_a = gather_wide(jnp.concatenate([sent[:, :wide], back[:, :wide]], axis=1), first)
+    both_b = gather_narrow(jnp.concatenate([sent[:, wide:], back[:, wide:]], axis=1), first)
+    sent_a, back_a = both_a[:, :wide], both_a[:, wide:]
+    sent_b, back_b = both_b[:, :narrow], both_b[:, narrow:]
 
     f32 = jnp.float32
     gate = jnp.dot(sent_a, gate_mat[:wide], preferred_element_type=f32) + jnp.dot(

time: 423 us -> 389 us (0.920)
  waiting for transfers between devices: 310 us -> 285 us
  local copies, waits for them, and re-layouts: 6.81 us -> 1.05 us
    all_gather x2 -> x1, waiting for transfers between devices: 64.7 us -> 46.3 us  [gather_wide(): own = lax.all_gather(x, 'z', axis=0, tiled=True)]
    all_gather x2 -> x1, waiting for transfers between devices: 89.2 us -> 74.5 us  [gather_narrow(): return lax.all_gather(pair, 'z', axis=0, tiled=True)]
    ppermute x2 -> x1, waiting for transfers between devices: 0.01 us -> 8.96 us  [gather_wide(): other = lax.ppermute(own, 'xlo', SWAP)]
    dot_general x0 -> x2, matrix products: none -> 6.83 us  [pick_rows(): jnp.dot(table, rows, preferred_element_type=jnp.float32).astype(rows.dtype)]
    broadcast_in_dim x2 -> x0, other arithmetic: 6.59 us -> none  [body(): return (next_input[None], prior_grad[None])]
    gather x2 -> x0, local copies, waits for them, and re-layouts: 4.63 us -> none  [pick_rows(): taken = jnp.take(rows, jnp.maximum(route - 1, 0), axis=0)]
    ppermute x2 -> x1, waiting for transfers between devices: 8.89 us -> 9.08 us  [gather_narrow(): other = lax.ppermute(x, 'xlo', SWAP)]
  transfers between devices with their start and end apart: 22 -> 18, of which waited for: 12 -> 9; matrix products, arithmetic and copies ran while one was open for 10% -> 8% of each run, Pallas kernels for 0% -> 0%
where the time goes in v5:
time: 389 us; the launch traced here: 385 us
  waiting for transfers between devices  285 us (73%)
  starting transfers between devices  32 us (8%)
  matrix products  31.3 us (8%)
  other arithmetic  21.3 us (5%)
  between operations  14.5 us (4%)
    ppermute x2, waiting for transfers between devices, scatter_wide(): got = lax.ppermute(give, 'xlo', SWAP)  88.4 us
    all_gather x1, waiting for transfers between devices, gather_narrow(): return lax.all_gather(pair, 'z', axis=0, tiled=True)  74.5 us
    reduce_scatter x2, waiting for transfers between devices, scatter_wide(): lax.psum_scatter(total.reshape(zs * rows, -1), 'z', scatter_dimension=0,...  52.8 us
    all_gather x1, waiting for transfers between devices, gather_wide(): own = lax.all_gather(x, 'z', axis=0, tiled=True)  46.3 us
    ppermute x6, starting transfers between devices, from_behind(): return lax.ppermute(x, axis, pairs)  26 us
    ppermute x1, waiting for transfers between devices, gather_narrow(): other = lax.ppermute(x, 'xlo', SWAP)  9.08 us
    ppermute x1, waiting for transfers between devices, gather_wide(): other = lax.ppermute(own, 'xlo', SWAP)  8.96 us
  transfers between devices with their start and end apart: 18, of which 9 were waited for; matrix products, arithmetic and copies ran while one was open for 8% of the time, Pallas kernels for 0%

profile of v5, /device:TPU:5, one launch (start us, length us, event | category | flops | bytes accessed | tf_op | source)
XLA Modules:
  0.0 384.8 jit_solution(11544573245350840175)
XLA Ops:
  7.2 0.8 select_reduce_fusion.1
  8.1 0.7 select_reduce_fusion.2
  8.8 2.0 convolution_convert_fusion.3
  11.2 0.8 pad_maximum_fusion
  12.3 1.0 collective-permute-start.2
  13.3 9.1 %collective-permute-done.2 = bf16[32,6144]{1,0:T(8,128)(2,1)S(1)} collective-permute-done((bf16[32,6144]{1,0:T(8,128)(2,1)S(1)}, bf16[32,6144]{1,0:T(8,128)(2,1)S(1)}, u32[]{:S(2)}, u32[]{:S(2)}) %collective-permute-start.2) | collective-permute-done | bytes 393248 | tf_op jit(solution)/shard_map/ppermute | solution.py:44
  22.3 1.0 maximum_select_fusion.1
  23.4 46.3 %all-gather.3.cloned.1.call-done = bf16[256,8192]{1,0:T(8,128)(2,1)} async-done(((bf16[32,8192]{1,0:T(8,128)(2,1)}), bf16[256,8192]{1,0:T(8,128)(2,1)}) %all-gather.3.cloned.1.call-update) | async-done | bytes 4194320 | tf_op jit(solution)/shard_map/all_gather | solution.py:35
  69.8 0.9 collective-permute-start.1
  70.7 74.5 %all-gather.5.cloned.1.call-done = bf16[512,6144]{1,0:T(8,128)(2,1)} async-done(((bf16[64,6144]{1,0:T(8,128)(2,1)}), bf16[512,6144]{1,0:T(8,128)(2,1)}) %all-gather.5.cloned.1.call-update) | async-done | bytes 6291472 | tf_op jit(solution)/shard_map/all_gather | solution.py:46
  145.2 3.2 fusion.11
  148.4 0.8 copy-done.8
  149.1 2.2 fusion.13
  151.4 1.0 fusion.9
  152.4 9.0 %collective-permute-done.1 = bf16[256,8192]{1,0:T(8,128)(2,1)} collective-permute-done((bf16[256,8192]{1,0:T(8,128)(2,1)}, bf16[256,8192]{1,0:T(8,128)(2,1)}, u32[]{:S(2)}, u32[]{:S(2)}) %collective-permute-start.1) | collective-permute-done | bytes 4194336 | tf_op jit(solution)/shard_map/ppermute | solution.py:36
  161.4 5.4 %maximum_select_fusion = bf16[8,2,32,8192]{3,2,1,0:T(8,128)(2,1)S(1)} fusion(bf16[8,1,32,8192]{3,2,1,0:T(8,128)(2,1)} %bitcast.5, bf16[8,1,32,8192]{3,2,1,0:T(8,128)(2,1)S(1)} %bitcast.104, pred[]{:T(512)S(6)} %eq.57), kind=kLoop, calls=%fused_computation.2 | loop fusion | flops 12582912 | bytes 16777216 | tf_op jit(solution)/shard_map/jit(_where)/select_n | solution.py:31
  166.8 1.3 fusion.19
  168.3 1.3 fusion.16
  169.6 1.3 multiply_convert_fusion.2
  170.9 1.0 fusion.41
  171.9 2.7 add_convert_fusion.1
  174.6 2.6 convolution_convert_fusion.6
  177.5 2.6 fusion.27
  180.1 1.3 add_convert_fusion
  181.6 1.0 collective-permute-start.8
  182.6 44.6 %collective-permute-done.8 = bf16[8,32,4096]{2,1,0:T(8,128)(2,1)S(1)} collective-permute-done((bf16[8,32,4096]{2,1,0:T(8,128)(2,1)S(1)}, bf16[8,32,4096]{2,1,0:T(8,128)(2,1)S(1)}, u32[]{:S(2)}, u32[]{:S(2)}) %collective-permute-start.8) | collective-permute-done | bytes 2097184 | tf_op jit(solution)/shard_map/ppermute | solution.py:54
  227.2 2.4 fusion.3
  229.7 1.2 convolution_convert_fusion.5
  231.2 1.0 collective-permute-start.3
  232.2 43.7 %collective-permute-done.3 = bf16[8,32,4096]{2,1,0:T(8,128)(2,1)S(1)} collective-permute-done((bf16[8,32,4096]{2,1,0:T(8,128)(2,1)S(1)}, bf16[8,32,4096]{2,1,0:T(8,128)(2,1)S(1)}, u32[]{:S(2)}, u32[]{:S(2)}) %collective-permute-start.3) | collective-permute-done | bytes 2097184 | tf_op jit(solution)/shard_map/ppermute | solution.py:54
  275.9 2.6 fusion.4
  278.6 5.3 %collective-permute-start.7 = (s32[128]{0:T(128)S(1)}, s32[128]{0:T(128)S(1)}, u32[]{:S(2)}, u32[]{:S(2)}) collective-permute-start(s32[128]{0:T(128)S(1)} %add_select_fusion), channel_id=1, source_target_pairs={{16,0},{32,16},{48,32},{64,48},{80,64},{96,80},{112,96},{128,112},... | collective-permute-start | bytes 1544 | tf_op jit(solution)/shard_map/ppermute | solution.py:15
  283.9 3.0 collective-permute-start
  286.9 1.9 collective-permute-start.11
  288.8 6.0 %collective-permute-start.6 = (bf16[128,7168]{1,0:T(8,128)(2,1)}, bf16[128,7168]{1,0:T(8,128)(2,1)}, u32[]{:S(2)}, u32[]{:S(2)}) collective-permute-start(bf16[128,7168]{1,0:T(8,128)(2,1)} %bitcast.110), channel_id=1, source_target_pairs={{0,16},{16,32},{32,48},{48,64},{64,80},{80,96},{96,112},{112,128},... | collective-permute-start | bytes 5505032 | tf_op jit(solution)/shard_map/ppermute | solution.py:15
  295.1 1.7 broadcast_select_fusion
  296.8 1.8 collective-permute-start.9
  298.6 1.8 broadcast_select_fusion.1
  300.4 10.0 %reduce-scatter.9.cloned.1.call-done = bf16[32,4096]{1,0:T(8,128)(2,1)} async-done(((bf16[256,4096]{1,0:T(8,128)(2,1)}), bf16[32,4096]{1,0:T(8,128)(2,1)}) %reduce-scatter.9.cloned.1.call-update) | async-done | bytes 262160 | tf_op jit(solution)/shard_map/reduce_scatter | solution.py:56
  310.4 1.0 convert_element_type.125
  311.3 42.9 %reduce-scatter.5.cloned.1.call-done = bf16[32,4096]{1,0:T(8,128)(2,1)} async-done(((bf16[256,4096]{1,0:T(8,128)(2,1)}), bf16[32,4096]{1,0:T(8,128)(2,1)}) %reduce-scatter.5.cloned.1.call-update) | async-done | bytes 262160 | tf_op jit(solution)/shard_map/reduce_scatter | solution.py:56
  354.2 1.0 convert_element_type.110
  355.2 1.2 convert_add_fusion.2
  356.8 6.6 %collective-permute-start.10 = (bf16[32,7168]{1,0:T(8,128)(2,1)S(1)}, bf16[32,7168]{1,0:T(8,128)(2,1)S(1)}, u32[]{:S(2)}, u32[]{:S(2)}) collective-permute-start(bf16[32,7168]{1,0:T(8,128)(2,1)S(1)} %fusion.38), channel_id=1, source_target_pairs={{16,0},{32,16},{48,32},{64,48},{80,64},{96,80},{112,96},{128,112},... | collective-permute-start | bytes 1376264 | tf_op jit(solution)/shard_map/ppermute | solution.py:15
  363.7 3.1 collective-permute-start.5
  366.8 4.3 %collective-permute-done.10 = bf16[32,7168]{1,0:T(8,128)(2,1)S(1)} collective-permute-done((bf16[32,7168]{1,0:T(8,128)(2,1)S(1)}, bf16[32,7168]{1,0:T(8,128)(2,1)S(1)}, u32[]{:S(2)}, u32[]{:S(2)}) %collective-permute-start.10) | collective-permute-done | bytes 458784 | tf_op jit(solution)/shard_map/ppermute | solution.py:15
  371.1 3.4 select_bitcast_fusion.2
  374.5 3.4 select_bitcast_fusion.3
  (56 shorter events, 2.5 us)
Async XLA Ops:
  7.2 3.7 copy-start.3
  7.2 62.6 %all-gather.3.cloned.1.call-start = ((), (), s32[]{:S(2)}) async-start(), calls=%async_computation.4 | async-start | bytes 4718592 | tf_op jit(solution)/shard_map/all_gather | solution.py:35
  12.1 133.1 %all-gather.5.cloned.1.call-start = ((), (), s32[]{:S(2)}) async-start(), calls=%async_computation.5 | async-start | bytes 7077888 | tf_op jit(solution)/shard_map/all_gather | solution.py:46
  12.3 10.1 %collective-permute-start.2 = (bf16[32,6144]{1,0:T(8,128)(2,1)S(1)}, bf16[32,6144]{1,0:T(8,128)(2,1)S(1)}, u32[]{:S(2)}, u32[]{:S(2)}) collective-permute-start(bf16[32,6144]{1,0:T(8,128)(2,1)S(1)} %get-tuple-element.8), channel_id=1, source_target_pairs={{0,8},{8,0},{1,9},{9,1},{2,10},{10,2},{3,11},{11,3},{4,12},{12,4},... | collective-permute-start | bytes 1179656 | tf_op jit(solution)/shard_map/ppermute | solution.py:44
  23.4 271.7 %reduce-scatter.11.cloned.1.call-start = ((), (), s32[]{:S(2)}) async-start(), calls=%async_computation.9 | async-start | bytes 3538944 | tf_op jit(solution)/shard_map/reduce_scatter | solution.py:61
  69.8 91.6 %collective-permute-start.1 = (bf16[256,8192]{1,0:T(8,128)(2,1)}, bf16[256,8192]{1,0:T(8,128)(2,1)}, u32[]{:S(2)}, u32[]{:S(2)}) collective-permute-start(bf16[256,8192]{1,0:T(8,128)(2,1)} %all-gather.3.cloned.1.call-done), channel_id=1, source_target_pairs={{0,8},{8,0},{1,9},{9,1},{2,10},{10,2},{3,11},{11,3},{4,12},{12,4},... | collective-permute-start | bytes 12582920 | tf_op jit(solution)/shard_map/ppermute | solution.py:36
  145.2 4.0 %copy-start.8 = (bf16[512,6144]{1,0:T(8,128)(2,1)S(1)}, bf16[512,6144]{1,0:T(8,128)(2,1)}, u32[]{:S(2)}) copy-start(bf16[512,6144]{1,0:T(8,128)(2,1)} %all-gather.5.cloned.1.call-done) | copy-start | bytes 18874372
  149.1 2.3 copy-start.2
  151.4 10.0 %copy-start.1 = (bf16[256,8192]{1,0:T(8,128)(2,1)S(1)}, bf16[256,8192]{1,0:T(8,128)(2,1)}, u32[]{:S(2)}) copy-start(bf16[256,8192]{1,0:T(8,128)(2,1)} %all-gather.3.cloned.1.call-done) | copy-start | bytes 12582916
  161.4 5.4 %copy-start.5 = (bf16[1,7168,128]{2,1,0:T(8,128)(2,1)S(1)}, bf16[1,7168,128]{2,1,0:T(8,128)(2,1)}, u32[]{:S(2)}) copy-start(bf16[1,7168,128]{2,1,0:T(8,128)(2,1)} %param.14) | copy-start | bytes 5505028
  166.8 1.5 copy-start.4
  174.6 124.0 %reduce-scatter.7.cloned.1.call-start = ((), (), s32[]{:S(2)}) async-start(), calls=%async_computation.7 | async-start | bytes 3538944 | tf_op jit(solution)/shard_map/reduce_scatter | solution.py:61
  177.3 133.1 %reduce-scatter.9.cloned.1.call-start = ((), (), s32[]{:S(2)}) async-start(), calls=%async_computation.8 | async-start | bytes 2359296 | tf_op jit(solution)/shard_map/reduce_scatter | solution.py:56
  177.5 2.6 copy-start.6
  181.6 45.6 %collective-permute-start.8 = (bf16[8,32,4096]{2,1,0:T(8,128)(2,1)S(1)}, bf16[8,32,4096]{2,1,0:T(8,128)(2,1)S(1)}, u32[]{:S(2)}, u32[]{:S(2)}) collective-permute-start(bf16[8,32,4096]{2,1,0:T(8,128)(2,1)S(1)} %select_bitcast_fusion), channel_id=1, source_target_pairs={{0,8},{8,0},{1,9},{9,1},{2,10},{10,2},{3,11},{11,3},{4,12},{12,4},... | collective-permute-start | bytes 6291464 | tf_op jit(solution)/shard_map/ppermute | solution.py:54
  229.7 124.5 %reduce-scatter.5.cloned.1.call-start = ((), (), s32[]{:S(2)}) async-start(), calls=%async_computation.6 | async-start | bytes 2359296 | tf_op jit(solution)/shard_map/reduce_scatter | solution.py:56
  231.2 55.7 %copy-start = (bf16[1,128,7168]{2,1,0:T(8,128)(2,1)S(1)}, bf16[1,128,7168]{2,1,0:T(8,128)(2,1)}, u32[]{:S(2)}) copy-start(bf16[1,128,7168]{2,1,0:T(8,128)(2,1)} %param.9) | copy-start | bytes 5505028
  231.2 44.7 %collective-permute-start.3 = (bf16[8,32,4096]{2,1,0:T(8,128)(2,1)S(1)}, bf16[8,32,4096]{2,1,0:T(8,128)(2,1)S(1)}, u32[]{:S(2)}, u32[]{:S(2)}) collective-permute-start(bf16[8,32,4096]{2,1,0:T(8,128)(2,1)S(1)} %select_bitcast_fusion.1), channel_id=1, source_target_pairs={{0,8},{8,0},{1,9},{9,1},{2,10},{10,2},{3,11},{11,3},{4,12},{12,4},... | collective-permute-start | bytes 6291464 | tf_op jit(solution)/shard_map/ppermute | solution.py:54
  278.6 16.4 %collective-permute-start.7 = (s32[128]{0:T(128)S(1)}, s32[128]{0:T(128)S(1)}, u32[]{:S(2)}, u32[]{:S(2)}) collective-permute-start(s32[128]{0:T(128)S(1)} %add_select_fusion), channel_id=1, source_target_pairs={{16,0},{32,16},{48,32},{64,48},{80,64},{96,80},{112,96},{128,112},... | collective-permute-start | bytes 1544 | tf_op jit(solution)/shard_map/ppermute | solution.py:15
  283.9 82.8 %collective-permute-start = (s32[128]{0:T(128)S(1)}, s32[128]{0:T(128)S(1)}, u32[]{:S(2)}, u32[]{:S(2)}) collective-permute-start(s32[128]{0:T(128)S(1)} %add_select_fusion), channel_id=1, source_target_pairs={{0,16},{16,32},{32,48},{48,64},{64,80},{80,96},{96,112},{112,128},... | collective-permute-start | bytes 1544 | tf_op jit(solution)/shard_map/ppermute | solution.py:15
  286.9 79.9 %collective-permute-start.11 = (bf16[128,7168]{1,0:T(8,128)(2,1)S(1)}, bf16[128,7168]{1,0:T(8,128)(2,1)}, u32[]{:S(2)}, u32[]{:S(2)}) collective-permute-start(bf16[128,7168]{1,0:T(8,128)(2,1)S(1)} %bitcast.103), channel_id=1, source_target_pairs={{16,0},{32,16},{48,32},{64,48},{80,64},{96,80},{112,96},{128,112},... | collective-permute-start | bytes 5505032 | tf_op jit(solution)/shard_map/ppermute | solution.py:15
  288.8 85.7 %collective-permute-start.6 = (bf16[128,7168]{1,0:T(8,128)(2,1)}, bf16[128,7168]{1,0:T(8,128)(2,1)}, u32[]{:S(2)}, u32[]{:S(2)}) collective-permute-start(bf16[128,7168]{1,0:T(8,128)(2,1)} %bitcast.110), channel_id=1, source_target_pairs={{0,16},{16,32},{32,48},{48,64},{64,80},{80,96},{96,112},{112,128},... | collective-permute-start | bytes 5505032 | tf_op jit(solution)/shard_map/ppermute | solution.py:15
  296.8 58.4 %collective-permute-start.9 = (bf16[32,3072]{1,0:T(8,128)(2,1)}, bf16[32,3072]{1,0:T(8,128)(2,1)}, u32[]{:S(2)}, u32[]{:S(2)}) collective-permute-start(bf16[32,3072]{1,0:T(8,128)(2,1)} %broadcast_select_fusion), channel_id=1, source_target_pairs={{0,8},{8,0},{1,9},{9,1},{2,10},{10,2},{3,11},{11,3},{4,12},{12,4},... | collective-permute-start | bytes 589832 | tf_op jit(solution)/shard_map/ppermute | solution.py:65
  298.6 64.8 %copy-start.7 = (bf16[64,3072]{1,0:T(8,128)(2,1)S(1)}, bf16[64,3072]{1,0:T(8,128)(2,1)}, u32[]{:S(2)}) copy-start(bf16[64,3072]{1,0:T(8,128)(2,1)} %reduce-scatter.7.cloned.1.call-done) | copy-start | bytes 1179652
  300.4 63.0 %collective-permute-start.4 = (bf16[32,3072]{1,0:T(8,128)(2,1)}, bf16[32,3072]{1,0:T(8,128)(2,1)S(1)}, u32[]{:S(2)}, u32[]{:S(2)}) collective-permute-start(bf16[32,3072]{1,0:T(8,128)(2,1)} %broadcast_select_fusion.1), channel_id=1, source_target_pairs={{0,8},{8,0},{1,9},{9,1},{2,10},{10,2},{3,11},{11,3},{4,12},{12,4},... | collective-permute-start | bytes 589832 | tf_op jit(solution)/shard_map/ppermute | solution.py:65
  356.8 14.3 %collective-permute-start.10 = (bf16[32,7168]{1,0:T(8,128)(2,1)S(1)}, bf16[32,7168]{1,0:T(8,128)(2,1)S(1)}, u32[]{:S(2)}, u32[]{:S(2)}) collective-permute-start(bf16[32,7168]{1,0:T(8,128)(2,1)S(1)} %fusion.38), channel_id=1, source_target_pairs={{16,0},{32,16},{48,32},{64,48},{80,64},{96,80},{112,96},{128,112},... | collective-permute-start | bytes 1376264 | tf_op jit(solution)/shard_map/ppermute | solution.py:15
  363.7 10.9 %collective-permute-start.5 = (bf16[32,7168]{1,0:T(8,128)(2,1)S(1)}, bf16[32,7168]{1,0:T(8,128)(2,1)S(1)}, u32[]{:S(2)}, u32[]{:S(2)}) collective-permute-start(bf16[32,7168]{1,0:T(8,128)(2,1)S(1)} %fusion.37), channel_id=1, source_target_pairs={{0,16},{16,32},{32,48},{48,64},{64,80},{80,96},{96,112},{112,128},... | collective-permute-start | bytes 1376264 | tf_op jit(solution)/shard_map/ppermute | solution.py:15
Sparse Core Ops, SparseCore 0:
  12.2 57.4 all-gather.2
  72.1 73.0 all-gather.4
  174.7 43.5 reduce-scatter.10
  220.7 46.3 reduce-scatter.6
  269.6 40.7 reduce-scatter.8
  312.8 41.3 reduce-scatter.4

commit v6 on v5

--- a/solution.py
+++ b/solution.py
@@ -46,15 +46,21 @@
     return lax.all_gather(pair, "z", axis=0, tiled=True)
 
 
-def scatter_wide(q, first, rows):
-    zs = q.shape[0] // (2 * rows)
-    q = q.reshape(zs, 2, rows, -1)
-    keep = jnp.where(first, q[:, 0], q[:, 1])
-    give = jnp.where(first, q[:, 1], q[:, 0])
-    got = lax.ppermute(give, "xlo", SWAP)
-    total = (keep.astype(jnp.float32) + got.astype(jnp.float32)).astype(jnp.bfloat16)
-    part = lax.psum_scatter(total.reshape(zs * rows, -1), "z", scatter_dimension=0, tiled=True)
-    return part.astype(jnp.float32)
+def scatter_wide(qs, first, rows):
+    totals = []
+    for q in qs:
+        zs = q.shape[0] // (2 * rows)
+        q = q.reshape(zs, 2, rows, -1)
+        keep = jnp.where(first, q[:, 0], q[:, 1])
+        give = jnp.where(first, q[:, 1], q[:, 0])
+        got = lax.ppermute(give, "xlo", SWAP)
+        total = (keep.astype(jnp.float32) + got.astype(jnp.float32)).astype(jnp.bfloat16)
+        totals.append(total.reshape(zs * rows, -1))
+    part = lax.psum_scatter(
+        jnp.concatenate(totals, axis=1), "z", scatter_dimension=0, tiled=True
+    ).astype(jnp.float32)
+    cut = totals[0].shape[1]
+    return part[:, :cut], part[:, cut:]
 
 
 def scatter_narrow(q, first, rows):
@@ -78,7 +84,8 @@
     up_mat = up_weight[0]
     down_mat = down_weight[0]
     width = local.shape[1]
-    wide = (width // 7 * 4) // 128 * 128
+    wide = (width // 2) // 128 * 128
+    wide_r = (width // 7 * 4) // 128 * 128
     hit = named == section
     chosen = jnp.any(hit, axis=1)
     slot = jnp.sum(jnp.where(hit, slot_index[0], 0), axis=1)
@@ -114,8 +121,8 @@
     )
     act, slope = silu_parts(gate)
     hidden = (act * up).astype(jnp.bfloat16)
-    ahead_a = jnp.dot(hidden, down_mat[:, :wide], preferred_element_type=f32).astype(jnp.bfloat16)
-    ahead_b = jnp.dot(hidden, down_mat[:, wide:], preferred_element_type=f32).astype(jnp.bfloat16)
+    ahead_a = jnp.dot(hidden, down_mat[:, :wide_r], preferred_element_type=f32).astype(jnp.bfloat16)
+    ahead_b = jnp.dot(hidden, down_mat[:, wide_r:], preferred_element_type=f32).astype(jnp.bfloat16)
     comb_b = scatter_narrow(ahead_b, first, CAP)
     grad_hidden = jnp.dot(back_a, down_mat[:, :wide].T, preferred_element_type=f32) + jnp.dot(
         back_b, down_mat[:, wide:].T, preferred_element_type=f32
@@ -123,16 +130,15 @@
     grad_up = (grad_hidden * act).astype(jnp.bfloat16)
     grad_gate = (grad_hidden * up * slope).astype(jnp.bfloat16)
     behind_b = (
-        jnp.dot(grad_gate, gate_mat[wide:].T, preferred_element_type=f32)
-        + jnp.dot(grad_up, up_mat[wide:].T, preferred_element_type=f32)
+        jnp.dot(grad_gate, gate_mat[wide_r:].T, preferred_element_type=f32)
+        + jnp.dot(grad_up, up_mat[wide_r:].T, preferred_element_type=f32)
     ).astype(jnp.bfloat16)
     behind_a = (
-        jnp.dot(grad_gate, gate_mat[:wide].T, preferred_element_type=f32)
-        + jnp.dot(grad_up, up_mat[:wide].T, preferred_element_type=f32)
+        jnp.dot(grad_gate, gate_mat[:wide_r].T, preferred_element_type=f32)
+        + jnp.dot(grad_up, up_mat[:wide_r].T, preferred_element_type=f32)
     ).astype(jnp.bfloat16)
-    comb_a = scatter_wide(ahead_a, first, CAP)
     inw_b = scatter_narrow(behind_b, first, CAP)
-    inw_a = scatter_wide(behind_a, first, CAP)
+    comb_a, inw_a = scatter_wide([ahead_a, behind_a], first, CAP)
     combined = jnp.concatenate([comb_a, comb_b], axis=1)
     inward = jnp.concatenate([inw_a, inw_b], axis=1)
 

time: 389 us -> 365 us (0.938)
  waiting for transfers between devices: 285 us -> 261 us
    all_gather x1, waiting for transfers between devices: 74.5 us -> 0.01 us  [gather_narrow(): return lax.all_gather(pair, 'z', axis=0, tiled=True)]
    ppermute x1, waiting for transfers between devices: 8.96 us -> 79.5 us  [gather_wide(): other = lax.ppermute(own, 'xlo', SWAP)]
    reduce_scatter x2 -> x1, waiting for transfers between devices: 52.8 us -> 0.02 us  [scatter_wide(): lax.psum_scatter(jnp.concatenate(totals, axis=1), 'z', scatter_dimension=...]
    ppermute x2, waiting for transfers between devices: 0.01 us -> 40.2 us  [scatter_narrow(): got = lax.ppermute(give, 'xlo', SWAP)]
    all_gather x1, waiting for transfers between devices: 46.3 us -> 40 us  [gather_wide(): own = lax.all_gather(x, 'z', axis=0, tiled=True)]
  transfers between devices with their start and end apart: 18 -> 17, of which waited for: 9 -> 8; matrix products, arithmetic and copies ran while one was open for 8% -> 9% of each run, Pallas kernels for 0% -> 0%
where the time goes in v6:
time: 365 us; the launch traced here: 364 us
  waiting for transfers between devices  261 us (72%)
  matrix products  35 us (10%)
  starting transfers between devices  29.6 us (8%)
  other arithmetic  22.6 us (6%)
  between operations  14.2 us (4%)
    ppermute x2, waiting for transfers between devices, scatter_wide(): got = lax.ppermute(give, 'xlo', SWAP)  85.1 us
    ppermute x1, waiting for transfers between devices, gather_wide(): other = lax.ppermute(own, 'xlo', SWAP)  79.5 us
    ppermute x2, waiting for transfers between devices, scatter_narrow(): got = lax.ppermute(give, 'xlo', SWAP)  40.2 us
    all_gather x1, waiting for transfers between devices, gather_wide(): own = lax.all_gather(x, 'z', axis=0, tiled=True)  40 us
    ppermute x6, starting transfers between devices, from_behind(): return lax.ppermute(x, axis, pairs)  24 us
    ppermute x1, waiting for transfers between devices, gather_narrow(): other = lax.ppermute(x, 'xlo', SWAP)  10.5 us
    select_n x2, other arithmetic, in_order(): jnp.where(first, jnp.stack([mine, other], axis), jnp.stack([other, mine],...  8.29 us
  transfers between devices with their start and end apart: 17, of which 8 were waited for; matrix products, arithmetic and copies ran while one was open for 9% of the time, Pallas kernels for 0%

profile of v6, /device:TPU:5, one launch (start us, length us, event | category | flops | bytes accessed | tf_op | source)
XLA Modules:
  0.0 364.1 jit_solution(11465493748711507275)
XLA Ops:
  7.2 0.8 select_reduce_fusion.1
  8.1 0.7 select_reduce_fusion.2
  8.8 2.0 convolution_convert_fusion.3
  11.3 0.8 pad_maximum_fusion.1
  12.2 1.0 collective-permute-start.2
  13.2 10.5 %collective-permute-done.2 = bf16[32,7168]{1,0:T(8,128)(2,1)S(1)} collective-permute-done((bf16[32,7168]{1,0:T(8,128)(2,1)S(1)}, bf16[32,7168]{1,0:T(8,128)(2,1)S(1)}, u32[]{:S(2)}, u32[]{:S(2)}) %collective-permute-start.2) | collective-permute-done | bytes 458784 | tf_op jit(solution)/shard_map/ppermute | solution.py:44
  23.7 1.1 maximum_select_fusion.1
  24.8 40.0 %all-gather.3.cloned.1.call-done = bf16[256,7168]{1,0:T(8,128)(2,1)} async-done(((bf16[32,7168]{1,0:T(8,128)(2,1)}), bf16[256,7168]{1,0:T(8,128)(2,1)}) %all-gather.3.cloned.1.call-update) | async-done | bytes 3670032 | tf_op jit(solution)/shard_map/all_gather | solution.py:35
  64.8 0.9 collective-permute-start.1
  65.7 79.5 %collective-permute-done.1 = bf16[256,7168]{1,0:T(8,128)(2,1)S(1)} collective-permute-done((bf16[256,7168]{1,0:T(8,128)(2,1)}, bf16[256,7168]{1,0:T(8,128)(2,1)S(1)}, u32[]{:S(2)}, u32[]{:S(2)}) %collective-permute-start.1) | collective-permute-done | bytes 3670048 | tf_op jit(solution)/shard_map/ppermute | solution.py:36
  145.2 7.2 %maximum_select_fusion = bf16[8,2,32,7168]{3,2,1,0:T(8,128)(2,1)} fusion(bf16[8,1,32,7168]{3,2,1,0:T(8,128)(2,1)S(1)} %bitcast.112, bf16[8,1,32,7168]{3,2,1,0:T(8,128)(2,1)} %bitcast.111, pred[]{:T(512)S(6)} %eq.57), kind=kLoop, calls=%fused_computation.7 | loop fusion | flops 11010048 | bytes 14680065 | tf_op jit(solution)/shard_map/jit(_where)/select_n | solution.py:31
  152.5 3.3 fusion.7
  155.8 4.4 %fusion.19 = f32[512,128]{1,0:T(8,128)S(1)} fusion(f32[512,128]{1,0:T(8,128)S(1)} %fusion.7, bf16[512,7168]{1,0:T(8,128)(2,1)} %bitcast.104, bf16[1,7168,128]{2,1,0:T(8,128)(2,1)S(1)} %copy-done.6), kind=kOutput, calls=%fused_computation.39 | convolution fusion | flops 469827584 | bytes 5111808 | tf_op jit(solution)/shard_map/dot_general | solution.py:119
  160.3 1.1 fusion.9
  161.4 1.1 fusion.16
  162.9 1.1 fusion.3
  164.0 1.2 multiply_convert_fusion.2
  165.2 1.0 fusion.46
  166.2 3.8 %add_convert_fusion.1 = bf16[512,3072]{1,0:T(8,128)(2,1)} fusion(f32[512,3072]{1,0:T(8,128)S(1)} %fusion.46, bf16[512,128]{1,0:T(8,128)(2,1)S(1)} %get-tuple-element.6, bf16[1,7168,128]{2,1,0:T(8,128)(2,1)} %param.14), kind=kOutput, calls=%fused_computation.8 | convolution fusion | flops 405798912 | bytes 10354688 | tf_op jit(solution)/shard_map/dot_general | solution.py:134
  170.2 2.7 convolution_convert_fusion.6
  173.0 3.2 convolution_convert_fusion.5
  176.2 2.6 select_bitcast_fusion.1
  178.8 1.0 collective-permute-start.3
  179.8 1.2 fusion.27
  181.1 1.3 add_convert_fusion
  182.6 0.7 collective-permute-start.4
  183.2 41.3 %collective-permute-done.3 = bf16[8,32,4096]{2,1,0:T(8,128)(2,1)S(1)} collective-permute-done((bf16[8,32,4096]{2,1,0:T(8,128)(2,1)S(1)}, bf16[8,32,4096]{2,1,0:T(8,128)(2,1)S(1)}, u32[]{:S(2)}, u32[]{:S(2)}) %collective-permute-start.3) | collective-permute-done | bytes 2097184 | tf_op jit(solution)/shard_map/ppermute | solution.py:56
  224.5 1.1 fusion.2
  225.6 43.9 %collective-permute-done.4 = bf16[8,32,4096]{2,1,0:T(8,128)(2,1)S(1)} collective-permute-done((bf16[8,32,4096]{2,1,0:T(8,128)(2,1)S(1)}, bf16[8,32,4096]{2,1,0:T(8,128)(2,1)S(1)}, u32[]{:S(2)}, u32[]{:S(2)}) %collective-permute-start.4) | collective-permute-done | bytes 2097184 | tf_op jit(solution)/shard_map/ppermute | solution.py:56
  269.5 1.0 fusion.1
  270.5 2.4 pad_maximum_fusion
  272.9 4.5 %collective-permute-start.8 = (s32[128]{0:T(128)S(1)}, s32[128]{0:T(128)S(1)}, u32[]{:S(2)}, u32[]{:S(2)}) collective-permute-start(s32[128]{0:T(128)S(1)} %add_select_fusion), channel_id=1, source_target_pairs={{16,0},{32,16},{48,32},{64,48},{80,64},{96,80},{112,96},{128,112},... | collective-permute-start | bytes 1544 | tf_op jit(solution)/shard_map/ppermute | solution.py:15
  277.4 3.6 collective-permute-start
  281.0 1.9 collective-permute-start.11
  283.0 6.0 %collective-permute-start.7 = (bf16[128,7168]{1,0:T(8,128)(2,1)}, bf16[128,7168]{1,0:T(8,128)(2,1)}, u32[]{:S(2)}, u32[]{:S(2)}) collective-permute-start(bf16[128,7168]{1,0:T(8,128)(2,1)} %bitcast.117), channel_id=1, source_target_pairs={{0,16},{16,32},{32,48},{48,64},{64,80},{80,96},{96,112},{112,128},... | collective-permute-start | bytes 5505032 | tf_op jit(solution)/shard_map/ppermute | solution.py:15
  289.2 1.0 broadcast_select_fusion
  290.2 1.3 collective-permute-start.9
  291.5 1.1 broadcast_select_fusion.1
  292.9 39.2 %collective-permute-done.9 = bf16[32,3072]{1,0:T(8,128)(2,1)S(1)} collective-permute-done((bf16[32,3072]{1,0:T(8,128)(2,1)S(1)}, bf16[32,3072]{1,0:T(8,128)(2,1)S(1)}, u32[]{:S(2)}, u32[]{:S(2)}) %collective-permute-start.9) | collective-permute-done | bytes 196640 | tf_op jit(solution)/shard_map/ppermute | solution.py:71
  332.2 1.1 convert_add_fusion.2
  333.3 1.0 collective-permute-done.5
  334.3 1.1 convert_add_fusion.3
  335.4 1.1 fusion.77
  336.9 1.9 collective-permute-start.10
  339.0 6.0 %collective-permute-start.6 = (bf16[32,7168]{1,0:T(8,128)(2,1)S(1)}, bf16[32,7168]{1,0:T(8,128)(2,1)S(1)}, u32[]{:S(2)}, u32[]{:S(2)}) collective-permute-start(bf16[32,7168]{1,0:T(8,128)(2,1)S(1)} %fusion.34), channel_id=1, source_target_pairs={{0,16},{16,32},{32,48},{48,64},{64,80},{80,96},{96,112},{112,128},... | collective-permute-start | bytes 1376264 | tf_op jit(solution)/shard_map/ppermute | solution.py:15
  345.1 5.6 %collective-permute-done.10 = bf16[32,7168]{1,0:T(8,128)(2,1)S(1)} collective-permute-done((bf16[32,7168]{1,0:T(8,128)(2,1)S(1)}, bf16[32,7168]{1,0:T(8,128)(2,1)S(1)}, u32[]{:S(2)}, u32[]{:S(2)}) %collective-permute-start.10) | collective-permute-done | bytes 458784 | tf_op jit(solution)/shard_map/ppermute | solution.py:15
  350.7 3.4 select_bitcast_fusion.2
  354.1 3.4 select_bitcast_fusion.3
  (56 shorter events, 2.7 us)
Async XLA Ops:
  7.2 3.7 %copy-start.3 = (bf16[1,128,7168]{2,1,0:T(8,128)(2,1)S(1)}, bf16[1,128,7168]{2,1,0:T(8,128)(2,1)}, u32[]{:S(2)}) copy-start(bf16[1,128,7168]{2,1,0:T(8,128)(2,1)} %param.8) | copy-start | bytes 5505028
  7.2 57.7 %all-gather.3.cloned.1.call-start = ((), (), s32[]{:S(2)}) async-start(), calls=%async_computation.3 | async-start | bytes 4128768 | tf_op jit(solution)/shard_map/all_gather | solution.py:35
  12.1 140.3 %all-gather.5.cloned.1.call-start = ((), (), s32[]{:S(2)}) async-start(), calls=%async_computation.4 | async-start | bytes 8257536 | tf_op jit(solution)/shard_map/all_gather | solution.py:46
  12.2 11.5 %collective-permute-start.2 = (bf16[32,7168]{1,0:T(8,128)(2,1)S(1)}, bf16[32,7168]{1,0:T(8,128)(2,1)S(1)}, u32[]{:S(2)}, u32[]{:S(2)}) collective-permute-start(bf16[32,7168]{1,0:T(8,128)(2,1)S(1)} %get-tuple-element.14), channel_id=1, source_target_pairs={{0,8},{8,0},{1,9},{9,1},{2,10},{10,2},{3,11},{11,3},{4,12},{12,4},... | collective-permute-start | bytes 1376264 | tf_op jit(solution)/shard_map/ppermute | solution.py:44
  24.8 264.4 %reduce-scatter.8.cloned.1.call-start = ((), (), s32[]{:S(2)}) async-start(), calls=%async_computation.7 | async-start | bytes 3538944 | tf_op jit(solution)/shard_map/reduce_scatter | solution.py:67
  64.8 80.4 %collective-permute-start.1 = (bf16[256,7168]{1,0:T(8,128)(2,1)}, bf16[256,7168]{1,0:T(8,128)(2,1)S(1)}, u32[]{:S(2)}, u32[]{:S(2)}) collective-permute-start(bf16[256,7168]{1,0:T(8,128)(2,1)} %all-gather.3.cloned.1.call-done), channel_id=1, source_target_pairs={{0,8},{8,0},{1,9},{9,1},{2,10},{10,2},{3,11},{11,3},{4,12},{12,4},... | collective-permute-start | bytes 11010056 | tf_op jit(solution)/shard_map/ppermute | solution.py:36
  145.2 7.2 %copy-start.6 = (bf16[1,7168,128]{2,1,0:T(8,128)(2,1)S(1)}, bf16[1,7168,128]{2,1,0:T(8,128)(2,1)}, u32[]{:S(2)}) copy-start(bf16[1,7168,128]{2,1,0:T(8,128)(2,1)} %param.14) | copy-start | bytes 5505028
  152.4 7.8 %copy-start.8 = (bf16[512,7168]{1,0:T(8,128)(2,1)S(1)}, bf16[512,7168]{1,0:T(8,128)(2,1)}, u32[]{:S(2)}) copy-start(bf16[512,7168]{1,0:T(8,128)(2,1)} %all-gather.5.cloned.1.call-done) | copy-start | bytes 22020100
  152.5 8.9 %slice-start = ((s8[7340032]{0:T(1024)(128)(4,1)}), s8[4194304]{0:T(1024)(128)(4,1)S(1)}, s32[]{:S(2)}) async-start(s8[7340032]{0:T(1024)(128)(4,1)} %bitcast.105), calls=%async_computation.8 | async-start | bytes 8388608
  155.8 4.5 %copy-start.4 = (bf16[1,7168,128]{2,1,0:T(8,128)(2,1)S(1)}, bf16[1,7168,128]{2,1,0:T(8,128)(2,1)}, u32[]{:S(2)}) copy-start(bf16[1,7168,128]{2,1,0:T(8,128)(2,1)} %param.13) | copy-start | bytes 5505028
  155.8 5.6 %slice-start.1 = ((s8[7340032]{0:T(1024)(128)(4,1)}), s8[3145728]{0:T(1024)(128)(4,1)S(1)}, s32[]{:S(2)}) async-start(s8[7340032]{0:T(1024)(128)(4,1)} %bitcast.105), calls=%async_computation.9 | async-start | bytes 6291456
  161.4 1.5 copy-start.2
  170.0 121.5 %reduce-scatter.6.cloned.1.call-start = ((), (), s32[]{:S(2)}) async-start(), calls=%async_computation.6 | async-start | bytes 3538944 | tf_op jit(solution)/shard_map/reduce_scatter | solution.py:67
  176.2 159.2 %reduce-scatter.4.cloned.1.call-start = ((), (), s32[]{:S(2)}) async-start(), calls=%async_computation.5 | async-start | bytes 4718592 | tf_op jit(solution)/shard_map/reduce_scatter | solution.py:59
  176.2 3.6 copy-start.5
  178.8 2.3 copy-start.7
  178.8 45.7 %collective-permute-start.3 = (bf16[8,32,4096]{2,1,0:T(8,128)(2,1)S(1)}, bf16[8,32,4096]{2,1,0:T(8,128)(2,1)S(1)}, u32[]{:S(2)}, u32[]{:S(2)}) collective-permute-start(bf16[8,32,4096]{2,1,0:T(8,128)(2,1)S(1)} %select_bitcast_fusion.1), channel_id=1, source_target_pairs={{0,8},{8,0},{1,9},{9,1},{2,10},{10,2},{3,11},{11,3},{4,12},{12,4},... | collective-permute-start | bytes 6291464 | tf_op jit(solution)/shard_map/ppermute | solution.py:56
  182.3 42.2 %copy-start = (bf16[512,4096]{1,0:T(8,128)(2,1)S(1)}, bf16[512,4096]{1,0:T(8,128)(2,1)}, u32[]{:S(2)}) copy-start(bf16[512,4096]{1,0:T(8,128)(2,1)} %convolution_convert_fusion.5) | copy-start | bytes 12582916
  182.6 86.9 %collective-permute-start.4 = (bf16[8,32,4096]{2,1,0:T(8,128)(2,1)S(1)}, bf16[8,32,4096]{2,1,0:T(8,128)(2,1)S(1)}, u32[]{:S(2)}, u32[]{:S(2)}) collective-permute-start(bf16[8,32,4096]{2,1,0:T(8,128)(2,1)S(1)} %select_bitcast_fusion), channel_id=1, source_target_pairs={{0,8},{8,0},{1,9},{9,1},{2,10},{10,2},{3,11},{11,3},{4,12},{12,4},... | collective-permute-start | bytes 6291464 | tf_op jit(solution)/shard_map/ppermute | solution.py:56
  272.9 8.2 %copy-start.1 = (bf16[1,128,7168]{2,1,0:T(8,128)(2,1)S(1)}, bf16[1,128,7168]{2,1,0:T(8,128)(2,1)}, u32[]{:S(2)}) copy-start(bf16[1,128,7168]{2,1,0:T(8,128)(2,1)} %param.9) | copy-start | bytes 5505028
  272.9 16.2 %collective-permute-start.8 = (s32[128]{0:T(128)S(1)}, s32[128]{0:T(128)S(1)}, u32[]{:S(2)}, u32[]{:S(2)}) collective-permute-start(s32[128]{0:T(128)S(1)} %add_select_fusion), channel_id=1, source_target_pairs={{16,0},{32,16},{48,32},{64,48},{80,64},{96,80},{112,96},{128,112},... | collective-permute-start | bytes 1544 | tf_op jit(solution)/shard_map/ppermute | solution.py:15
  277.4 67.6 %collective-permute-start = (s32[128]{0:T(128)S(1)}, s32[128]{0:T(128)S(1)}, u32[]{:S(2)}, u32[]{:S(2)}) collective-permute-start(s32[128]{0:T(128)S(1)} %add_select_fusion), channel_id=1, source_target_pairs={{0,16},{16,32},{32,48},{48,64},{64,80},{80,96},{96,112},{112,128},... | collective-permute-start | bytes 1544 | tf_op jit(solution)/shard_map/ppermute | solution.py:15
  281.0 64.0 %collective-permute-start.11 = (bf16[128,7168]{1,0:T(8,128)(2,1)S(1)}, bf16[128,7168]{1,0:T(8,128)(2,1)}, u32[]{:S(2)}, u32[]{:S(2)}) collective-permute-start(bf16[128,7168]{1,0:T(8,128)(2,1)S(1)} %bitcast.109), channel_id=1, source_target_pairs={{16,0},{32,16},{48,32},{64,48},{80,64},{96,80},{112,96},{128,112},... | collective-permute-start | bytes 5505032 | tf_op jit(solution)/shard_map/ppermute | solution.py:15
  283.0 71.1 %collective-permute-start.7 = (bf16[128,7168]{1,0:T(8,128)(2,1)}, bf16[128,7168]{1,0:T(8,128)(2,1)}, u32[]{:S(2)}, u32[]{:S(2)}) collective-permute-start(bf16[128,7168]{1,0:T(8,128)(2,1)} %bitcast.117), channel_id=1, source_target_pairs={{0,16},{16,32},{32,48},{48,64},{64,80},{80,96},{96,112},{112,128},... | collective-permute-start | bytes 5505032 | tf_op jit(solution)/shard_map/ppermute | solution.py:15
  290.2 41.9 %collective-permute-start.9 = (bf16[32,3072]{1,0:T(8,128)(2,1)S(1)}, bf16[32,3072]{1,0:T(8,128)(2,1)S(1)}, u32[]{:S(2)}, u32[]{:S(2)}) collective-permute-start(bf16[32,3072]{1,0:T(8,128)(2,1)S(1)} %broadcast_select_fusion), channel_id=1, source_target_pairs={{0,8},{8,0},{1,9},{9,1},{2,10},{10,2},{3,11},{11,3},{4,12},{12,4},... | collective-permute-start | bytes 589832 | tf_op jit(solution)/shard_map/ppermute | solution.py:71
  292.6 41.7 %collective-permute-start.5 = (bf16[32,3072]{1,0:T(8,128)(2,1)S(1)}, bf16[32,3072]{1,0:T(8,128)(2,1)S(1)}, u32[]{:S(2)}, u32[]{:S(2)}) collective-permute-start(bf16[32,3072]{1,0:T(8,128)(2,1)S(1)} %broadcast_select_fusion.1), channel_id=1, source_target_pairs={{0,8},{8,0},{1,9},{9,1},{2,10},{10,2},{3,11},{11,3},{4,12},{12,4},... | collective-permute-start | bytes 589832 | tf_op jit(solution)/shard_map/ppermute | solution.py:71
  336.9 13.8 %collective-permute-start.10 = (bf16[32,7168]{1,0:T(8,128)(2,1)S(1)}, bf16[32,7168]{1,0:T(8,128)(2,1)S(1)}, u32[]{:S(2)}, u32[]{:S(2)}) collective-permute-start(bf16[32,7168]{1,0:T(8,128)(2,1)S(1)} %fusion.35), channel_id=1, source_target_pairs={{16,0},{32,16},{48,32},{64,48},{80,64},{96,80},{112,96},{128,112},... | collective-permute-start | bytes 1376264 | tf_op jit(solution)/shard_map/ppermute | solution.py:15
  339.0 15.1 %collective-permute-start.6 = (bf16[32,7168]{1,0:T(8,128)(2,1)S(1)}, bf16[32,7168]{1,0:T(8,128)(2,1)S(1)}, u32[]{:S(2)}, u32[]{:S(2)}) collective-permute-start(bf16[32,7168]{1,0:T(8,128)(2,1)S(1)} %fusion.34), channel_id=1, source_target_pairs={{0,16},{16,32},{32,48},{48,64},{64,80},{80,96},{96,112},{112,128},... | collective-permute-start | bytes 1376264 | tf_op jit(solution)/shard_map/ppermute | solution.py:15
Sparse Core Ops, SparseCore 0:
  12.2 52.5 all-gather.2
  67.2 82.8 all-gather.4
  170.1 43.5 reduce-scatter.7
  216.1 46.3 reduce-scatter.5
  273.0 55.6 reduce-scatter.3

commit v7 on v5

--- a/solution.py
+++ b/solution.py
@@ -78,7 +78,8 @@
     up_mat = up_weight[0]
     down_mat = down_weight[0]
     width = local.shape[1]
-    wide = (width // 7 * 4) // 128 * 128
+    wide = (width // 2) // 128 * 128
+    wide_r = (width // 7 * 4) // 128 * 128
     hit = named == section
     chosen = jnp.any(hit, axis=1)
     slot = jnp.sum(jnp.where(hit, slot_index[0], 0), axis=1)
@@ -114,8 +115,8 @@
     )
     act, slope = silu_parts(gate)
     hidden = (act * up).astype(jnp.bfloat16)
-    ahead_a = jnp.dot(hidden, down_mat[:, :wide], preferred_element_type=f32).astype(jnp.bfloat16)
-    ahead_b = jnp.dot(hidden, down_mat[:, wide:], preferred_element_type=f32).astype(jnp.bfloat16)
+    ahead_a = jnp.dot(hidden, down_mat[:, :wide_r], preferred_element_type=f32).astype(jnp.bfloat16)
+    ahead_b = jnp.dot(hidden, down_mat[:, wide_r:], preferred_element_type=f32).astype(jnp.bfloat16)
     comb_b = scatter_narrow(ahead_b, first, CAP)
     grad_hidden = jnp.dot(back_a, down_mat[:, :wide].T, preferred_element_type=f32) + jnp.dot(
         back_b, down_mat[:, wide:].T, preferred_element_type=f32
@@ -123,12 +124,12 @@
     grad_up = (grad_hidden * act).astype(jnp.bfloat16)
     grad_gate = (grad_hidden * up * slope).astype(jnp.bfloat16)
     behind_b = (
-        jnp.dot(grad_gate, gate_mat[wide:].T, preferred_element_type=f32)
-        + jnp.dot(grad_up, up_mat[wide:].T, preferred_element_type=f32)
+        jnp.dot(grad_gate, gate_mat[wide_r:].T, preferred_element_type=f32)
+        + jnp.dot(grad_up, up_mat[wide_r:].T, preferred_element_type=f32)
     ).astype(jnp.bfloat16)
     behind_a = (
-        jnp.dot(grad_gate, gate_mat[:wide].T, preferred_element_type=f32)
-        + jnp.dot(grad_up, up_mat[:wide].T, preferred_element_type=f32)
+        jnp.dot(grad_gate, gate_mat[:wide_r].T, preferred_element_type=f32)
+        + jnp.dot(grad_up, up_mat[:wide_r].T, preferred_element_type=f32)
     ).astype(jnp.bfloat16)
     comb_a = scatter_wide(ahead_a, first, CAP)
     inw_b = scatter_narrow(behind_b, first, CAP)

time: 389 us -> 385 us (0.990)
  waiting for transfers between devices: 285 us -> 276 us
    all_gather x1, waiting for transfers between devices: 74.5 us -> 0.01 us  [gather_narrow(): return lax.all_gather(pair, 'z', axis=0, tiled=True)]
    ppermute x1, waiting for transfers between devices: 8.96 us -> 79.5 us  [gather_wide(): other = lax.ppermute(own, 'xlo', SWAP)]
    all_gather x1, waiting for transfers between devices: 46.3 us -> 40 us  [gather_wide(): own = lax.all_gather(x, 'z', axis=0, tiled=True)]
  transfers between devices with their start and end apart: 18 -> 18, of which waited for: 9 -> 8; matrix products, arithmetic and copies ran while one was open for 8% -> 9% of each run, Pallas kernels for 0% -> 0%
where the time goes in v7:
time: 385 us; the launch traced here: 380 us
  waiting for transfers between devices  276 us (72%)
  matrix products  34.4 us (9%)
  starting transfers between devices  31.9 us (8%)
  other arithmetic  23.2 us (6%)
  between operations  14.5 us (4%)
    ppermute x2, waiting for transfers between devices, scatter_wide(): got = lax.ppermute(give, 'xlo', SWAP)  88.5 us
    ppermute x1, waiting for transfers between devices, gather_wide(): other = lax.ppermute(own, 'xlo', SWAP)  79.5 us
    reduce_scatter x2, waiting for transfers between devices, scatter_wide(): lax.psum_scatter(total.reshape(zs * rows, -1), 'z', scatter_dimension=0,...  52.7 us
    all_gather x1, waiting for transfers between devices, gather_wide(): own = lax.all_gather(x, 'z', axis=0, tiled=True)  40 us
    ppermute x6, starting transfers between devices, from_behind(): return lax.ppermute(x, axis, pairs)  25.8 us
    ppermute x1, waiting for transfers between devices, gather_narrow(): other = lax.ppermute(x, 'xlo', SWAP)  10.5 us
    select_n x2, other arithmetic, in_order(): jnp.where(first, jnp.stack([mine, other], axis), jnp.stack([other, mine],...  8.28 us
  transfers between devices with their start and end apart: 18, of which 8 were waited for; matrix products, arithmetic and copies ran while one was open for 9% of the time, Pallas kernels for 0%

profile of v7, /device:TPU:5, one launch (start us, length us, event | category | flops | bytes accessed | tf_op | source)
XLA Modules:
  0.0 380.1 jit_solution(2604059128895331042)
XLA Ops:
  7.2 0.8 select_reduce_fusion.1
  8.1 0.7 select_reduce_fusion.2
  8.8 2.0 convolution_convert_fusion.3
  10.9 0.4 convolution_convert_fusion.4
  11.3 0.8 pad_maximum_fusion
  12.2 1.0 collective-permute-start.2
  13.2 10.5 %collective-permute-done.2 = bf16[32,7168]{1,0:T(8,128)(2,1)S(1)} collective-permute-done((bf16[32,7168]{1,0:T(8,128)(2,1)S(1)}, bf16[32,7168]{1,0:T(8,128)(2,1)S(1)}, u32[]{:S(2)}, u32[]{:S(2)}) %collective-permute-start.2) | collective-permute-done | bytes 458784 | tf_op jit(solution)/shard_map/ppermute | solution.py:44
  23.7 1.1 maximum_select_fusion.1
  24.8 40.0 %all-gather.3.cloned.1.call-done = bf16[256,7168]{1,0:T(8,128)(2,1)} async-done(((bf16[32,7168]{1,0:T(8,128)(2,1)}), bf16[256,7168]{1,0:T(8,128)(2,1)}) %all-gather.3.cloned.1.call-update) | async-done | bytes 3670032 | tf_op jit(solution)/shard_map/all_gather | solution.py:35
  64.8 0.9 collective-permute-start.1
  65.7 79.5 %collective-permute-done.1 = bf16[256,7168]{1,0:T(8,128)(2,1)S(1)} collective-permute-done((bf16[256,7168]{1,0:T(8,128)(2,1)}, bf16[256,7168]{1,0:T(8,128)(2,1)S(1)}, u32[]{:S(2)}, u32[]{:S(2)}) %collective-permute-start.1) | collective-permute-done | bytes 3670048 | tf_op jit(solution)/shard_map/ppermute | solution.py:36
  145.2 7.2 %maximum_select_fusion = bf16[8,2,32,7168]{3,2,1,0:T(8,128)(2,1)} fusion(bf16[8,1,32,7168]{3,2,1,0:T(8,128)(2,1)S(1)} %bitcast.112, bf16[8,1,32,7168]{3,2,1,0:T(8,128)(2,1)} %bitcast.111, pred[]{:T(512)S(6)} %eq.57), kind=kLoop, calls=%fused_computation.7 | loop fusion | flops 11010048 | bytes 14680065 | tf_op jit(solution)/shard_map/jit(_where)/select_n | solution.py:31
  152.5 3.3 fusion.7
  155.8 4.5 %fusion.19 = f32[512,128]{1,0:T(8,128)S(1)} fusion(f32[512,128]{1,0:T(8,128)S(1)} %fusion.7, bf16[512,7168]{1,0:T(8,128)(2,1)} %bitcast.104, bf16[1,7168,128]{2,1,0:T(8,128)(2,1)S(1)} %copy-done.4), kind=kOutput, calls=%fused_computation.38 | convolution fusion | flops 469827584 | bytes 5111808 | tf_op jit(solution)/shard_map/dot_general | solution.py:113
  160.3 1.1 fusion.9
  161.4 1.1 fusion.16
  162.9 1.1 fusion.3
  164.1 1.2 multiply_convert_fusion.2
  165.2 1.0 fusion.46
  166.2 3.8 add_convert_fusion.1
  170.1 2.6 convolution_convert_fusion.6
  173.0 2.6 fusion.27
  175.6 1.3 add_convert_fusion
  177.1 1.0 collective-permute-start.8
  178.1 44.7 %collective-permute-done.8 = bf16[8,32,4096]{2,1,0:T(8,128)(2,1)S(1)} collective-permute-done((bf16[8,32,4096]{2,1,0:T(8,128)(2,1)S(1)}, bf16[8,32,4096]{2,1,0:T(8,128)(2,1)S(1)}, u32[]{:S(2)}, u32[]{:S(2)}) %collective-permute-start.8) | collective-permute-done | bytes 2097184 | tf_op jit(solution)/shard_map/ppermute | solution.py:54
  222.8 2.4 fusion.1
  225.3 1.2 convolution_convert_fusion.5
  226.8 1.0 collective-permute-start.3
  227.8 43.8 %collective-permute-done.3 = bf16[8,32,4096]{2,1,0:T(8,128)(2,1)S(1)} collective-permute-done((bf16[8,32,4096]{2,1,0:T(8,128)(2,1)S(1)}, bf16[8,32,4096]{2,1,0:T(8,128)(2,1)S(1)}, u32[]{:S(2)}, u32[]{:S(2)}) %collective-permute-start.3) | collective-permute-done | bytes 2097184 | tf_op jit(solution)/shard_map/ppermute | solution.py:54
  271.6 2.6 fusion.2
  274.2 5.2 %collective-permute-start.7 = (s32[128]{0:T(128)S(1)}, s32[128]{0:T(128)S(1)}, u32[]{:S(2)}, u32[]{:S(2)}) collective-permute-start(s32[128]{0:T(128)S(1)} %add_select_fusion), channel_id=1, source_target_pairs={{16,0},{32,16},{48,32},{64,48},{80,64},{96,80},{112,96},{128,112},... | collective-permute-start | bytes 1544 | tf_op jit(solution)/shard_map/ppermute | solution.py:15
  279.5 3.0 collective-permute-start
  282.5 1.9 collective-permute-start.11
  284.4 6.0 %collective-permute-start.6 = (bf16[128,7168]{1,0:T(8,128)(2,1)}, bf16[128,7168]{1,0:T(8,128)(2,1)}, u32[]{:S(2)}, u32[]{:S(2)}) collective-permute-start(bf16[128,7168]{1,0:T(8,128)(2,1)} %bitcast.117), channel_id=1, source_target_pairs={{0,16},{16,32},{32,48},{48,64},{64,80},{80,96},{96,112},{112,128},... | collective-permute-start | bytes 5505032 | tf_op jit(solution)/shard_map/ppermute | solution.py:15
  290.6 1.7 broadcast_select_fusion
  292.4 1.8 collective-permute-start.9
  294.2 1.8 broadcast_select_fusion.1
  295.9 9.9 %reduce-scatter.9.cloned.1.call-done = bf16[32,4096]{1,0:T(8,128)(2,1)} async-done(((bf16[256,4096]{1,0:T(8,128)(2,1)}), bf16[32,4096]{1,0:T(8,128)(2,1)}) %reduce-scatter.9.cloned.1.call-update) | async-done | bytes 262160 | tf_op jit(solution)/shard_map/reduce_scatter | solution.py:56
  305.8 1.0 convert_element_type.125
  306.8 42.9 %reduce-scatter.5.cloned.1.call-done = bf16[32,4096]{1,0:T(8,128)(2,1)} async-done(((bf16[256,4096]{1,0:T(8,128)(2,1)}), bf16[32,4096]{1,0:T(8,128)(2,1)}) %reduce-scatter.5.cloned.1.call-update) | async-done | bytes 262160 | tf_op jit(solution)/shard_map/reduce_scatter | solution.py:56
  349.7 1.0 convert_element_type.110
  350.7 1.2 convert_add_fusion.2
  351.9 0.4 fusion.35
  352.2 6.6 %collective-permute-start.10 = (bf16[32,7168]{1,0:T(8,128)(2,1)S(1)}, bf16[32,7168]{1,0:T(8,128)(2,1)S(1)}, u32[]{:S(2)}, u32[]{:S(2)}) collective-permute-start(bf16[32,7168]{1,0:T(8,128)(2,1)S(1)} %fusion.35), channel_id=1, source_target_pairs={{16,0},{32,16},{48,32},{64,48},{80,64},{96,80},{112,96},{128,112},... | collective-permute-start | bytes 1376264 | tf_op jit(solution)/shard_map/ppermute | solution.py:15
  359.1 3.1 collective-permute-start.5
  362.2 4.2 %collective-permute-done.10 = bf16[32,7168]{1,0:T(8,128)(2,1)S(1)} collective-permute-done((bf16[32,7168]{1,0:T(8,128)(2,1)S(1)}, bf16[32,7168]{1,0:T(8,128)(2,1)S(1)}, u32[]{:S(2)}, u32[]{:S(2)}) %collective-permute-start.10) | collective-permute-done | bytes 458784 | tf_op jit(solution)/shard_map/ppermute | solution.py:15
  366.4 3.4 select_bitcast_fusion.2
  369.8 3.4 select_bitcast_fusion.3
  (57 shorter events, 1.9 us)
Async XLA Ops:
  7.2 3.7 copy-start.2
  7.2 57.7 %all-gather.3.cloned.1.call-start = ((), (), s32[]{:S(2)}) async-start(), calls=%async_computation.4 | async-start | bytes 4128768 | tf_op jit(solution)/shard_map/all_gather | solution.py:35
  12.1 140.3 %all-gather.5.cloned.1.call-start = ((), (), s32[]{:S(2)}) async-start(), calls=%async_computation.5 | async-start | bytes 8257536 | tf_op jit(solution)/shard_map/all_gather | solution.py:46
  12.2 11.5 %collective-permute-start.2 = (bf16[32,7168]{1,0:T(8,128)(2,1)S(1)}, bf16[32,7168]{1,0:T(8,128)(2,1)S(1)}, u32[]{:S(2)}, u32[]{:S(2)}) collective-permute-start(bf16[32,7168]{1,0:T(8,128)(2,1)S(1)} %get-tuple-element.12), channel_id=1, source_target_pairs={{0,8},{8,0},{1,9},{9,1},{2,10},{10,2},{3,11},{11,3},{4,12},{12,4},... | collective-permute-start | bytes 1376264 | tf_op jit(solution)/shard_map/ppermute | solution.py:44
  24.8 265.8 %reduce-scatter.11.cloned.1.call-start = ((), (), s32[]{:S(2)}) async-start(), calls=%async_computation.9 | async-start | bytes 3538944 | tf_op jit(solution)/shard_map/reduce_scatter | solution.py:61
  64.8 80.4 %collective-permute-start.1 = (bf16[256,7168]{1,0:T(8,128)(2,1)}, bf16[256,7168]{1,0:T(8,128)(2,1)S(1)}, u32[]{:S(2)}, u32[]{:S(2)}) collective-permute-start(bf16[256,7168]{1,0:T(8,128)(2,1)} %all-gather.3.cloned.1.call-done), channel_id=1, source_target_pairs={{0,8},{8,0},{1,9},{9,1},{2,10},{10,2},{3,11},{11,3},{4,12},{12,4},... | collective-permute-start | bytes 11010056 | tf_op jit(solution)/shard_map/ppermute | solution.py:36
  145.2 7.2 %copy-start.4 = (bf16[1,7168,128]{2,1,0:T(8,128)(2,1)S(1)}, bf16[1,7168,128]{2,1,0:T(8,128)(2,1)}, u32[]{:S(2)}) copy-start(bf16[1,7168,128]{2,1,0:T(8,128)(2,1)} %param.14) | copy-start | bytes 5505028
  152.4 7.8 %copy-start.7 = (bf16[512,7168]{1,0:T(8,128)(2,1)S(1)}, bf16[512,7168]{1,0:T(8,128)(2,1)}, u32[]{:S(2)}) copy-start(bf16[512,7168]{1,0:T(8,128)(2,1)} %all-gather.5.cloned.1.call-done) | copy-start | bytes 22020100
  152.4 9.0 %slice-start = ((s8[7340032]{0:T(1024)(128)(4,1)}), s8[4194304]{0:T(1024)(128)(4,1)S(1)}, s32[]{:S(2)}) async-start(s8[7340032]{0:T(1024)(128)(4,1)} %bitcast.105), calls=%async_computation.10 | async-start | bytes 8388608
  155.8 4.5 %copy-start.3 = (bf16[1,7168,128]{2,1,0:T(8,128)(2,1)S(1)}, bf16[1,7168,128]{2,1,0:T(8,128)(2,1)}, u32[]{:S(2)}) copy-start(bf16[1,7168,128]{2,1,0:T(8,128)(2,1)} %param.13) | copy-start | bytes 5505028
  155.8 5.6 %slice-start.1 = ((s8[7340032]{0:T(1024)(128)(4,1)}), s8[3145728]{0:T(1024)(128)(4,1)S(1)}, s32[]{:S(2)}) async-start(s8[7340032]{0:T(1024)(128)(4,1)} %bitcast.105), calls=%async_computation.11 | async-start | bytes 6291456
  161.4 1.5 copy-start.1
  170.0 124.1 %reduce-scatter.7.cloned.1.call-start = ((), (), s32[]{:S(2)}) async-start(), calls=%async_computation.7 | async-start | bytes 3538944 | tf_op jit(solution)/shard_map/reduce_scatter | solution.py:61
  172.7 133.1 %reduce-scatter.9.cloned.1.call-start = ((), (), s32[]{:S(2)}) async-start(), calls=%async_computation.8 | async-start | bytes 2359296 | tf_op jit(solution)/shard_map/reduce_scatter | solution.py:56
  172.9 2.6 copy-start.5
  177.1 45.7 %collective-permute-start.8 = (bf16[8,32,4096]{2,1,0:T(8,128)(2,1)S(1)}, bf16[8,32,4096]{2,1,0:T(8,128)(2,1)S(1)}, u32[]{:S(2)}, u32[]{:S(2)}) collective-permute-start(bf16[8,32,4096]{2,1,0:T(8,128)(2,1)S(1)} %select_bitcast_fusion), channel_id=1, source_target_pairs={{0,8},{8,0},{1,9},{9,1},{2,10},{10,2},{3,11},{11,3},{4,12},{12,4},... | collective-permute-start | bytes 6291464 | tf_op jit(solution)/shard_map/ppermute | solution.py:54
  225.2 124.4 %reduce-scatter.5.cloned.1.call-start = ((), (), s32[]{:S(2)}) async-start(), calls=%async_computation.6 | async-start | bytes 2359296 | tf_op jit(solution)/shard_map/reduce_scatter | solution.py:56
  226.8 55.7 %copy-start = (bf16[1,128,7168]{2,1,0:T(8,128)(2,1)S(1)}, bf16[1,128,7168]{2,1,0:T(8,128)(2,1)}, u32[]{:S(2)}) copy-start(bf16[1,128,7168]{2,1,0:T(8,128)(2,1)} %param.9) | copy-start | bytes 5505028
  226.8 44.8 %collective-permute-start.3 = (bf16[8,32,4096]{2,1,0:T(8,128)(2,1)S(1)}, bf16[8,32,4096]{2,1,0:T(8,128)(2,1)S(1)}, u32[]{:S(2)}, u32[]{:S(2)}) collective-permute-start(bf16[8,32,4096]{2,1,0:T(8,128)(2,1)S(1)} %select_bitcast_fusion.1), channel_id=1, source_target_pairs={{0,8},{8,0},{1,9},{9,1},{2,10},{10,2},{3,11},{11,3},{4,12},{12,4},... | collective-permute-start | bytes 6291464 | tf_op jit(solution)/shard_map/ppermute | solution.py:54
  274.2 16.3 %collective-permute-start.7 = (s32[128]{0:T(128)S(1)}, s32[128]{0:T(128)S(1)}, u32[]{:S(2)}, u32[]{:S(2)}) collective-permute-start(s32[128]{0:T(128)S(1)} %add_select_fusion), channel_id=1, source_target_pairs={{16,0},{32,16},{48,32},{64,48},{80,64},{96,80},{112,96},{128,112},... | collective-permute-start | bytes 1544 | tf_op jit(solution)/shard_map/ppermute | solution.py:15
  279.5 82.7 %collective-permute-start = (s32[128]{0:T(128)S(1)}, s32[128]{0:T(128)S(1)}, u32[]{:S(2)}, u32[]{:S(2)}) collective-permute-start(s32[128]{0:T(128)S(1)} %add_select_fusion), channel_id=1, source_target_pairs={{0,16},{16,32},{32,48},{48,64},{64,80},{80,96},{96,112},{112,128},... | collective-permute-start | bytes 1544 | tf_op jit(solution)/shard_map/ppermute | solution.py:15
  282.5 79.7 %collective-permute-start.11 = (bf16[128,7168]{1,0:T(8,128)(2,1)S(1)}, bf16[128,7168]{1,0:T(8,128)(2,1)}, u32[]{:S(2)}, u32[]{:S(2)}) collective-permute-start(bf16[128,7168]{1,0:T(8,128)(2,1)S(1)} %bitcast.109), channel_id=1, source_target_pairs={{16,0},{32,16},{48,32},{64,48},{80,64},{96,80},{112,96},{128,112},... | collective-permute-start | bytes 5505032 | tf_op jit(solution)/shard_map/ppermute | solution.py:15
  284.4 85.4 %collective-permute-start.6 = (bf16[128,7168]{1,0:T(8,128)(2,1)}, bf16[128,7168]{1,0:T(8,128)(2,1)}, u32[]{:S(2)}, u32[]{:S(2)}) collective-permute-start(bf16[128,7168]{1,0:T(8,128)(2,1)} %bitcast.117), channel_id=1, source_target_pairs={{0,16},{16,32},{32,48},{48,64},{64,80},{80,96},{96,112},{112,128},... | collective-permute-start | bytes 5505032 | tf_op jit(solution)/shard_map/ppermute | solution.py:15
  292.4 58.3 %collective-permute-start.9 = (bf16[32,3072]{1,0:T(8,128)(2,1)}, bf16[32,3072]{1,0:T(8,128)(2,1)}, u32[]{:S(2)}, u32[]{:S(2)}) collective-permute-start(bf16[32,3072]{1,0:T(8,128)(2,1)} %broadcast_select_fusion), channel_id=1, source_target_pairs={{0,8},{8,0},{1,9},{9,1},{2,10},{10,2},{3,11},{11,3},{4,12},{12,4},... | collective-permute-start | bytes 589832 | tf_op jit(solution)/shard_map/ppermute | solution.py:65
  294.2 64.7 %copy-start.6 = (bf16[64,3072]{1,0:T(8,128)(2,1)S(1)}, bf16[64,3072]{1,0:T(8,128)(2,1)}, u32[]{:S(2)}) copy-start(bf16[64,3072]{1,0:T(8,128)(2,1)} %reduce-scatter.7.cloned.1.call-done) | copy-start | bytes 1179652
  295.9 62.9 %collective-permute-start.4 = (bf16[32,3072]{1,0:T(8,128)(2,1)}, bf16[32,3072]{1,0:T(8,128)(2,1)S(1)}, u32[]{:S(2)}, u32[]{:S(2)}) collective-permute-start(bf16[32,3072]{1,0:T(8,128)(2,1)} %broadcast_select_fusion.1), channel_id=1, source_target_pairs={{0,8},{8,0},{1,9},{9,1},{2,10},{10,2},{3,11},{11,3},{4,12},{12,4},... | collective-permute-start | bytes 589832 | tf_op jit(solution)/shard_map/ppermute | solution.py:65
  352.2 14.2 %collective-permute-start.10 = (bf16[32,7168]{1,0:T(8,128)(2,1)S(1)}, bf16[32,7168]{1,0:T(8,128)(2,1)S(1)}, u32[]{:S(2)}, u32[]{:S(2)}) collective-permute-start(bf16[32,7168]{1,0:T(8,128)(2,1)S(1)} %fusion.35), channel_id=1, source_target_pairs={{16,0},{32,16},{48,32},{64,48},{80,64},{96,80},{112,96},{128,112},... | collective-permute-start | bytes 1376264 | tf_op jit(solution)/shard_map/ppermute | solution.py:15
  359.1 10.7 %collective-permute-start.5 = (bf16[32,7168]{1,0:T(8,128)(2,1)S(1)}, bf16[32,7168]{1,0:T(8,128)(2,1)S(1)}, u32[]{:S(2)}, u32[]{:S(2)}) collective-permute-start(bf16[32,7168]{1,0:T(8,128)(2,1)S(1)} %fusion.34), channel_id=1, source_target_pairs={{0,16},{16,32},{32,48},{48,64},{64,80},{80,96},{96,112},{112,128},... | collective-permute-start | bytes 1376264 | tf_op jit(solution)/shard_map/ppermute | solution.py:15
Sparse Core Ops, SparseCore 0:
  12.2 52.5 all-gather.2
  67.2 82.8 all-gather.4
  170.2 43.4 reduce-scatter.10
  216.1 46.4 reduce-scatter.6
  265.0 40.7 reduce-scatter.8
  308.2 41.4 reduce-scatter.4

commit v8 on v7

--- a/solution.py
+++ b/solution.py
@@ -31,13 +31,10 @@
     return jnp.where(first, jnp.stack([mine, other], axis), jnp.stack([other, mine], axis))
 
 
-def gather_wide(x, first):
+def gather_wide(x):
     own = lax.all_gather(x, "z", axis=0, tiled=True)
     other = lax.ppermute(own, "xlo", SWAP)
-    zs = own.shape[0] // x.shape[0]
-    rows = x.shape[0]
-    both = in_order(first, own.reshape(zs, rows, -1), other.reshape(zs, rows, -1), 1)
-    return both.reshape(zs * 2 * rows, -1)
+    return own, other
 
 
 def gather_narrow(x, first):
@@ -101,16 +98,24 @@
     back = jnp.dot(table, carried, preferred_element_type=jnp.float32).astype(jnp.bfloat16)
 
     narrow = width - wide
-    both_a = gather_wide(jnp.concatenate([sent[:, :wide], back[:, :wide]], axis=1), first)
+    own_a, other_a = gather_wide(jnp.concatenate([sent[:, :wide], back[:, :wide]], axis=1))
     both_b = gather_narrow(jnp.concatenate([sent[:, wide:], back[:, wide:]], axis=1), first)
-    sent_a, back_a = both_a[:, :wide], both_a[:, wide:]
+    zs = own_a.shape[0] // CAP
+
+    def rows_in_order(rows, mat):
+        mine = jnp.dot(rows[0], mat, preferred_element_type=jnp.float32).reshape(zs, CAP, -1)
+        theirs = jnp.dot(rows[1], mat, preferred_element_type=jnp.float32).reshape(zs, CAP, -1)
+        return in_order(first, mine, theirs, 1).reshape(zs * 2 * CAP, -1)
+
+    sent_a = (own_a[:, :wide], other_a[:, :wide])
+    back_a = (own_a[:, wide:], other_a[:, wide:])
     sent_b, back_b = both_b[:, :narrow], both_b[:, narrow:]
 
     f32 = jnp.float32
-    gate = jnp.dot(sent_a, gate_mat[:wide], preferred_element_type=f32) + jnp.dot(
+    gate = rows_in_order(sent_a, gate_mat[:wide]) + jnp.dot(
         sent_b, gate_mat[wide:], preferred_element_type=f32
     )
-    up = jnp.dot(sent_a, up_mat[:wide], preferred_element_type=f32) + jnp.dot(
+    up = rows_in_order(sent_a, up_mat[:wide]) + jnp.dot(
         sent_b, up_mat[wide:], preferred_element_type=f32
     )
     act, slope = silu_parts(gate)
@@ -118,7 +123,7 @@
     ahead_a = jnp.dot(hidden, down_mat[:, :wide_r], preferred_element_type=f32).astype(jnp.bfloat16)
     ahead_b = jnp.dot(hidden, down_mat[:, wide_r:], preferred_element_type=f32).astype(jnp.bfloat16)
     comb_b = scatter_narrow(ahead_b, first, CAP)
-    grad_hidden = jnp.dot(back_a, down_mat[:, :wide].T, preferred_element_type=f32) + jnp.dot(
+    grad_hidden = rows_in_order(back_a, down_mat[:, :wide].T) + jnp.dot(
         back_b, down_mat[:, wide:].T, preferred_element_type=f32
     )
     grad_up = (grad_hidden * act).astype(jnp.bfloat16)

time: 385 us -> 377 us (0.979)
  other arithmetic: 23.2 us -> 15.9 us
  local copies, waits for them, and re-layouts: 0.45 us -> 5.17 us
    select_n x2 -> x3, other arithmetic: 8.28 us -> 1.13 us  [in_order(): jnp.where(first, jnp.stack([mine, other], axis), jnp.stack([other, mine],...]
    ppermute x1, waiting for transfers between devices: 79.5 us -> 74 us  [gather_wide(): other = lax.ppermute(own, 'xlo', SWAP)]
  transfers between devices with their start and end apart: 18 -> 18, of which waited for: 8 -> 9; matrix products, arithmetic and copies ran while one was open for 9% -> 8% of each run, Pallas kernels for 0% -> 0%
where the time goes in v8:
time: 377 us; the launch traced here: 372 us
  waiting for transfers between devices  273 us (72%)
  matrix products  31.8 us (8%)
  starting transfers between devices  31.4 us (8%)
  other arithmetic  15.9 us (4%)
  between operations  14.6 us (4%)
  local copies, waits for them, and re-layouts  5.17 us (1%)
    ppermute x2, waiting for transfers between devices, scatter_wide(): got = lax.ppermute(give, 'xlo', SWAP)  90.1 us
    ppermute x1, waiting for transfers between devices, gather_wide(): other = lax.ppermute(own, 'xlo', SWAP)  74 us
    reduce_scatter x2, waiting for transfers between devices, scatter_wide(): lax.psum_scatter(total.reshape(zs * rows, -1), 'z', scatter_dimension=0,...  51.2 us
    all_gather x1, waiting for transfers between devices, gather_wide(): own = lax.all_gather(x, 'z', axis=0, tiled=True)  40 us
    ppermute x6, starting transfers between devices, from_behind(): return lax.ppermute(x, axis, pairs)  25.6 us
    ppermute x1, waiting for transfers between devices, gather_narrow(): other = lax.ppermute(x, 'xlo', SWAP)  10.5 us
  transfers between devices with their start and end apart: 18, of which 9 were waited for; matrix products, arithmetic and copies ran while one was open for 8% of the time, Pallas kernels for 0%

profile of v8, /device:TPU:5, one launch (start us, length us, event | category | flops | bytes accessed | tf_op | source)
XLA Modules:
  0.0 371.6 jit_solution(4529905051845474447)
XLA Ops:
  7.2 0.8 select_reduce_fusion.1
  8.1 0.7 select_reduce_fusion.2
  8.8 2.0 convolution_convert_fusion.3
  11.3 0.8 pad_maximum_fusion
  12.2 1.0 collective-permute-start.2
  13.2 10.5 %collective-permute-done.2 = bf16[32,7168]{1,0:T(8,128)(2,1)S(1)} collective-permute-done((bf16[32,7168]{1,0:T(8,128)(2,1)S(1)}, bf16[32,7168]{1,0:T(8,128)(2,1)S(1)}, u32[]{:S(2)}, u32[]{:S(2)}) %collective-permute-start.2) | collective-permute-done | bytes 458784 | tf_op jit(solution)/shard_map/ppermute | solution.py:41
  23.7 1.1 maximum_select_fusion
  24.8 40.0 %all-gather.3.cloned.1.call-done = bf16[256,7168]{1,0:T(8,128)(2,1)} async-done(((bf16[32,7168]{1,0:T(8,128)(2,1)}), bf16[256,7168]{1,0:T(8,128)(2,1)}) %all-gather.3.cloned.1.call-update) | async-done | bytes 3670032 | tf_op jit(solution)/shard_map/all_gather | solution.py:35
  64.8 0.9 collective-permute-start.1
  65.7 1.8 slice.166
  68.2 0.8 copy-done.3
  69.7 0.9 copy-done.1
  71.2 74.0 %collective-permute-done.1 = bf16[256,7168]{1,0:T(8,128)(2,1)S(1)} collective-permute-done((bf16[256,7168]{1,0:T(8,128)(2,1)}, bf16[256,7168]{1,0:T(8,128)(2,1)S(1)}, u32[]{:S(2)}, u32[]{:S(2)}) %collective-permute-start.1) | collective-permute-done | bytes 3670048 | tf_op jit(solution)/shard_map/ppermute | solution.py:36
  146.7 0.7 fusion.9
  147.4 2.6 all-gather.5.cloned.1.call-done
  150.1 3.6 fusion.17
  153.7 1.4 copy-done.11
  155.1 1.1 fusion.14
  156.2 1.2 multiply_convert_fusion.2
  157.4 1.0 fusion.49
  158.4 3.8 %add_convert_fusion.1 = bf16[512,3072]{1,0:T(8,128)(2,1)} fusion(f32[512,3072]{1,0:T(8,128)S(1)} %fusion.49, bf16[512,128]{1,0:T(8,128)(2,1)S(1)} %get-tuple-element.4, bf16[1,7168,128]{2,1,0:T(8,128)(2,1)} %param.14), kind=kOutput, calls=%fused_computation.7 | convolution fusion | flops 405798912 | bytes 10354688 | tf_op jit(solution)/shard_map/dot_general | solution.py:133
  162.5 2.6 convolution_convert_fusion.6
  165.2 2.6 fusion.25
  167.8 1.3 add_convert_fusion
  169.3 1.0 collective-permute-start.8
  170.3 45.5 %collective-permute-done.8 = bf16[8,32,4096]{2,1,0:T(8,128)(2,1)S(1)} collective-permute-done((bf16[8,32,4096]{2,1,0:T(8,128)(2,1)S(1)}, bf16[8,32,4096]{2,1,0:T(8,128)(2,1)S(1)}, u32[]{:S(2)}, u32[]{:S(2)}) %collective-permute-start.8) | collective-permute-done | bytes 2097184 | tf_op jit(solution)/shard_map/ppermute | solution.py:51
  215.7 2.4 fusion.1
  218.2 1.2 convolution_convert_fusion.5
  219.7 1.0 collective-permute-start.3
  220.7 44.6 %collective-permute-done.3 = bf16[8,32,4096]{2,1,0:T(8,128)(2,1)S(1)} collective-permute-done((bf16[8,32,4096]{2,1,0:T(8,128)(2,1)S(1)}, bf16[8,32,4096]{2,1,0:T(8,128)(2,1)S(1)}, u32[]{:S(2)}, u32[]{:S(2)}) %collective-permute-start.3) | collective-permute-done | bytes 2097184 | tf_op jit(solution)/shard_map/ppermute | solution.py:51
  265.3 2.6 fusion.2
  267.9 4.6 %collective-permute-start.7 = (s32[128]{0:T(128)S(1)}, s32[128]{0:T(128)S(1)}, u32[]{:S(2)}, u32[]{:S(2)}) collective-permute-start(s32[128]{0:T(128)S(1)} %add_select_fusion), channel_id=1, source_target_pairs={{16,0},{32,16},{48,32},{64,48},{80,64},{96,80},{112,96},{128,112},... | collective-permute-start | bytes 1544 | tf_op jit(solution)/shard_map/ppermute | solution.py:15
  272.5 3.5 collective-permute-start
  276.1 1.9 collective-permute-start.11
  278.0 6.0 %collective-permute-start.6 = (bf16[128,7168]{1,0:T(8,128)(2,1)}, bf16[128,7168]{1,0:T(8,128)(2,1)}, u32[]{:S(2)}, u32[]{:S(2)}) collective-permute-start(bf16[128,7168]{1,0:T(8,128)(2,1)} %bitcast.131), channel_id=1, source_target_pairs={{0,16},{16,32},{32,48},{48,64},{64,80},{80,96},{96,112},{112,128},... | collective-permute-start | bytes 5505032 | tf_op jit(solution)/shard_map/ppermute | solution.py:15
  284.2 1.8 broadcast_select_fusion
  286.0 1.3 collective-permute-start.9
  287.3 1.7 broadcast_select_fusion.1
  289.2 8.4 %reduce-scatter.9.cloned.1.call-done = bf16[32,4096]{1,0:T(8,128)(2,1)} async-done(((bf16[256,4096]{1,0:T(8,128)(2,1)}), bf16[32,4096]{1,0:T(8,128)(2,1)}) %reduce-scatter.9.cloned.1.call-update) | async-done | bytes 262160 | tf_op jit(solution)/shard_map/reduce_scatter | solution.py:53
  297.6 1.0 convert_element_type.125
  298.6 42.8 %reduce-scatter.5.cloned.1.call-done = bf16[32,4096]{1,0:T(8,128)(2,1)} async-done(((bf16[256,4096]{1,0:T(8,128)(2,1)}), bf16[32,4096]{1,0:T(8,128)(2,1)}) %reduce-scatter.5.cloned.1.call-update) | async-done | bytes 262160 | tf_op jit(solution)/shard_map/reduce_scatter | solution.py:53
  341.4 1.0 convert_element_type.110
  342.4 1.0 convert_add_fusion.2
  343.8 6.8 %collective-permute-start.10 = (bf16[32,7168]{1,0:T(8,128)(2,1)S(1)}, bf16[32,7168]{1,0:T(8,128)(2,1)S(1)}, u32[]{:S(2)}, u32[]{:S(2)}) collective-permute-start(bf16[32,7168]{1,0:T(8,128)(2,1)S(1)} %fusion.32), channel_id=1, source_target_pairs={{16,0},{32,16},{48,32},{64,48},{80,64},{96,80},{112,96},{128,112},... | collective-permute-start | bytes 1376264 | tf_op jit(solution)/shard_map/ppermute | solution.py:15
  350.9 2.7 collective-permute-start.5
  353.7 4.3 %collective-permute-done.10 = bf16[32,7168]{1,0:T(8,128)(2,1)S(1)} collective-permute-done((bf16[32,7168]{1,0:T(8,128)(2,1)S(1)}, bf16[32,7168]{1,0:T(8,128)(2,1)S(1)}, u32[]{:S(2)}, u32[]{:S(2)}) %collective-permute-start.10) | collective-permute-done | bytes 458784 | tf_op jit(solution)/shard_map/ppermute | solution.py:15
  357.9 3.4 select_bitcast_fusion.2
  361.4 3.4 select_bitcast_fusion.3
  (69 shorter events, 5.9 us)
Async XLA Ops:
  7.2 3.7 copy-start.2
  7.2 57.7 %all-gather.3.cloned.1.call-start = ((), (), s32[]{:S(2)}) async-start(), calls=%async_computation.4 | async-start | bytes 4128768 | tf_op jit(solution)/shard_map/all_gather | solution.py:35
  12.1 138.0 %all-gather.5.cloned.1.call-start = ((), (), s32[]{:S(2)}) async-start(), calls=%async_computation.5 | async-start | bytes 8257536 | tf_op jit(solution)/shard_map/all_gather | solution.py:43
  12.2 11.5 %collective-permute-start.2 = (bf16[32,7168]{1,0:T(8,128)(2,1)S(1)}, bf16[32,7168]{1,0:T(8,128)(2,1)S(1)}, u32[]{:S(2)}, u32[]{:S(2)}) collective-permute-start(bf16[32,7168]{1,0:T(8,128)(2,1)S(1)} %get-tuple-element.8), channel_id=1, source_target_pairs={{0,8},{8,0},{1,9},{9,1},{2,10},{10,2},{3,11},{11,3},{4,12},{12,4},... | collective-permute-start | bytes 1376264 | tf_op jit(solution)/shard_map/ppermute | solution.py:41
  24.8 42.8 %copy-start.5 = (bf16[1,7168,128]{2,1,0:T(8,128)(2,1)S(1)}, bf16[1,7168,128]{2,1,0:T(8,128)(2,1)}, u32[]{:S(2)}) copy-start(bf16[1,7168,128]{2,1,0:T(8,128)(2,1)} %param.14) | copy-start | bytes 5505028
  24.8 259.4 %reduce-scatter.11.cloned.1.call-start = ((), (), s32[]{:S(2)}) async-start(), calls=%async_computation.9 | async-start | bytes 3538944 | tf_op jit(solution)/shard_map/reduce_scatter | solution.py:58
  64.8 80.4 %collective-permute-start.1 = (bf16[256,7168]{1,0:T(8,128)(2,1)}, bf16[256,7168]{1,0:T(8,128)(2,1)S(1)}, u32[]{:S(2)}, u32[]{:S(2)}) collective-permute-start(bf16[256,7168]{1,0:T(8,128)(2,1)} %all-gather.3.cloned.1.call-done), channel_id=1, source_target_pairs={{0,8},{8,0},{1,9},{9,1},{2,10},{10,2},{3,11},{11,3},{4,12},{12,4},... | collective-permute-start | bytes 11010056 | tf_op jit(solution)/shard_map/ppermute | solution.py:36
  65.7 3.9 %copy-start.10 = (bf16[256,7168]{1,0:T(8,128)(2,1)S(1)}, bf16[256,7168]{1,0:T(8,128)(2,1)}, u32[]{:S(2)}) copy-start(bf16[256,7168]{1,0:T(8,128)(2,1)} %all-gather.3.cloned.1.call-done) | copy-start | bytes 11010052
  67.5 1.5 copy-start.3
  69.0 1.5 copy-start.1
  71.2 74.2 %copy-start.6 = (bf16[1,7168,128]{2,1,0:T(8,128)(2,1)S(1)}, bf16[1,7168,128]{2,1,0:T(8,128)(2,1)}, u32[]{:S(2)}) copy-start(bf16[1,7168,128]{2,1,0:T(8,128)(2,1)} %param.14) | copy-start | bytes 5505028
  150.1 3.6 copy-start.4
  150.1 5.0 %copy-start.11 = (bf16[512,7168]{1,0:T(8,128)(2,1)S(1)}, bf16[512,7168]{1,0:T(8,128)(2,1)}, u32[]{:S(2)}) copy-start(bf16[512,7168]{1,0:T(8,128)(2,1)} %all-gather.5.cloned.1.call-done) | copy-start | bytes 22020100
  162.3 125.1 %reduce-scatter.7.cloned.1.call-start = ((), (), s32[]{:S(2)}) async-start(), calls=%async_computation.7 | async-start | bytes 3538944 | tf_op jit(solution)/shard_map/reduce_scatter | solution.py:58
  165.1 132.5 %reduce-scatter.9.cloned.1.call-start = ((), (), s32[]{:S(2)}) async-start(), calls=%async_computation.8 | async-start | bytes 2359296 | tf_op jit(solution)/shard_map/reduce_scatter | solution.py:53
  165.2 2.6 copy-start.7
  169.3 46.4 %collective-permute-start.8 = (bf16[8,32,4096]{2,1,0:T(8,128)(2,1)S(1)}, bf16[8,32,4096]{2,1,0:T(8,128)(2,1)S(1)}, u32[]{:S(2)}, u32[]{:S(2)}) collective-permute-start(bf16[8,32,4096]{2,1,0:T(8,128)(2,1)S(1)} %select_bitcast_fusion), channel_id=1, source_target_pairs={{0,8},{8,0},{1,9},{9,1},{2,10},{10,2},{3,11},{11,3},{4,12},{12,4},... | collective-permute-start | bytes 6291464 | tf_op jit(solution)/shard_map/ppermute | solution.py:51
  218.2 123.2 %reduce-scatter.5.cloned.1.call-start = ((), (), s32[]{:S(2)}) async-start(), calls=%async_computation.6 | async-start | bytes 2359296 | tf_op jit(solution)/shard_map/reduce_scatter | solution.py:53
  219.7 45.6 %collective-permute-start.3 = (bf16[8,32,4096]{2,1,0:T(8,128)(2,1)S(1)}, bf16[8,32,4096]{2,1,0:T(8,128)(2,1)S(1)}, u32[]{:S(2)}, u32[]{:S(2)}) collective-permute-start(bf16[8,32,4096]{2,1,0:T(8,128)(2,1)S(1)} %select_bitcast_fusion.1), channel_id=1, source_target_pairs={{0,8},{8,0},{1,9},{9,1},{2,10},{10,2},{3,11},{11,3},{4,12},{12,4},... | collective-permute-start | bytes 6291464 | tf_op jit(solution)/shard_map/ppermute | solution.py:51
  267.9 8.2 %copy-start = (bf16[1,128,7168]{2,1,0:T(8,128)(2,1)S(1)}, bf16[1,128,7168]{2,1,0:T(8,128)(2,1)}, u32[]{:S(2)}) copy-start(bf16[1,128,7168]{2,1,0:T(8,128)(2,1)} %param.9) | copy-start | bytes 5505028
  267.9 16.2 %collective-permute-start.7 = (s32[128]{0:T(128)S(1)}, s32[128]{0:T(128)S(1)}, u32[]{:S(2)}, u32[]{:S(2)}) collective-permute-start(s32[128]{0:T(128)S(1)} %add_select_fusion), channel_id=1, source_target_pairs={{16,0},{32,16},{48,32},{64,48},{80,64},{96,80},{112,96},{128,112},... | collective-permute-start | bytes 1544 | tf_op jit(solution)/shard_map/ppermute | solution.py:15
  272.5 81.1 %collective-permute-start = (s32[128]{0:T(128)S(1)}, s32[128]{0:T(128)S(1)}, u32[]{:S(2)}, u32[]{:S(2)}) collective-permute-start(s32[128]{0:T(128)S(1)} %add_select_fusion), channel_id=1, source_target_pairs={{0,16},{16,32},{32,48},{48,64},{64,80},{80,96},{96,112},{112,128},... | collective-permute-start | bytes 1544 | tf_op jit(solution)/shard_map/ppermute | solution.py:15
  276.1 77.6 %collective-permute-start.11 = (bf16[128,7168]{1,0:T(8,128)(2,1)S(1)}, bf16[128,7168]{1,0:T(8,128)(2,1)}, u32[]{:S(2)}, u32[]{:S(2)}) collective-permute-start(bf16[128,7168]{1,0:T(8,128)(2,1)S(1)} %bitcast.120), channel_id=1, source_target_pairs={{16,0},{32,16},{48,32},{64,48},{80,64},{96,80},{112,96},{128,112},... | collective-permute-start | bytes 5505032 | tf_op jit(solution)/shard_map/ppermute | solution.py:15
  278.0 83.4 %collective-permute-start.6 = (bf16[128,7168]{1,0:T(8,128)(2,1)}, bf16[128,7168]{1,0:T(8,128)(2,1)}, u32[]{:S(2)}, u32[]{:S(2)}) collective-permute-start(bf16[128,7168]{1,0:T(8,128)(2,1)} %bitcast.131), channel_id=1, source_target_pairs={{0,16},{16,32},{32,48},{48,64},{64,80},{80,96},{96,112},{112,128},... | collective-permute-start | bytes 5505032 | tf_op jit(solution)/shard_map/ppermute | solution.py:15
  284.2 58.1 %copy-start.9 = (bf16[64,3072]{1,0:T(8,128)(2,1)S(1)}, bf16[64,3072]{1,0:T(8,128)(2,1)}, u32[]{:S(2)}) copy-start(bf16[64,3072]{1,0:T(8,128)(2,1)} %reduce-scatter.11.cloned.1.call-done) | copy-start | bytes 1179652
  286.0 56.3 %collective-permute-start.9 = (bf16[32,3072]{1,0:T(8,128)(2,1)}, bf16[32,3072]{1,0:T(8,128)(2,1)}, u32[]{:S(2)}, u32[]{:S(2)}) collective-permute-start(bf16[32,3072]{1,0:T(8,128)(2,1)} %broadcast_select_fusion), channel_id=1, source_target_pairs={{0,8},{8,0},{1,9},{9,1},{2,10},{10,2},{3,11},{11,3},{4,12},{12,4},... | collective-permute-start | bytes 589832 | tf_op jit(solution)/shard_map/ppermute | solution.py:62
  289.0 61.6 %collective-permute-start.4 = (bf16[32,3072]{1,0:T(8,128)(2,1)}, bf16[32,3072]{1,0:T(8,128)(2,1)S(1)}, u32[]{:S(2)}, u32[]{:S(2)}) collective-permute-start(bf16[32,3072]{1,0:T(8,128)(2,1)} %broadcast_select_fusion.1), channel_id=1, source_target_pairs={{0,8},{8,0},{1,9},{9,1},{2,10},{10,2},{3,11},{11,3},{4,12},{12,4},... | collective-permute-start | bytes 589832 | tf_op jit(solution)/shard_map/ppermute | solution.py:62
  342.3 8.3 %copy-start.8 = (bf16[64,3072]{1,0:T(8,128)(2,1)S(1)}, bf16[64,3072]{1,0:T(8,128)(2,1)}, u32[]{:S(2)}) copy-start(bf16[64,3072]{1,0:T(8,128)(2,1)} %reduce-scatter.7.cloned.1.call-done) | copy-start | bytes 1179652
  343.8 14.1 %collective-permute-start.10 = (bf16[32,7168]{1,0:T(8,128)(2,1)S(1)}, bf16[32,7168]{1,0:T(8,128)(2,1)S(1)}, u32[]{:S(2)}, u32[]{:S(2)}) collective-permute-start(bf16[32,7168]{1,0:T(8,128)(2,1)S(1)} %fusion.32), channel_id=1, source_target_pairs={{16,0},{32,16},{48,32},{64,48},{80,64},{96,80},{112,96},{128,112},... | collective-permute-start | bytes 1376264 | tf_op jit(solution)/shard_map/ppermute | solution.py:15
  350.9 10.4 %collective-permute-start.5 = (bf16[32,7168]{1,0:T(8,128)(2,1)S(1)}, bf16[32,7168]{1,0:T(8,128)(2,1)S(1)}, u32[]{:S(2)}, u32[]{:S(2)}) collective-permute-start(bf16[32,7168]{1,0:T(8,128)(2,1)S(1)} %fusion.31), channel_id=1, source_target_pairs={{0,16},{16,32},{32,48},{48,64},{64,80},{80,96},{96,112},{112,128},... | collective-permute-start | bytes 1376264 | tf_op jit(solution)/shard_map/ppermute | solution.py:15
Sparse Core Ops, SparseCore 0:
  12.2 52.5 all-gather.2
  67.2 82.8 all-gather.4
  162.4 42.4 reduce-scatter.10
  207.3 46.4 reduce-scatter.6
  256.2 41.3 reduce-scatter.8
  300.0 41.3 reduce-scatter.4

commit v9 on v8

--- a/solution.py
+++ b/solution.py
@@ -103,7 +103,8 @@
     zs = own_a.shape[0] // CAP
 
     def rows_in_order(rows, mat):
-        mine = jnp.dot(rows[0], mat, preferred_element_type=jnp.float32).reshape(zs, CAP, -1)
+        mine = jnp.dot(rows[0], mat, preferred_element_type=jnp.float32)
+        mine = mine.reshape(zs, CAP, -1)
         theirs = jnp.dot(rows[1], mat, preferred_element_type=jnp.float32).reshape(zs, CAP, -1)
         return in_order(first, mine, theirs, 1).reshape(zs * 2 * CAP, -1)
 
@@ -140,12 +141,14 @@
     inw_b = scatter_narrow(behind_b, first, CAP)
     inw_a = scatter_wide(behind_a, first, CAP)
     combined = jnp.concatenate([comb_a, comb_b], axis=1)
-    inward = jnp.concatenate([inw_a, inw_b], axis=1)
 
     out_rows = (sent.astype(f32) + wslot[:, None] * combined).astype(jnp.bfloat16)
-    grad_rows = (cot_sent.astype(f32) + inward).astype(jnp.bfloat16)
+    rows_a = (cot_sent[:, :wide_r].astype(f32) + inw_a).astype(jnp.bfloat16)
+    rows_b = (cot_sent[:, wide_r:].astype(f32) + inw_b).astype(jnp.bfloat16)
     out_prev = from_behind(out_rows, "section", 1)
-    grad_next = from_behind(grad_rows, "section", -1)
+    grad_next_b = from_behind(rows_b, "section", -1)
+    grad_next_a = from_behind(rows_a, "section", -1)
+    grad_next = jnp.concatenate([grad_next_a, grad_next_b], axis=1)
     next_input = pick_rows(route_prev, out_prev, tok_prev)
     prior_grad = pick_rows(route_next, grad_next, cot_next)
     return (next_input[None], prior_grad[None])

time: 377 us -> 426 us (1.13)
  waiting for transfers between devices: 273 us -> 317 us
    reduce_scatter x2, waiting for transfers between devices: 0.02 us -> 54.1 us  [scatter_narrow(): t = lax.psum_scatter(q, 'z', scatter_dimension=0, tiled=True)]
    reduce_scatter x2, waiting for transfers between devices: 51.2 us -> 41.3 us  [scatter_wide(): lax.psum_scatter(total.reshape(zs * rows, -1), 'z', scatter_dimension=0,...]
    ppermute x6 -> x7, starting transfers between devices: 25.6 us -> 28.8 us  [from_behind(): return lax.ppermute(x, axis, pairs)]
  transfers between devices with their start and end apart: 18 -> 19, of which waited for: 9 -> 12; matrix products, arithmetic and copies ran while one was open for 8% -> 8% of each run, Pallas kernels for 0% -> 0%
where the time goes in v9:
time: 426 us; the launch traced here: 422 us
  waiting for transfers between devices  317 us (74%)
  starting transfers between devices  35 us (8%)
  matrix products  31.6 us (7%)
  other arithmetic  17.7 us (4%)
  between operations  14.6 us (3%)
  local copies, waits for them, and re-layouts  5.44 us (1%)
    ppermute x2, waiting for transfers between devices, scatter_wide(): got = lax.ppermute(give, 'xlo', SWAP)  90 us
    ppermute x1, waiting for transfers between devices, gather_wide(): other = lax.ppermute(own, 'xlo', SWAP)  74 us
    reduce_scatter x2, waiting for transfers between devices, scatter_narrow(): t = lax.psum_scatter(q, 'z', scatter_dimension=0, tiled=True)  54.1 us
    reduce_scatter x2, waiting for transfers between devices, scatter_wide(): lax.psum_scatter(total.reshape(zs * rows, -1), 'z', scatter_dimension=0,...  41.3 us
    all_gather x1, waiting for transfers between devices, gather_wide(): own = lax.all_gather(x, 'z', axis=0, tiled=True)  40 us
    ppermute x7, starting transfers between devices, from_behind(): return lax.ppermute(x, axis, pairs)  28.8 us
    ppermute x1, waiting for transfers between devices, gather_narrow(): other = lax.ppermute(x, 'xlo', SWAP)  10.5 us
  transfers between devices with their start and end apart: 19, of which 12 were waited for; matrix products, arithmetic and copies ran while one was open for 8% of the time, Pallas kernels for 0%

profile of v9, /device:TPU:5, one launch (start us, length us, event | category | flops | bytes accessed | tf_op | source)
XLA Modules:
  0.0 421.6 jit_solution(14949771703033737656)
XLA Ops:
  7.2 0.8 select_reduce_fusion.1
  8.8 2.0 convolution_convert_fusion.3
  12.2 1.0 collective-permute-start.2
  13.2 10.5 %collective-permute-done.2 = bf16[32,7168]{1,0:T(8,128)(2,1)S(1)} collective-permute-done((bf16[32,7168]{1,0:T(8,128)(2,1)S(1)}, bf16[32,7168]{1,0:T(8,128)(2,1)S(1)}, u32[]{:S(2)}, u32[]{:S(2)}) %collective-permute-start.2) | collective-permute-done | bytes 458784 | tf_op jit(solution)/shard_map/ppermute | solution.py:41
  23.7 1.1 maximum_select_fusion
  24.8 40.0 %all-gather.3.cloned.1.call-done = bf16[256,7168]{1,0:T(8,128)(2,1)} async-done(((bf16[32,7168]{1,0:T(8,128)(2,1)}), bf16[256,7168]{1,0:T(8,128)(2,1)}) %all-gather.3.cloned.1.call-update) | async-done | bytes 3670032 | tf_op jit(solution)/shard_map/all_gather | solution.py:35
  64.8 0.9 collective-permute-start.1
  65.7 1.8 slice.174
  68.2 0.8 copy-done.3
  69.7 0.9 copy-done.1
  71.2 74.0 %collective-permute-done.1 = bf16[256,7168]{1,0:T(8,128)(2,1)S(1)} collective-permute-done((bf16[256,7168]{1,0:T(8,128)(2,1)}, bf16[256,7168]{1,0:T(8,128)(2,1)S(1)}, u32[]{:S(2)}, u32[]{:S(2)}) %collective-permute-start.1) | collective-permute-done | bytes 3670048 | tf_op jit(solution)/shard_map/ppermute | solution.py:36
  147.4 2.6 all-gather.5.cloned.1.call-done
  150.1 3.6 fusion.16
  153.7 1.4 copy-done.12
  155.1 1.1 fusion.13
  156.2 1.2 multiply_convert_fusion.2
  157.4 1.3 fusion.24
  158.9 1.3 add_convert_fusion
  160.4 1.0 collective-permute-start.8
  161.4 45.4 %collective-permute-done.8 = bf16[8,32,4096]{2,1,0:T(8,128)(2,1)S(1)} collective-permute-done((bf16[8,32,4096]{2,1,0:T(8,128)(2,1)S(1)}, bf16[8,32,4096]{2,1,0:T(8,128)(2,1)S(1)}, u32[]{:S(2)}, u32[]{:S(2)}) %collective-permute-start.8) | collective-permute-done | bytes 2097184 | tf_op jit(solution)/shard_map/ppermute | solution.py:51
  206.9 2.4 fusion
  209.6 2.1 fusion.47
  211.7 3.8 add_convert_fusion.1
  215.6 2.6 convolution_convert_fusion.6
  218.3 1.2 convolution_convert_fusion.5
  219.7 1.0 collective-permute-start.3
  220.7 44.6 %collective-permute-done.3 = bf16[8,32,4096]{2,1,0:T(8,128)(2,1)S(1)} collective-permute-done((bf16[8,32,4096]{2,1,0:T(8,128)(2,1)S(1)}, bf16[8,32,4096]{2,1,0:T(8,128)(2,1)S(1)}, u32[]{:S(2)}, u32[]{:S(2)}) %collective-permute-start.3) | collective-permute-done | bytes 2097184 | tf_op jit(solution)/shard_map/ppermute | solution.py:51
  265.3 2.6 fusion.1
  268.4 4.6 %collective-permute-start.7 = (s32[128]{0:T(128)}, s32[128]{0:T(128)S(1)}, u32[]{:S(2)}, u32[]{:S(2)}) collective-permute-start(s32[128]{0:T(128)} %add_select_fusion), channel_id=1, source_target_pairs={{16,0},{32,16},{48,32},{64,48},{80,64},{96,80},{112,96},{128,112},... | collective-permute-start | bytes 1544 | tf_op jit(solution)/shard_map/ppermute | solution.py:15
  273.0 3.5 collective-permute-start
  276.6 1.9 collective-permute-start.12
  278.5 6.0 %collective-permute-start.6 = (bf16[128,7168]{1,0:T(8,128)(2,1)}, bf16[128,7168]{1,0:T(8,128)(2,1)}, u32[]{:S(2)}, u32[]{:S(2)}) collective-permute-start(bf16[128,7168]{1,0:T(8,128)(2,1)} %bitcast.130), channel_id=1, source_target_pairs={{0,16},{16,32},{32,48},{48,64},{64,80},{80,96},{96,112},{112,128},... | collective-permute-start | bytes 5505032 | tf_op jit(solution)/shard_map/ppermute | solution.py:15
  285.6 1.7 add_convert_fusion.2
  287.3 1.9 collective-permute-start.9
  289.2 7.6 %reduce-scatter.11.cloned.1.call-done = bf16[64,3072]{1,0:T(8,128)(2,1)} async-done(((bf16[512,3072]{1,0:T(8,128)(2,1)}), bf16[64,3072]{1,0:T(8,128)(2,1)}) %reduce-scatter.11.cloned.1.call-update) | async-done | bytes 393232 | tf_op jit(solution)/shard_map/reduce_scatter | solution.py:58
  296.9 1.8 broadcast_select_fusion
  299.5 46.4 %reduce-scatter.7.cloned.1.call-done = bf16[64,3072]{1,0:T(8,128)(2,1)} async-done(((bf16[512,3072]{1,0:T(8,128)(2,1)}), bf16[64,3072]{1,0:T(8,128)(2,1)}) %reduce-scatter.7.cloned.1.call-update) | async-done | bytes 393232 | tf_op jit(solution)/shard_map/reduce_scatter | solution.py:58
  345.9 1.8 broadcast_select_fusion.1
  347.7 41.3 %reduce-scatter.5.cloned.1.call-done = bf16[32,4096]{1,0:T(8,128)(2,1)} async-done(((bf16[256,4096]{1,0:T(8,128)(2,1)}), bf16[32,4096]{1,0:T(8,128)(2,1)}) %reduce-scatter.5.cloned.1.call-update) | async-done | bytes 262160 | tf_op jit(solution)/shard_map/reduce_scatter | solution.py:53
  389.0 1.0 convert_element_type.116
  390.0 1.1 collective-permute-start.4
  391.1 1.0 add_convert_fusion.3
  392.1 2.7 collective-permute-done.4
  394.9 8.1 %collective-permute-start.11 = (bf16[32,3072]{1,0:T(8,128)(2,1)S(1)}, bf16[32,3072]{1,0:T(8,128)(2,1)S(1)}, u32[]{:S(2)}, u32[]{:S(2)}) collective-permute-start(bf16[32,3072]{1,0:T(8,128)(2,1)S(1)} %add_convert_fusion.3), channel_id=1, source_target_pairs={{16,0},{32,16},{48,32},{64,48},{80,64},{96,80},{112,96},{128,112},... | collective-permute-start | bytes 589832 | tf_op jit(solution)/shard_map/ppermute | solution.py:15
  403.2 2.7 collective-permute-start.5
  406.0 1.1 collective-permute-done.11
  407.1 3.5 select_bitcast_fusion.2
  411.4 3.4 select_bitcast_fusion.3
  (73 shorter events, 10.7 us)
Async XLA Ops:
  7.2 3.7 copy-start.2
  7.2 57.7 %all-gather.3.cloned.1.call-start = ((), (), s32[]{:S(2)}) async-start(), calls=%async_computation.4 | async-start | bytes 4128768 | tf_op jit(solution)/shard_map/all_gather | solution.py:35
  12.1 138.0 %all-gather.5.cloned.1.call-start = ((), (), s32[]{:S(2)}) async-start(), calls=%async_computation.5 | async-start | bytes 8257536 | tf_op jit(solution)/shard_map/all_gather | solution.py:43
  12.2 11.5 %collective-permute-start.2 = (bf16[32,7168]{1,0:T(8,128)(2,1)S(1)}, bf16[32,7168]{1,0:T(8,128)(2,1)S(1)}, u32[]{:S(2)}, u32[]{:S(2)}) collective-permute-start(bf16[32,7168]{1,0:T(8,128)(2,1)S(1)} %get-tuple-element.8), channel_id=1, source_target_pairs={{0,8},{8,0},{1,9},{9,1},{2,10},{10,2},{3,11},{11,3},{4,12},{12,4},... | collective-permute-start | bytes 1376264 | tf_op jit(solution)/shard_map/ppermute | solution.py:41
  24.8 42.8 %copy-start.5 = (bf16[1,7168,128]{2,1,0:T(8,128)(2,1)S(1)}, bf16[1,7168,128]{2,1,0:T(8,128)(2,1)}, u32[]{:S(2)}) copy-start(bf16[1,7168,128]{2,1,0:T(8,128)(2,1)} %param.14) | copy-start | bytes 5505028
  24.8 260.8 %reduce-scatter.9.cloned.1.call-start = ((), (), s32[]{:S(2)}) async-start(), calls=%async_computation.8 | async-start | bytes 2359296 | tf_op jit(solution)/shard_map/reduce_scatter | solution.py:53
  64.8 80.4 %collective-permute-start.1 = (bf16[256,7168]{1,0:T(8,128)(2,1)}, bf16[256,7168]{1,0:T(8,128)(2,1)S(1)}, u32[]{:S(2)}, u32[]{:S(2)}) collective-permute-start(bf16[256,7168]{1,0:T(8,128)(2,1)} %all-gather.3.cloned.1.call-done), channel_id=1, source_target_pairs={{0,8},{8,0},{1,9},{9,1},{2,10},{10,2},{3,11},{11,3},{4,12},{12,4},... | collective-permute-start | bytes 11010056 | tf_op jit(solution)/shard_map/ppermute | solution.py:36
  65.7 3.9 copy-start.10
  67.5 1.5 copy-start.3
  69.0 1.5 copy-start.1
  71.2 74.2 %copy-start.6 = (bf16[1,7168,128]{2,1,0:T(8,128)(2,1)S(1)}, bf16[1,7168,128]{2,1,0:T(8,128)(2,1)}, u32[]{:S(2)}) copy-start(bf16[1,7168,128]{2,1,0:T(8,128)(2,1)} %param.14) | copy-start | bytes 5505028
  150.1 3.6 copy-start.4
  150.1 5.0 %copy-start.12 = (bf16[512,7168]{1,0:T(8,128)(2,1)S(1)}, bf16[512,7168]{1,0:T(8,128)(2,1)}, u32[]{:S(2)}) copy-start(bf16[512,7168]{1,0:T(8,128)(2,1)} %all-gather.5.cloned.1.call-done) | copy-start | bytes 22020100
  157.4 1.5 copy-start.7
  160.4 46.4 %collective-permute-start.8 = (bf16[8,32,4096]{2,1,0:T(8,128)(2,1)S(1)}, bf16[8,32,4096]{2,1,0:T(8,128)(2,1)S(1)}, u32[]{:S(2)}, u32[]{:S(2)}) collective-permute-start(bf16[8,32,4096]{2,1,0:T(8,128)(2,1)S(1)} %select_bitcast_fusion), channel_id=1, source_target_pairs={{0,8},{8,0},{1,9},{9,1},{2,10},{10,2},{3,11},{11,3},{4,12},{12,4},... | collective-permute-start | bytes 6291464 | tf_op jit(solution)/shard_map/ppermute | solution.py:51
  209.3 87.5 %reduce-scatter.11.cloned.1.call-start = ((), (), s32[]{:S(2)}) async-start(), calls=%async_computation.9 | async-start | bytes 3538944 | tf_op jit(solution)/shard_map/reduce_scatter | solution.py:58
  215.5 130.4 %reduce-scatter.7.cloned.1.call-start = ((), (), s32[]{:S(2)}) async-start(), calls=%async_computation.7 | async-start | bytes 3538944 | tf_op jit(solution)/shard_map/reduce_scatter | solution.py:58
  218.2 170.8 %reduce-scatter.5.cloned.1.call-start = ((), (), s32[]{:S(2)}) async-start(), calls=%async_computation.6 | async-start | bytes 2359296 | tf_op jit(solution)/shard_map/reduce_scatter | solution.py:53
  219.7 45.6 %collective-permute-start.3 = (bf16[8,32,4096]{2,1,0:T(8,128)(2,1)S(1)}, bf16[8,32,4096]{2,1,0:T(8,128)(2,1)S(1)}, u32[]{:S(2)}, u32[]{:S(2)}) collective-permute-start(bf16[8,32,4096]{2,1,0:T(8,128)(2,1)S(1)} %select_bitcast_fusion.1), channel_id=1, source_target_pairs={{0,8},{8,0},{1,9},{9,1},{2,10},{10,2},{3,11},{11,3},{4,12},{12,4},... | collective-permute-start | bytes 6291464 | tf_op jit(solution)/shard_map/ppermute | solution.py:51
  267.9 8.6 %copy-start = (bf16[1,128,7168]{2,1,0:T(8,128)(2,1)S(1)}, bf16[1,128,7168]{2,1,0:T(8,128)(2,1)}, u32[]{:S(2)}) copy-start(bf16[1,128,7168]{2,1,0:T(8,128)(2,1)} %param.9) | copy-start | bytes 5505028
  268.4 16.6 %collective-permute-start.7 = (s32[128]{0:T(128)}, s32[128]{0:T(128)S(1)}, u32[]{:S(2)}, u32[]{:S(2)}) collective-permute-start(s32[128]{0:T(128)} %add_select_fusion), channel_id=1, source_target_pairs={{16,0},{32,16},{48,32},{64,48},{80,64},{96,80},{112,96},{128,112},... | collective-permute-start | bytes 1544 | tf_op jit(solution)/shard_map/ppermute | solution.py:15
  273.0 130.2 %collective-permute-start = (s32[128]{0:T(128)}, s32[128]{0:T(128)S(1)}, u32[]{:S(2)}, u32[]{:S(2)}) collective-permute-start(s32[128]{0:T(128)} %add_select_fusion), channel_id=1, source_target_pairs={{0,16},{16,32},{32,48},{48,64},{64,80},{80,96},{96,112},{112,128},... | collective-permute-start | bytes 1544 | tf_op jit(solution)/shard_map/ppermute | solution.py:15
  276.6 129.4 %collective-permute-start.12 = (bf16[128,7168]{1,0:T(8,128)(2,1)S(1)}, bf16[128,7168]{1,0:T(8,128)(2,1)}, u32[]{:S(2)}, u32[]{:S(2)}) collective-permute-start(bf16[128,7168]{1,0:T(8,128)(2,1)S(1)} %bitcast.119), channel_id=1, source_target_pairs={{16,0},{32,16},{48,32},{64,48},{80,64},{96,80},{112,96},{128,112},... | collective-permute-start | bytes 5505032 | tf_op jit(solution)/shard_map/ppermute | solution.py:15
  278.5 132.1 %collective-permute-start.6 = (bf16[128,7168]{1,0:T(8,128)(2,1)}, bf16[128,7168]{1,0:T(8,128)(2,1)}, u32[]{:S(2)}, u32[]{:S(2)}) collective-permute-start(bf16[128,7168]{1,0:T(8,128)(2,1)} %bitcast.130), channel_id=1, source_target_pairs={{0,16},{16,32},{32,48},{48,64},{64,80},{80,96},{96,112},{112,128},... | collective-permute-start | bytes 5505032 | tf_op jit(solution)/shard_map/ppermute | solution.py:15
  287.3 118.7 %collective-permute-start.9 = (bf16[32,4096]{1,0:T(8,128)(2,1)}, bf16[32,4096]{1,0:T(8,128)(2,1)}, u32[]{:S(2)}, u32[]{:S(2)}) collective-permute-start(bf16[32,4096]{1,0:T(8,128)(2,1)} %add_convert_fusion.2), channel_id=1, source_target_pairs={{16,0},{32,16},{48,32},{64,48},{80,64},{96,80},{112,96},{128,112},... | collective-permute-start | bytes 786440 | tf_op jit(solution)/shard_map/ppermute | solution.py:15
  296.9 94.2 %copy-start.9 = (bf16[64,3072]{1,0:T(8,128)(2,1)S(1)}, bf16[64,3072]{1,0:T(8,128)(2,1)}, u32[]{:S(2)}) copy-start(bf16[64,3072]{1,0:T(8,128)(2,1)} %reduce-scatter.11.cloned.1.call-done) | copy-start | bytes 1179652
  298.7 91.4 %collective-permute-start.10 = (bf16[32,3072]{1,0:T(8,128)(2,1)}, bf16[32,3072]{1,0:T(8,128)(2,1)}, u32[]{:S(2)}, u32[]{:S(2)}) collective-permute-start(bf16[32,3072]{1,0:T(8,128)(2,1)} %broadcast_select_fusion), channel_id=1, source_target_pairs={{0,8},{8,0},{1,9},{9,1},{2,10},{10,2},{3,11},{11,3},{4,12},{12,4},... | collective-permute-start | bytes 589832 | tf_op jit(solution)/shard_map/ppermute | solution.py:62
  345.9 57.0 %copy-start.8 = (bf16[64,3072]{1,0:T(8,128)(2,1)S(1)}, bf16[64,3072]{1,0:T(8,128)(2,1)}, u32[]{:S(2)}) copy-start(bf16[64,3072]{1,0:T(8,128)(2,1)} %reduce-scatter.7.cloned.1.call-done) | copy-start | bytes 1179652
  390.0 17.1 %copy-start.11 = (pred[128]{0:T(512)(128)(4,1)S(1)}, pred[128]{0:T(512)(128)(4,1)}, u32[]{:S(2)}) copy-start(pred[128]{0:T(512)(128)(4,1)} %broadcast_compare_fusion.1) | copy-start | bytes 388
  390.0 4.8 %collective-permute-start.4 = (bf16[32,3072]{1,0:T(8,128)(2,1)}, bf16[32,3072]{1,0:T(8,128)(2,1)S(1)}, u32[]{:S(2)}, u32[]{:S(2)}) collective-permute-start(bf16[32,3072]{1,0:T(8,128)(2,1)} %broadcast_select_fusion.1), channel_id=1, source_target_pairs={{0,8},{8,0},{1,9},{9,1},{2,10},{10,2},{3,11},{11,3},{4,12},{12,4},... | collective-permute-start | bytes 589832 | tf_op jit(solution)/shard_map/ppermute | solution.py:62
  394.9 12.3 %collective-permute-start.11 = (bf16[32,3072]{1,0:T(8,128)(2,1)S(1)}, bf16[32,3072]{1,0:T(8,128)(2,1)S(1)}, u32[]{:S(2)}, u32[]{:S(2)}) collective-permute-start(bf16[32,3072]{1,0:T(8,128)(2,1)S(1)} %add_convert_fusion.3), channel_id=1, source_target_pairs={{16,0},{32,16},{48,32},{64,48},{80,64},{96,80},{112,96},{128,112},... | collective-permute-start | bytes 589832 | tf_op jit(solution)/shard_map/ppermute | solution.py:15
  403.2 8.2 %collective-permute-start.5 = (bf16[32,7168]{1,0:T(8,128)(2,1)S(1)}, bf16[32,7168]{1,0:T(8,128)(2,1)S(1)}, u32[]{:S(2)}, u32[]{:S(2)}) collective-permute-start(bf16[32,7168]{1,0:T(8,128)(2,1)S(1)} %fusion.30), channel_id=1, source_target_pairs={{0,16},{16,32},{32,48},{48,64},{64,80},{80,96},{96,112},{112,128},... | collective-permute-start | bytes 1376264 | tf_op jit(solution)/shard_map/ppermute | solution.py:15
Sparse Core Ops, SparseCore 0:
  12.2 52.5 all-gather.2
  67.2 82.8 all-gather.4
  209.4 38.0 reduce-scatter.8
  250.0 46.8 reduce-scatter.10
  299.3 46.5 reduce-scatter.6
  348.3 40.6 reduce-scatter.4
